TPU v7x, 128 devices: a whole 4x4x4 slice. The times are simulated.
128 devices in a mesh: gz: 64 (over x_hi, z, y, core), row: 2 (over x_lo).
Axes of the slice: x: 4 (x_hi: 2, x_lo: 2; x = x_hi * 2 + x_lo), y: 4, z: 4, core: 2. Of those that a mesh axis runs over, the one named last changes fastest.
Arguments:
- axial_vel: float32 [1024, 256, 256], P('gz', 'row'), may hold values from -6 to 6
- radial_vel: float32 [1024, 256, 256], P('gz', 'row'), may hold values from -6 to 6
- swirl_vel: float32 [1024, 256, 256], P('gz', 'row'), may hold values from -6 to 6
- inflow_rate: float32 [48], replicated, may hold values from 0.25 to 2
- canopy_gore: int32 [1024, 256, 256], P('gz', 'row'), may hold values from 0 to 48, as said below
Outputs:
- axial_out: float32 [1024, 256, 256], P('gz', 'row')
- radial_projected_velocity: float32 [1024, 256, 256], P('gz', 'row')
- swirl_out: float32 [1024, 256, 256], P('gz', 'row')
Inputs may be any that keep to these rules, and one draw needn't show every extreme that they name: `canopy_gore`: a canopy cell in azimuthal column t holds gore floor(t * 48 / 256); other cells hold 48.
All inputs are finite; a program needn't handle non-finite values.
Results may differ from a plain program's by a relative error of at most 0.0009.
Values sent between devices are 32-bit elements; how exact they have to be, the bound alone decides.
No kernel may reach another device: no remote copies, remote signals or barrier semaphores. Data moves between devices by JAX's collectives and lax.ppermute only.
A program may use at most 64 MiB of HBM per device.

v0:
```python
import math

import numpy as np

import jax
import jax.numpy as jnp
from jax import lax
from jax.sharding import PartitionSpec as P

NX = 1024
NR = 256
NT = 256
GORES = 48


helmholtz_shift = 0.001
maximal_precision = lax.Precision.HIGHEST


def extended(block, sides, width):
    for axis, dim in sides:
        count = lax.axis_size(axis)
        forward = [(i, i + 1) for i in range(count - 1)]
        backward = [(target, source) for source, target in forward]
        low = lax.ppermute(
            lax.slice_in_dim(block, block.shape[dim] - width, None, axis=dim), axis, forward
        )
        high = lax.ppermute(lax.slice_in_dim(block, 0, width, axis=dim), axis, backward)
        block = jnp.concatenate([low, block, high], axis=dim)
    return block


def azimuth_basis(extent, mode_ids):
    positions = jnp.arange(extent, dtype=jnp.int32)
    half_way = extent // 2
    frequency = jnp.where(mode_ids <= half_way, mode_ids, mode_ids - half_way)
    phases = positions[:, None] * frequency[None, :] % extent
    angles = phases.astype(jnp.float32) * (2.0 * math.pi / extent)
    weights = jnp.where(
        (mode_ids == 0) | (mode_ids == half_way), math.sqrt(1.0 / extent), math.sqrt(2.0 / extent)
    ).astype(jnp.float32)
    return (
        jnp.where((mode_ids > half_way)[None, :], jnp.sin(angles), jnp.cos(angles))
        * weights[None, :]
    )


def azimuth_eigen(mode_ids):
    half_way = NT // 2
    frequency = jnp.where(mode_ids <= half_way, mode_ids, mode_ids - half_way)
    angles = frequency.astype(jnp.float32) * (2.0 * math.pi / NT)
    arc_step = 0.75 * NR * 2.0 * math.pi / NT
    return (2.0 - 2.0 * jnp.cos(angles)) / (arc_step * arc_step)


def axial_basis(extent):
    indices = jnp.arange(extent, dtype=jnp.int32) + 1
    phases = indices[:, None] * indices[None, :] % (2 * (extent + 1))
    angles = phases.astype(jnp.float32) * (math.pi / (extent + 1))
    return jnp.sin(angles) * math.sqrt(2.0 / (extent + 1))


def axial_eigen(extent):
    indices = jnp.arange(extent, dtype=jnp.int32) + 1
    return 2.0 - 2.0 * jnp.cos(indices.astype(jnp.float32) * (math.pi / (extent + 1)))


def radial_basis(extent):
    mode_ids = jnp.arange(extent, dtype=jnp.int32)[:, None]
    cell_ids = jnp.arange(extent, dtype=jnp.int32)[None, :]
    phases = mode_ids * (2 * cell_ids + 1) % (4 * extent)
    angles = phases.astype(jnp.float32) * (math.pi / (2 * extent))
    weights = jnp.where(mode_ids == 0, math.sqrt(1.0 / extent), math.sqrt(2.0 / extent)).astype(
        jnp.float32
    )
    return jnp.cos(angles) * weights


def radial_eigen(mode_ids):
    return 2.0 - 2.0 * jnp.cos(mode_ids.astype(jnp.float32) * (math.pi / NR))


def cell_radius(cell_ids):
    return cell_ids.astype(jnp.float32) + (0.25 * NR + 0.5)


def fixed_azimuth_basis():
    positions = np.arange(NT)[:, None]
    modes = np.arange(NT)[None, :]
    frequency = np.where(modes <= NT // 2, modes, modes - NT // 2)
    angles = (positions * frequency % NT) * (2.0 * math.pi / NT)
    weights = np.where((modes == 0) | (modes == NT // 2), math.sqrt(1.0 / NT), math.sqrt(2.0 / NT))
    return (np.where(modes > NT // 2, np.sin(angles), np.cos(angles)) * weights).astype(np.float32)


def fixed_axial_basis():
    indices = np.arange(1, NX + 1)
    phases = indices[:, None] * indices[None, :] % (2 * (NX + 1))
    return (np.sin(phases * (math.pi / (NX + 1))) * math.sqrt(2.0 / (NX + 1))).astype(np.float32)


def fixed_radial_basis():
    modes = np.arange(NR)[:, None]
    cells = np.arange(NR)[None, :]
    angles = (modes * (2 * cells + 1) % (4 * NR)) * (math.pi / (2 * NR))
    weights = np.where(modes == 0, math.sqrt(1.0 / NR), math.sqrt(2.0 / NR))
    return (np.cos(angles) * weights).astype(np.float32)


AZIMUTH_TABLE = fixed_azimuth_basis()
AXIAL_TABLE = fixed_axial_basis()
RADIAL_TABLE = fixed_radial_basis()


def denominator_of(mode_ids, radial_ids):
    total = azimuth_eigen(mode_ids)[:, None, None] + axial_eigen(NX)[None, :, None]
    return total + radial_eigen(radial_ids)[None, None, :] + helmholtz_shift


def canopy_source(gore_map, rate_table):
    gore_ids = jnp.arange(rate_table.shape[0], dtype=jnp.int32)
    column_gore = jnp.arange(NT, dtype=jnp.int32) * GORES // NT
    matches = column_gore[:, None] == gore_ids[None, :]
    column_rate = jnp.sum(jnp.where(matches, rate_table[None, :], 0.0), axis=1)
    return jnp.where(gore_map < GORES, column_rate[None, None, :], 0.0)


def body(axial_vel, radial_vel, swirl_vel, inflow_rate, canopy_gore):
    radial_block = axial_vel.shape[1]
    axial_block = axial_vel.shape[0]
    row_index = lax.axis_index("row")
    row_count = lax.axis_size("row")
    gz_count = lax.axis_size("gz")
    both = ("gz", "row")
    device_count = gz_count * row_count
    spacing = 2.0 * math.pi / NT
    own_first = row_index * radial_block
    own_cells = own_first + jnp.arange(radial_block, dtype=jnp.int32)
    radius = cell_radius(own_cells)[None, :, None]
    axial_pad = extended(axial_vel, (("gz", 0),), 1)
    radial_flux = extended(radial_vel * radius, (("row", 1),), 1)
    divergence = 0.5 * (axial_pad[2:] - axial_pad[:-2])
    divergence = divergence + (radial_flux[:, 2:] - radial_flux[:, :-2]) / (2.0 * radius)
    divergence = divergence + (jnp.roll(swirl_vel, -1, 2) - jnp.roll(swirl_vel, 1, 2)) / (
        2.0 * radius * spacing
    )
    right_side = divergence - canopy_source(canopy_gore, inflow_rate)
    all_modes = jnp.arange(NT, dtype=jnp.int32)
    fourier = jnp.asarray(AZIMUTH_TABLE)
    spectrum_in = jnp.einsum("xrt,tm->mxr", right_side, fourier, precision=maximal_precision)
    modes_each = NT // device_count
    spectrum_in = spectrum_in.reshape(device_count, modes_each, axial_block, radial_block)
    resident = lax.all_to_all(spectrum_in, both, split_axis=0, concat_axis=0, tiled=True)
    resident = resident.reshape(gz_count, row_count, modes_each, axial_block, radial_block)
    mode_ids = lax.axis_index(both) * modes_each + jnp.arange(modes_each, dtype=jnp.int32)
    axial_table = jnp.asarray(AXIAL_TABLE).reshape(NX, gz_count, axial_block)
    radial_table = jnp.asarray(RADIAL_TABLE)
    axial_coefficient = jnp.einsum(
        "kgx,grmxj->mkrj", axial_table, resident, precision=maximal_precision
    ).reshape(modes_each, NX, NR)
    spectrum = jnp.einsum("sj,mkj->mks", radial_table, axial_coefficient, precision=maximal_precision)
    scaled = spectrum / denominator_of(mode_ids, jnp.arange(NR, dtype=jnp.int32))
    radial_returned = jnp.einsum("sj,mks->mkj", radial_table, scaled, precision=maximal_precision)
    radial_returned = radial_returned.reshape(modes_each, NX, row_count, radial_block)
    physical_space = jnp.einsum(
        "kgx,mkrj->grmxj", axial_table, radial_returned, precision=maximal_precision
    ).reshape(device_count, modes_each, axial_block, radial_block)
    returned = lax.all_to_all(physical_space, both, split_axis=0, concat_axis=0, tiled=True)
    returned = returned.reshape(NT, axial_block, radial_block)
    pressure = -jnp.einsum("qxr,tq->xrt", returned, fourier, precision=maximal_precision)
    padded = extended(pressure, (("gz", 0), ("row", 1)), 1)
    lower_ghost = jnp.where(row_index == 0, pressure[:, :1], padded[1:-1, :1])
    upper_ghost = jnp.where(row_index == row_count - 1, pressure[:, -1:], padded[1:-1, -1:])
    above = jnp.concatenate([pressure[:, 1:], upper_ghost], axis=1)
    below = jnp.concatenate([lower_ghost, pressure[:, :-1]], axis=1)
    axial_out = axial_vel - 0.5 * (padded[2:, 1:-1] - padded[:-2, 1:-1])
    radial_projected_velocity = radial_vel - 0.5 * (above - below)
    swirl_out = swirl_vel - (jnp.roll(pressure, -1, 2) - jnp.roll(pressure, 1, 2)) / (
        2.0 * radius * spacing
    )
    return (axial_out, radial_projected_velocity, swirl_out)


def solution(mesh):
    placed = (
        P("gz", "row", None),
        P("gz", "row", None),
        P("gz", "row", None),
        P(),
        P("gz", "row", None),
    )
    return jax.shard_map(
        body,
        mesh=mesh,
        in_specs=placed,
        out_specs=(P("gz", "row", None), P("gz", "row", None), P("gz", "row", None)),
        check_vma=False,
    )
```

profile of v0, /device:TPU:6, one launch (start us, length us, event | category | flops | bytes accessed | tf_op | source)
XLA Modules:
  0.0 161.8 jit_solution(10829433169701075752)
XLA Ops:
  0.6 0.0 copy-start.3
  0.7 0.0 copy-start
  0.7 2.0 %broadcast_multiply_fusion = f32[16,128,256]{2,1,0:T(8,128)S(1)} fusion(f32[16,128,256]{2,1,0:T(8,128)} %param.9, f32[128]{0:T(128)S(1)} %convert_add_fusion), kind=kLoop, calls=%fused_computation.41 | loop fusion | flops 524288 | bytes 4194816 | tf_op jit(solution)/shard_map/mul | solution.py:141
  2.7 2.7 %collective-permute-start.2 = (f32[16,1,256]{2,1,0:T(1,128)S(1)}, f32[16,1,256]{2,1,0:T(1,128)S(1)}, u32[]{:S(2)}, u32[]{:S(2)}) collective-permute-start(f32[16,1,256]{2,1,0:T(1,128)S(1)} %get-tuple-element.21), channel_id=1, source_target_pairs={{1,0},{3,2},{5,4},{7,6},{9,8},{11,10},{13,12},{15,14},{17,16},{19,... | collective-permute-start | bytes 49160 | tf_op jit(solution)/shard_map/ppermute | solution.py:28
  5.5 1.3 collective-permute-start.3
  6.8 8.1 %collective-permute-start = (f32[1,128,256]{2,1,0:T(8,128)S(1)}, f32[1,128,256]{2,1,0:T(8,128)S(1)}, u32[]{:S(2)}, u32[]{:S(2)}) collective-permute-start(f32[1,128,256]{2,1,0:T(8,128)S(1)} %get-tuple-element.19), channel_id=1, source_target_pairs={{2,0},{4,2},{6,4},{8,6},{10,8},{12,10},{14,12},{16,14},{18,16},{20... | collective-permute-start | bytes 393224 | tf_op jit(solution)/shard_map/ppermute | solution.py:28
  14.9 1.9 %collective-permute-start.1 = (f32[1,128,256]{2,1,0:T(8,128)S(1)}, f32[1,128,256]{2,1,0:T(8,128)S(1)}, u32[]{:S(2)}, u32[]{:S(2)}) collective-permute-start(f32[1,128,256]{2,1,0:T(8,128)S(1)} %get-tuple-element.20), channel_id=1, source_target_pairs={{0,2},{2,4},{4,6},{6,8},{8,10},{10,12},{12,14},{14,16},{16,18},{18... | collective-permute-start | bytes 393224 | tf_op jit(solution)/shard_map/ppermute | solution.py:25
  16.8 0.7 fusion.51
  17.6 0.0 copy-start.7
  17.6 0.0 copy-start.5
  17.6 0.0 copy-start.8
  17.6 0.4 fusion.50
  18.0 0.2 copy-done.7
  18.2 0.1 select_reduce_fusion
  18.4 0.0 collective-permute-done
  18.4 8.5 %collective-permute-done.1 = f32[1,128,256]{2,1,0:T(8,128)S(1)} collective-permute-done((f32[1,128,256]{2,1,0:T(8,128)S(1)}, f32[1,128,256]{2,1,0:T(8,128)S(1)}, u32[]{:S(2)}, u32[]{:S(2)}) %collective-permute-start.1) | collective-permute-done | bytes 131104 | tf_op jit(solution)/shard_map/ppermute | solution.py:25
  26.9 3.3 %fusion.21 = f32[256,16,128]{2,0,1:T(8,128)S(1)} fusion(f32[256,256,1]{0,1,2:T(8,128)S(1)} %copy-done.5, f32[16,128,256]{2,1,0:T(8,128)S(1)} %broadcast_multiply_fusion, f32[16,1,256]{2,1,0:T(1,128)S(1)} %collective-permute-done.3, f32[16,1,256]{2,1,0:T(1,128)S(1)} %collective-permute-done.2, f32[16,128,256]{2,1,0:T(8,128)S(1)} %copy-done.3, ...), kind=kOutput, calls=%fused_computation.30 | convolution fusion | flops 1619525632 | bytes 13142016 | tf_op jit(solution)/shard_map/xrt,tm->mxr/dot_general | solution.py:150
  30.2 2.5 %copy.20 = f32[128,2,16,128]{3,2,1,0:T(8,128)} copy(f32[128,2,16,128]{3,1,0,2:T(2,128)S(1)} %bitcast.36) | data formatting | bytes 4194304 | tf_op jit(solution)/shard_map/reshape | solution.py:152
  32.7 5.8 %all-to-all-start = ((f32[128,2,16,128]{3,2,1,0:T(8,128)}), f32[128,2,16,128]{3,2,1,0:T(8,128)}, u32[]{:S(2)}, u32[]{:S(2)}) async-start(f32[128,2,16,128]{3,2,1,0:T(8,128)} %copy.20), calls=%async_computation | async-start | bytes 4194304 | tf_op jit(solution)/shard_map/all_to_all | solution.py:153
  38.7 0.1 broadcast_add_fusion
  38.7 28.8 %all-to-all-done = f32[128,2,16,128]{3,2,1,0:T(8,128)} async-done(((f32[128,2,16,128]{3,2,1,0:T(8,128)}), f32[128,2,16,128]{3,2,1,0:T(8,128)}, u32[]{:S(2)}, u32[]{:S(2)}) %all-to-all-start) | async-done | bytes 2097184 | tf_op jit(solution)/shard_map/all_to_all | solution.py:153
  67.5 9.6 %fusion.54 = f32[2,2,128,1024,1]{3,2,1,0,4:T(8,128)S(1)} fusion(f32[64,2,2,16,128]{4,3,2,1,0:T(8,128)} %bitcast.2, f32[1024,64,16,1,1]{0,2,4,3,1:T(8,128)} %constant.77), kind=kOutput, calls=%fused_computation.80 | convolution fusion | flops 6442450944 | bytes 8388608 | tf_op jit(solution)/shard_map/kgx,grmxj->mkrj/dot_general | solution.py:158
  77.1 0.0 copy-start.6
  77.1 0.2 copy.31
  77.4 0.7 copy-done.6
  78.1 3.7 %fusion.55 = f32[2,1024,256]{2,1,0:T(8,128)S(1)} fusion(f32[2,1024,256]{1,2,0:T(8,128)S(1)} %bitcast.34, f32[256,256,1]{1,0,2:T(8,128)S(1)} %copy-done.6), kind=kOutput, calls=%fused_computation.81 | convolution fusion | flops 1610612736 | bytes 4456448 | tf_op jit(solution)/shard_map/sj,mkj->mks/dot_general | solution.py:161
  81.7 0.0 copy-start.2
  81.7 2.4 %fusion.17 = f32[2,1024,256]{1,2,0:T(8,128)S(1)} fusion(f32[256,256,1]{1,0,2:T(8,128)S(1)} %copy-done.6, f32[2,1024,256]{2,1,0:T(8,128)S(1)} %fusion.55, f32[256]{0:T(256)S(1)} %multiply_subtract_fusion.1, f32[2,1024]{1,0:T(2,128)S(1)} %broadcast_add_fusion), kind=kOutput, calls=%fused_computation.26 | convolution fusion | flops 1612185600 | bytes 4465664 | tf_op jit(solution)/shard_map/sj,mks->mkj/dot_general | solution.py:163
  84.2 7.0 %convolution_bitcast_fusion = f32[64,2,2,16,128]{4,0,3,1,2:T(8,128)S(1)} fusion(f32[2,1024,2,128,1]{1,3,4,2,0:T(8,128)S(1)} %bitcast.35, f32[1024,64,16,1,1]{0,1,2,4,3:T(8,128)S(1)} %copy-done.2), kind=kOutput, calls=%fused_computation.31 | convolution fusion | flops 6442450944 | bytes 8388608 | tf_op jit(solution)/shard_map/kgx,mkrj->grmxj/dot_general | solution.py:165
  91.2 2.5 %copy.26 = f32[64,2,2,16,128]{4,3,2,1,0:T(8,128)} copy(f32[64,2,2,16,128]{4,0,3,1,2:T(8,128)S(1)} %convolution_bitcast_fusion) | data formatting | bytes 4194304 | tf_op jit(solution)/shard_map/kgx,mkrj->grmxj/transpose | solution.py:165
  93.7 6.6 %all-to-all-start.1 = ((f32[128,2,16,128]{3,2,1,0:T(8,128)}), f32[128,2,16,128]{3,2,1,0:T(8,128)}, u32[]{:S(2)}, u32[]{:S(2)}) async-start(f32[128,2,16,128]{3,2,1,0:T(8,128)} %bitcast.33), calls=%async_computation.1 | async-start | bytes 4194304 | tf_op jit(solution)/shard_map/all_to_all | solution.py:168
  100.4 29.1 %all-to-all-done.1 = f32[128,2,16,128]{3,2,1,0:T(8,128)} async-done(((f32[128,2,16,128]{3,2,1,0:T(8,128)}), f32[128,2,16,128]{3,2,1,0:T(8,128)}, u32[]{:S(2)}, u32[]{:S(2)}) %all-to-all-start.1) | async-done | bytes 2097184 | tf_op jit(solution)/shard_map/all_to_all | solution.py:168
  129.5 5.4 %fusion.23 = f32[16,128,256]{2,1,0:T(8,128)S(1)} fusion(f32[256,256,1]{0,1,2:T(8,128)S(1)} %copy-done.5, f32[256,16,128]{2,1,0:T(8,128)} %bitcast.15), kind=kOutput, calls=%fused_computation.32 | convolution fusion | flops 1611137024 | bytes 4456448 | tf_op jit(solution)/shard_map/qxr,tq->xrt/dot_general | solution.py:170
  134.8 0.7 fusion.47
  135.6 0.4 fusion.46
  136.0 3.0 %collective-permute-start.4 = (f32[1,128,256]{2,1,0:T(8,128)S(1)}, f32[1,128,256]{2,1,0:T(8,128)S(1)}, u32[]{:S(2)}, u32[]{:S(2)}) collective-permute-start(f32[1,128,256]{2,1,0:T(8,128)S(1)} %get-tuple-element.13), channel_id=1, source_target_pairs={{2,0},{4,2},{6,4},{8,6},{10,8},{12,10},{14,12},{16,14},{18,16},{20... | collective-permute-start | bytes 393224 | tf_op jit(solution)/shard_map/ppermute | solution.py:28
  139.0 1.9 %collective-permute-start.5 = (f32[1,128,256]{2,1,0:T(8,128)S(1)}, f32[1,128,256]{2,1,0:T(8,128)S(1)}, u32[]{:S(2)}, u32[]{:S(2)}) collective-permute-start(f32[1,128,256]{2,1,0:T(8,128)S(1)} %get-tuple-element.14), channel_id=1, source_target_pairs={{0,2},{2,4},{4,6},{6,8},{8,10},{10,12},{12,14},{14,16},{16,18},{18... | collective-permute-start | bytes 393224 | tf_op jit(solution)/shard_map/ppermute | solution.py:25
  140.9 2.3 %fusion.14 = f32[16,128,256]{2,1,0:T(8,128)} fusion(f32[16,128,256]{2,1,0:T(8,128)S(1)} %copy-done, f32[16,128,1]{2,1,0:T(8,128)S(1)} %get-tuple-element.6, f32[16,128,255]{2,1,0:T(8,128)S(1)} %get-tuple-element.8, f32[16,128,255]{2,1,0:T(8,128)S(1)} %get-tuple-element.7, f32[16,128,1]{2,1,0:T(8,128)S(1)} %get-tuple-element.5, f32[128]{0:T(128)S(1)} %get-tuple-element.23), kind=kLoop, calls=%fused_computation.23 | loop fusion | flops 2621440 | bytes 8389120 | tf_op jit(solution)/shard_map/sub | solution.py:178
  143.2 0.5 fusion.48
  143.7 0.0 copy-start.4
  143.7 7.3 %collective-permute-done.5 = f32[1,128,256]{2,1,0:T(8,128)S(1)} collective-permute-done((f32[1,128,256]{2,1,0:T(8,128)S(1)}, f32[1,128,256]{2,1,0:T(8,128)S(1)}, u32[]{:S(2)}, u32[]{:S(2)}) %collective-permute-start.5) | collective-permute-done | bytes 131104 | tf_op jit(solution)/shard_map/ppermute | solution.py:25
  151.0 3.1 %collective-permute-start.6 = (f32[18,1,256]{2,1,0:T(1,128)S(1)}, f32[18,1,256]{2,1,0:T(1,128)S(1)}, u32[]{:S(2)}, u32[]{:S(2)}) collective-permute-start(f32[18,1,256]{2,1,0:T(1,128)S(1)} %get-tuple-element.4), channel_id=1, source_target_pairs={{1,0},{3,2},{5,4},{7,6},{9,8},{11,10},{13,12},{15,14},{17,16},{19,... | collective-permute-start | bytes 55304 | tf_op jit(solution)/shard_map/ppermute | solution.py:28
  154.1 0.0 copy-start.1
  154.1 1.4 collective-permute-start.7
  155.5 1.8 %fusion.2 = f32[16,128,256]{2,1,0:T(8,128)} fusion(f32[16,128,256]{2,1,0:T(8,128)S(1)} %copy-done.4, f32[16,128,256]{2,1,0:T(8,128)S(1)} %fusion.23, f32[1,128,256]{2,1,0:T(8,128)S(1)} %collective-permute-done.5, f32[1,128,256]{2,1,0:T(8,128)S(1)} %collective-permute-done.4), kind=kLoop, calls=%fused_computation.3 | loop fusion | flops 2621440 | bytes 6553600 | tf_op jit(solution)/shard_map/sub | solution.py:176
  157.3 0.0 collective-permute-done.6
  157.3 2.6 %collective-permute-done.7 = f32[18,1,256]{2,1,0:T(1,128)S(1)} collective-permute-done((f32[18,1,256]{2,1,0:T(1,128)S(1)}, f32[18,1,256]{2,1,0:T(1,128)S(1)}, u32[]{:S(2)}, u32[]{:S(2)}) %collective-permute-start.7) | collective-permute-done | bytes 18464 | tf_op jit(solution)/shard_map/ppermute | solution.py:25
  159.9 1.8 %fusion.12 = f32[16,128,256]{2,1,0:T(8,128)} fusion(f32[16,128,256]{2,1,0:T(8,128)S(1)} %copy-done.1, f32[16,1,256]{2,1,0:T(1,128)S(1)} %get-tuple-element.10, f32[16,127,256]{2,1,0:T(8,128)S(1)} %get-tuple-element.12, f32[16,127,256]{2,1,0:T(8,128)S(1)} %get-tuple-element.11, f32[16,1,256]{2,1,0:T(1,128)S(1)} %get-tuple-element.9), kind=kLoop, calls=%fused_computation.20 | loop fusion | flops 2621440 | bytes 8388608 | tf_op jit(solution)/shard_map/sub | solution.py:177
  (21 shorter events, 0.3 us)
Async XLA Ops:
  0.6 6.1 %copy-start.3 = (f32[16,128,256]{2,1,0:T(8,128)S(1)}, f32[16,128,256]{2,1,0:T(8,128)}, u32[]{:S(2)}) copy-start(f32[16,128,256]{2,1,0:T(8,128)} %param.8) | copy-start | bytes 6291460
  0.7 16.2 %copy-start = (f32[16,128,256]{2,1,0:T(8,128)S(1)}, f32[16,128,256]{2,1,0:T(8,128)}, u32[]{:S(2)}) copy-start(f32[16,128,256]{2,1,0:T(8,128)} %param.10) | copy-start | bytes 6291460
  2.7 15.6 %collective-permute-start.2 = (f32[16,1,256]{2,1,0:T(1,128)S(1)}, f32[16,1,256]{2,1,0:T(1,128)S(1)}, u32[]{:S(2)}, u32[]{:S(2)}) collective-permute-start(f32[16,1,256]{2,1,0:T(1,128)S(1)} %get-tuple-element.21), channel_id=1, source_target_pairs={{1,0},{3,2},{5,4},{7,6},{9,8},{11,10},{13,12},{15,14},{17,16},{19,... | collective-permute-start | bytes 49160 | tf_op jit(solution)/shard_map/ppermute | solution.py:28
  5.5 12.9 %collective-permute-start.3 = (f32[16,1,256]{2,1,0:T(1,128)S(1)}, f32[16,1,256]{2,1,0:T(1,128)S(1)}, u32[]{:S(2)}, u32[]{:S(2)}) collective-permute-start(f32[16,1,256]{2,1,0:T(1,128)S(1)} %get-tuple-element.22), channel_id=1, source_target_pairs={{0,1},{2,3},{4,5},{6,7},{8,9},{10,11},{12,13},{14,15},{16,17},{18,... | collective-permute-start | bytes 49160 | tf_op jit(solution)/shard_map/ppermute | solution.py:25
  6.8 11.6 %collective-permute-start = (f32[1,128,256]{2,1,0:T(8,128)S(1)}, f32[1,128,256]{2,1,0:T(8,128)S(1)}, u32[]{:S(2)}, u32[]{:S(2)}) collective-permute-start(f32[1,128,256]{2,1,0:T(8,128)S(1)} %get-tuple-element.19), channel_id=1, source_target_pairs={{2,0},{4,2},{6,4},{8,6},{10,8},{12,10},{14,12},{16,14},{18,16},{20... | collective-permute-start | bytes 393224 | tf_op jit(solution)/shard_map/ppermute | solution.py:28
  14.9 12.0 %collective-permute-start.1 = (f32[1,128,256]{2,1,0:T(8,128)S(1)}, f32[1,128,256]{2,1,0:T(8,128)S(1)}, u32[]{:S(2)}, u32[]{:S(2)}) collective-permute-start(f32[1,128,256]{2,1,0:T(8,128)S(1)} %get-tuple-element.20), channel_id=1, source_target_pairs={{0,2},{2,4},{4,6},{6,8},{8,10},{10,12},{12,14},{14,16},{16,18},{18... | collective-permute-start | bytes 393224 | tf_op jit(solution)/shard_map/ppermute | solution.py:25
  17.6 0.7 copy-start.7
  17.6 9.3 %copy-start.5 = (f32[256,256,1]{0,1,2:T(8,128)S(1)}, f32[256,256,1]{0,1,2:T(8,128)}, u32[]{:S(2)}) copy-start(f32[256,256,1]{0,1,2:T(8,128)} %constant.76) | copy-start | bytes 786436
  17.6 9.3 %copy-start.8 = (s32[16,128,256]{2,1,0:T(8,128)S(1)}, s32[16,128,256]{2,1,0:T(8,128)}, u32[]{:S(2)}) copy-start(s32[16,128,256]{2,1,0:T(8,128)} %param.12) | copy-start | bytes 6291460
  32.7 34.8 %all-to-all-start = ((f32[128,2,16,128]{3,2,1,0:T(8,128)}), f32[128,2,16,128]{3,2,1,0:T(8,128)}, u32[]{:S(2)}, u32[]{:S(2)}) async-start(f32[128,2,16,128]{3,2,1,0:T(8,128)} %copy.20), calls=%async_computation | async-start | bytes 4194304 | tf_op jit(solution)/shard_map/all_to_all | solution.py:153
  77.1 1.0 copy-start.6
  81.7 2.4 %copy-start.2 = (f32[1024,64,16,1,1]{0,1,2,4,3:T(8,128)S(1)}, f32[1024,64,16,1,1]{0,1,2,4,3:T(8,128)}, u32[]{:S(2)}) copy-start(f32[1024,64,16,1,1]{0,1,2,4,3:T(8,128)} %constant.80) | copy-start | bytes 12582916
  93.7 35.7 %all-to-all-start.1 = ((f32[128,2,16,128]{3,2,1,0:T(8,128)}), f32[128,2,16,128]{3,2,1,0:T(8,128)}, u32[]{:S(2)}, u32[]{:S(2)}) async-start(f32[128,2,16,128]{3,2,1,0:T(8,128)} %bitcast.33), calls=%async_computation.1 | async-start | bytes 4194304 | tf_op jit(solution)/shard_map/all_to_all | solution.py:168
  136.0 7.7 %collective-permute-start.4 = (f32[1,128,256]{2,1,0:T(8,128)S(1)}, f32[1,128,256]{2,1,0:T(8,128)S(1)}, u32[]{:S(2)}, u32[]{:S(2)}) collective-permute-start(f32[1,128,256]{2,1,0:T(8,128)S(1)} %get-tuple-element.13), channel_id=1, source_target_pairs={{2,0},{4,2},{6,4},{8,6},{10,8},{12,10},{14,12},{16,14},{18,16},{20... | collective-permute-start | bytes 393224 | tf_op jit(solution)/shard_map/ppermute | solution.py:28
  139.0 12.0 %collective-permute-start.5 = (f32[1,128,256]{2,1,0:T(8,128)S(1)}, f32[1,128,256]{2,1,0:T(8,128)S(1)}, u32[]{:S(2)}, u32[]{:S(2)}) collective-permute-start(f32[1,128,256]{2,1,0:T(8,128)S(1)} %get-tuple-element.14), channel_id=1, source_target_pairs={{0,2},{2,4},{4,6},{6,8},{8,10},{10,12},{12,14},{14,16},{16,18},{18... | collective-permute-start | bytes 393224 | tf_op jit(solution)/shard_map/ppermute | solution.py:25
  143.7 11.8 %copy-start.4 = (f32[16,128,256]{2,1,0:T(8,128)S(1)}, f32[16,128,256]{2,1,0:T(8,128)}, u32[]{:S(2)}) copy-start(f32[16,128,256]{2,1,0:T(8,128)} %param.8) | copy-start | bytes 6291460
  151.0 6.3 %collective-permute-start.6 = (f32[18,1,256]{2,1,0:T(1,128)S(1)}, f32[18,1,256]{2,1,0:T(1,128)S(1)}, u32[]{:S(2)}, u32[]{:S(2)}) collective-permute-start(f32[18,1,256]{2,1,0:T(1,128)S(1)} %get-tuple-element.4), channel_id=1, source_target_pairs={{1,0},{3,2},{5,4},{7,6},{9,8},{11,10},{13,12},{15,14},{17,16},{19,... | collective-permute-start | bytes 55304 | tf_op jit(solution)/shard_map/ppermute | solution.py:28
  154.1 5.8 %copy-start.1 = (f32[16,128,256]{2,1,0:T(8,128)S(1)}, f32[16,128,256]{2,1,0:T(8,128)}, u32[]{:S(2)}) copy-start(f32[16,128,256]{2,1,0:T(8,128)} %param.9) | copy-start | bytes 6291460
  154.1 5.8 %collective-permute-start.7 = (f32[18,1,256]{2,1,0:T(1,128)S(1)}, f32[18,1,256]{2,1,0:T(1,128)S(1)}, u32[]{:S(2)}, u32[]{:S(2)}) collective-permute-start(f32[18,1,256]{2,1,0:T(1,128)S(1)} %get-tuple-element.3), channel_id=1, source_target_pairs={{0,1},{2,3},{4,5},{6,7},{8,9},{10,11},{12,13},{14,15},{16,17},{18,... | collective-permute-start | bytes 55304 | tf_op jit(solution)/shard_map/ppermute | solution.py:25
where the time goes:
time: 162 us
  waiting for transfers between devices  76.2 us (47%)
  starting transfers between devices  35.8 us (22%)
  matrix products  31.3 us (19%)
  local copies, waits for them, and re-layouts  9.03 us (6%)
  other arithmetic  8.33 us (5%)
    all_to_all x1, waiting for transfers between devices, body(): lax.all_to_all(physical_space, both, split_axis=0, concat_axis=0, tiled=T...  29.1 us
    all_to_all x1, waiting for transfers between devices, body(): lax.all_to_all(spectrum_in, both, split_axis=0, concat_axis=0, tiled=True)  28.8 us
    ppermute x4, waiting for transfers between devices, extended(): lax.ppermute(lax.slice_in_dim(block, block.shape[dim] - width, None, axis...  18.4 us
    ppermute x4, starting transfers between devices, extended(): lax.ppermute(lax.slice_in_dim(block, 0, width, axis=dim), axis, backward)  16.9 us
    dot_general x1, matrix products, body(): jnp.einsum('kgx,grmxj->mkrj', axial_table, resident, precision=maximal_pr...  9.63 us
    dot_general x1, matrix products, body(): jnp.einsum('kgx,mkrj->grmxj', axial_table, radial_returned, precision=max...  7.02 us
    all_to_all x1, starting transfers between devices, body(): lax.all_to_all(physical_space, both, split_axis=0, concat_axis=0, tiled=T...  6.64 us
    ppermute x4, starting transfers between devices, extended(): lax.ppermute(lax.slice_in_dim(block, block.shape[dim] - width, None, axis...  6.56 us
  transfers between devices with their start and end apart: 10, of which 5 were waited for; matrix products, arithmetic and copies ran while one was open for 4% of the time, Pallas kernels for 0%

commit v1 on v0

--- a/solution.py
+++ b/solution.py
@@ -28,6 +28,15 @@
         high = lax.ppermute(lax.slice_in_dim(block, 0, width, axis=dim), axis, backward)
         block = jnp.concatenate([low, block, high], axis=dim)
     return block
+
+
+def radial_neighbour(block, ghost_low, ghost_high):
+    row_index = lax.axis_index("row")
+    send = jnp.where(row_index == 0, block[:, -1:], block[:, :1])
+    received = lax.ppermute(send, "row", [(0, 1), (1, 0)])
+    low = jnp.where(row_index == 0, ghost_low, received)
+    high = jnp.where(row_index == 0, received, ghost_high)
+    return jnp.concatenate([low, block, high], axis=1)
 
 
 def azimuth_basis(extent, mode_ids):
@@ -138,7 +147,12 @@
     own_cells = own_first + jnp.arange(radial_block, dtype=jnp.int32)
     radius = cell_radius(own_cells)[None, :, None]
     axial_pad = extended(axial_vel, (("gz", 0),), 1)
-    radial_flux = extended(radial_vel * radius, (("row", 1),), 1)
+    flux = radial_vel * radius
+    if row_count == 2:
+        no_flux = jnp.zeros_like(flux[:, :1])
+        radial_flux = radial_neighbour(flux, no_flux, no_flux)
+    else:
+        radial_flux = extended(flux, (("row", 1),), 1)
     divergence = 0.5 * (axial_pad[2:] - axial_pad[:-2])
     divergence = divergence + (radial_flux[:, 2:] - radial_flux[:, :-2]) / (2.0 * radius)
     divergence = divergence + (jnp.roll(swirl_vel, -1, 2) - jnp.roll(swirl_vel, 1, 2)) / (
@@ -168,12 +182,18 @@
     returned = lax.all_to_all(physical_space, both, split_axis=0, concat_axis=0, tiled=True)
     returned = returned.reshape(NT, axial_block, radial_block)
     pressure = -jnp.einsum("qxr,tq->xrt", returned, fourier, precision=maximal_precision)
-    padded = extended(pressure, (("gz", 0), ("row", 1)), 1)
-    lower_ghost = jnp.where(row_index == 0, pressure[:, :1], padded[1:-1, :1])
-    upper_ghost = jnp.where(row_index == row_count - 1, pressure[:, -1:], padded[1:-1, -1:])
-    above = jnp.concatenate([pressure[:, 1:], upper_ghost], axis=1)
-    below = jnp.concatenate([lower_ghost, pressure[:, :-1]], axis=1)
-    axial_out = axial_vel - 0.5 * (padded[2:, 1:-1] - padded[:-2, 1:-1])
+    padded = extended(pressure, (("gz", 0),), 1)
+    if row_count == 2:
+        sideways = radial_neighbour(pressure, pressure[:, :1], pressure[:, -1:])
+        above = sideways[:, 2:]
+        below = sideways[:, :-2]
+    else:
+        wide = extended(pressure, (("row", 1),), 1)
+        lower_ghost = jnp.where(row_index == 0, pressure[:, :1], wide[:, :1])
+        upper_ghost = jnp.where(row_index == row_count - 1, pressure[:, -1:], wide[:, -1:])
+        above = jnp.concatenate([pressure[:, 1:], upper_ghost], axis=1)
+        below = jnp.concatenate([lower_ghost, pressure[:, :-1]], axis=1)
+    axial_out = axial_vel - 0.5 * (padded[2:] - padded[:-2])
     radial_projected_velocity = radial_vel - 0.5 * (above - below)
     swirl_out = swirl_vel - (jnp.roll(pressure, -1, 2) - jnp.roll(pressure, 1, 2)) / (
         2.0 * radius * spacing

time: 162 us -> 147 us (0.907)
  blocking collectives: 0 us -> 34.4 us
  waiting for transfers between devices: 76.2 us -> 45 us
  starting transfers between devices: 35.8 us -> 22.3 us
  local copies, waits for them, and re-layouts: 9.03 us -> 7.19 us
    all_to_all x0 -> x1, blocking collectives: none -> 34.4 us  [body(): lax.all_to_all(physical_space, both, split_axis=0, concat_axis=0, tiled=T...]
    all_to_all x1 -> x0, waiting for transfers between devices: 29.1 us -> none  [body(): lax.all_to_all(physical_space, both, split_axis=0, concat_axis=0, tiled=T...]
    all_to_all x1 -> x0, starting transfers between devices: 6.64 us -> none  [body(): lax.all_to_all(physical_space, both, split_axis=0, concat_axis=0, tiled=T...]
    ppermute x4 -> x2, starting transfers between devices: 16.9 us -> 12.2 us  [extended(): lax.ppermute(lax.slice_in_dim(block, 0, width, axis=dim), axis, backward)]
    ppermute x4 -> x2, starting transfers between devices: 6.56 us -> 3.84 us  [extended(): lax.ppermute(lax.slice_in_dim(block, block.shape[dim] - width, None, axis...]
    ppermute x4 -> x2, waiting for transfers between devices: 18.4 us -> 16.2 us  [extended(): lax.ppermute(lax.slice_in_dim(block, block.shape[dim] - width, None, axis...]
    sub x1 -> x0, other arithmetic: 1.78 us -> none  [body(): axial_out = axial_vel - 0.5 * (padded[2:, 1:-1] - padded[:-2, 1:-1])]
  transfers between devices with their start and end apart: 10 -> 7, of which waited for: 5 -> 3; matrix products, arithmetic and copies ran while one was open for 4% -> 3% of each run, Pallas kernels for 0% -> 0%
where the time goes in v1:
time: 147 us
  waiting for transfers between devices  45 us (31%)
  blocking collectives  34.4 us (23%)
  matrix products  29.8 us (20%)
  starting transfers between devices  22.3 us (15%)
  other arithmetic  7.49 us (5%)
  local copies, waits for them, and re-layouts  7.19 us (5%)
    all_to_all x1, blocking collectives, body(): lax.all_to_all(physical_space, both, split_axis=0, concat_axis=0, tiled=T...  34.4 us
    all_to_all x1, waiting for transfers between devices, body(): lax.all_to_all(spectrum_in, both, split_axis=0, concat_axis=0, tiled=True)  28.8 us
    ppermute x2, waiting for transfers between devices, extended(): lax.ppermute(lax.slice_in_dim(block, block.shape[dim] - width, None, axis...  16.2 us
    ppermute x2, starting transfers between devices, extended(): lax.ppermute(lax.slice_in_dim(block, 0, width, axis=dim), axis, backward)  12.2 us
    dot_general x1, matrix products, body(): jnp.einsum('kgx,grmxj->mkrj', axial_table, resident, precision=maximal_pr...  9.63 us
    dot_general x1, matrix products, body(): jnp.einsum('kgx,mkrj->grmxj', axial_table, radial_returned, precision=max...  7.01 us
    all_to_all x1, starting transfers between devices, body(): lax.all_to_all(spectrum_in, both, split_axis=0, concat_axis=0, tiled=True)  4.88 us
    ppermute x2, starting transfers between devices, extended(): lax.ppermute(lax.slice_in_dim(block, block.shape[dim] - width, None, axis...  3.84 us
  transfers between devices with their start and end apart: 7, of which 3 were waited for; matrix products, arithmetic and copies ran while one was open for 3% of the time, Pallas kernels for 0%

profile of v1, /device:TPU:6, one launch (start us, length us, event | category | flops | bytes accessed | tf_op | source)
XLA Modules:
  0.0 147.0 jit_solution(5731216051464818345)
XLA Ops:
  0.6 0.0 copy-start.3
  0.7 0.0 copy-start
  0.7 2.0 %broadcast_multiply_fusion = f32[16,128,256]{2,1,0:T(8,128)S(1)} fusion(f32[16,128,256]{2,1,0:T(8,128)} %param.9, f32[128]{0:T(128)S(1)} %convert_add_fusion), kind=kLoop, calls=%fused_computation.43 | loop fusion | flops 524288 | bytes 4194816 | tf_op jit(solution)/shard_map/mul | solution.py:150
  2.7 0.9 collective-permute-start.2
  3.6 0.0 copy-done.3
  3.6 8.1 %collective-permute-start = (f32[1,128,256]{2,1,0:T(8,128)S(1)}, f32[1,128,256]{2,1,0:T(8,128)S(1)}, u32[]{:S(2)}, u32[]{:S(2)}) collective-permute-start(f32[1,128,256]{2,1,0:T(8,128)S(1)} %get-tuple-element.17), channel_id=1, source_target_pairs={{2,0},{4,2},{6,4},{8,6},{10,8},{12,10},{14,12},{16,14},{18,16},{20... | collective-permute-start | bytes 393224 | tf_op jit(solution)/shard_map/ppermute | solution.py:28
  11.8 1.9 %collective-permute-start.1 = (f32[1,128,256]{2,1,0:T(8,128)S(1)}, f32[1,128,256]{2,1,0:T(8,128)S(1)}, u32[]{:S(2)}, u32[]{:S(2)}) collective-permute-start(f32[1,128,256]{2,1,0:T(8,128)S(1)} %get-tuple-element.18), channel_id=1, source_target_pairs={{0,2},{2,4},{4,6},{6,8},{8,10},{10,12},{12,14},{14,16},{16,18},{18... | collective-permute-start | bytes 393224 | tf_op jit(solution)/shard_map/ppermute | solution.py:25
  13.7 0.0 copy-done
  13.7 0.7 fusion.51
  14.4 0.0 copy-start.7
  14.4 0.0 copy-start.5
  14.5 0.0 copy-start.8
  14.5 0.4 fusion.50
  14.9 0.2 copy-done.7
  15.1 0.1 select_reduce_fusion
  15.2 0.0 collective-permute-done.2
  15.2 0.0 collective-permute-done
  15.2 8.5 %collective-permute-done.1 = f32[1,128,256]{2,1,0:T(8,128)S(1)} collective-permute-done((f32[1,128,256]{2,1,0:T(8,128)S(1)}, f32[1,128,256]{2,1,0:T(8,128)S(1)}, u32[]{:S(2)}, u32[]{:S(2)}) %collective-permute-start.1) | collective-permute-done | bytes 131104 | tf_op jit(solution)/shard_map/ppermute | solution.py:25
  23.8 0.0 copy-done.5
  23.8 3.3 %fusion.22 = f32[256,16,128]{2,0,1:T(8,128)S(1)} fusion(f32[256,256,1]{0,1,2:T(8,128)S(1)} %copy-done.5, f32[16,128,256]{2,1,0:T(8,128)S(1)} %broadcast_multiply_fusion, f32[16,1,256]{2,1,0:T(1,128)S(1)} %get-tuple-element.20, f32[16,1,256]{2,1,0:T(1,128)S(1)} %get-tuple-element.19, f32[16,128,256]{2,1,0:T(8,128)S(1)} %copy-done.3, ...), kind=kOutput, calls=%fused_computation.32 | convolution fusion | flops 1619525632 | bytes 13142016 | tf_op jit(solution)/shard_map/xrt,tm->mxr/dot_general | solution.py:164
  27.1 2.5 %copy.20 = f32[128,2,16,128]{3,2,1,0:T(8,128)} copy(f32[128,2,16,128]{3,1,0,2:T(2,128)S(1)} %bitcast.37) | data formatting | bytes 4194304 | tf_op jit(solution)/shard_map/reshape | solution.py:166
  29.6 4.9 %all-to-all-start = ((f32[128,2,16,128]{3,2,1,0:T(8,128)}), f32[128,2,16,128]{3,2,1,0:T(8,128)}, u32[]{:S(2)}, u32[]{:S(2)}) async-start(f32[128,2,16,128]{3,2,1,0:T(8,128)} %copy.20), calls=%async_computation | async-start | bytes 4194304 | tf_op jit(solution)/shard_map/all_to_all | solution.py:167
  34.6 0.1 broadcast_add_fusion
  34.7 28.8 %all-to-all-done = f32[128,2,16,128]{3,2,1,0:T(8,128)} async-done(((f32[128,2,16,128]{3,2,1,0:T(8,128)}), f32[128,2,16,128]{3,2,1,0:T(8,128)}, u32[]{:S(2)}, u32[]{:S(2)}) %all-to-all-start) | async-done | bytes 2097184 | tf_op jit(solution)/shard_map/all_to_all | solution.py:167
  63.5 9.6 %fusion.53 = f32[2,2,128,1024,1]{3,2,1,0,4:T(8,128)S(1)} fusion(f32[64,2,2,16,128]{4,3,2,1,0:T(8,128)} %bitcast.2, f32[1024,64,16,1,1]{0,2,4,3,1:T(8,128)} %constant.77), kind=kOutput, calls=%fused_computation.81 | convolution fusion | flops 6442450944 | bytes 8388608 | tf_op jit(solution)/shard_map/kgx,grmxj->mkrj/dot_general | solution.py:172
  73.1 0.0 copy-start.6
  73.1 0.2 copy.31
  73.4 0.7 copy-done.6
  74.1 3.7 %fusion.54 = f32[2,1024,256]{2,1,0:T(8,128)S(1)} fusion(f32[2,1024,256]{1,2,0:T(8,128)S(1)} %bitcast.34, f32[256,256,1]{1,0,2:T(8,128)S(1)} %copy-done.6), kind=kOutput, calls=%fused_computation.82 | convolution fusion | flops 1610612736 | bytes 4456448 | tf_op jit(solution)/shard_map/sj,mkj->mks/dot_general | solution.py:175
  77.7 0.0 copy-start.2
  77.7 2.4 %fusion.18 = f32[2,1024,256]{1,2,0:T(8,128)S(1)} fusion(f32[256,256,1]{1,0,2:T(8,128)S(1)} %copy-done.6, f32[2,1024,256]{2,1,0:T(8,128)S(1)} %fusion.54, f32[256]{0:T(256)S(1)} %multiply_subtract_fusion.1, f32[2,1024]{1,0:T(2,128)S(1)} %broadcast_add_fusion), kind=kOutput, calls=%fused_computation.28 | convolution fusion | flops 1612185600 | bytes 4465664 | tf_op jit(solution)/shard_map/sj,mks->mkj/dot_general | solution.py:177
  80.1 7.0 %convolution_bitcast_fusion = f32[64,2,2,16,128]{4,0,3,1,2:T(8,128)S(1)} fusion(f32[2,1024,2,128,1]{1,3,4,2,0:T(8,128)S(1)} %bitcast.36, f32[1024,64,16,1,1]{0,1,2,4,3:T(8,128)S(1)} %copy-done.2), kind=kOutput, calls=%fused_computation.33 | convolution fusion | flops 6442450944 | bytes 8388608 | tf_op jit(solution)/shard_map/kgx,mkrj->grmxj/dot_general | solution.py:179
  87.2 1.2 copy.26
  88.4 34.4 %all_to_all.10 = f32[128,2,16,128]{3,2,1,0:T(8,128)S(1)} all-to-all(f32[128,2,16,128]{3,2,1,0:T(8,128)S(1)} %bitcast.35), channel_id=1, replica_groups=mesh['gz'=64,'row'=2] {'gz','row'}, dimensions={0} | all-to-all | bytes 4194304 | tf_op jit(solution)/shard_map/all_to_all | solution.py:182
  122.8 3.8 %fusion.24 = f32[16,128,256]{2,1,0:T(8,128)S(1)} fusion(f32[256,256,1]{0,1,2:T(8,128)S(1)} %copy-done.5, f32[256,16,128]{2,1,0:T(8,128)S(1)} %bitcast.33), kind=kOutput, calls=%fused_computation.34 | convolution fusion | flops 1611137024 | bytes 4456448 | tf_op jit(solution)/shard_map/qxr,tq->xrt/dot_general | solution.py:184
  126.6 0.7 fusion.48
  127.3 0.4 fusion.47
  127.7 0.4 collective-permute-start.5
  128.2 4.1 %collective-permute-start.3 = (f32[1,128,256]{2,1,0:T(8,128)S(1)}, f32[1,128,256]{2,1,0:T(8,128)S(1)}, u32[]{:S(2)}, u32[]{:S(2)}) collective-permute-start(f32[1,128,256]{2,1,0:T(8,128)S(1)} %get-tuple-element.11), channel_id=1, source_target_pairs={{2,0},{4,2},{6,4},{8,6},{10,8},{12,10},{14,12},{16,14},{18,16},{20... | collective-permute-start | bytes 393224 | tf_op jit(solution)/shard_map/ppermute | solution.py:28
  132.3 1.9 %collective-permute-start.4 = (f32[1,128,256]{2,1,0:T(8,128)S(1)}, f32[1,128,256]{2,1,0:T(8,128)S(1)}, u32[]{:S(2)}, u32[]{:S(2)}) collective-permute-start(f32[1,128,256]{2,1,0:T(8,128)S(1)} %get-tuple-element.12), channel_id=1, source_target_pairs={{0,2},{2,4},{4,6},{6,8},{8,10},{10,12},{12,14},{14,16},{16,18},{18... | collective-permute-start | bytes 393224 | tf_op jit(solution)/shard_map/ppermute | solution.py:25
  134.2 0.0 copy-start.1
  134.2 0.0 copy-start.4
  134.2 2.3 %fusion.15 = f32[16,128,256]{2,1,0:T(8,128)} fusion(f32[16,128,256]{2,1,0:T(8,128)S(1)} %copy-done, f32[16,128,1]{2,1,0:T(8,128)S(1)} %get-tuple-element.6, f32[16,128,255]{2,1,0:T(8,128)S(1)} %get-tuple-element.8, f32[16,128,255]{2,1,0:T(8,128)S(1)} %get-tuple-element.7, f32[16,128,1]{2,1,0:T(8,128)S(1)} %get-tuple-element.5, f32[128]{0:T(128)S(1)} %get-tuple-element.21), kind=kLoop, calls=%fused_computation.25 | loop fusion | flops 2621440 | bytes 8389120 | tf_op jit(solution)/shard_map/sub | solution.py:198
  136.6 0.0 collective-permute-done.5
  136.6 0.0 collective-permute-done.3
  136.6 7.7 %collective-permute-done.4 = f32[1,128,256]{2,1,0:T(8,128)S(1)} collective-permute-done((f32[1,128,256]{2,1,0:T(8,128)S(1)}, f32[1,128,256]{2,1,0:T(8,128)S(1)}, u32[]{:S(2)}, u32[]{:S(2)}) %collective-permute-start.4) | collective-permute-done | bytes 131104 | tf_op jit(solution)/shard_map/ppermute | solution.py:25
  144.3 0.0 copy-done.1
  144.3 2.7 %fusion.2 = (f32[16,128,256]{2,1,0:T(8,128)}, f32[16,128,256]{2,1,0:T(8,128)}) fusion(f32[16,128,256]{2,1,0:T(8,128)S(1)} %copy-done.1, f32[16,128,256]{2,1,0:T(8,128)S(1)} %fusion.24, f32[16,1,256]{2,1,0:T(1,128)S(1)} %get-tuple-element.4, f32[16,1,256]{2,1,0:T(1,128)S(1)} %get-tuple-element.3, f32[16,128,256]{2,1,0:T(8,128)S(1)} %copy-done.4, ...), kind=kLoop, calls=%fused_computation.3 | loop fusion | flops 5242880 | bytes 10780672 | tf_op jit(solution)/shard_map/sub | solution.py:197
  (15 shorter events, 0.3 us)
Async XLA Ops:
  0.6 3.0 %copy-start.3 = (f32[16,128,256]{2,1,0:T(8,128)S(1)}, f32[16,128,256]{2,1,0:T(8,128)}, u32[]{:S(2)}) copy-start(f32[16,128,256]{2,1,0:T(8,128)} %param.8) | copy-start | bytes 6291460
  0.7 13.0 %copy-start = (f32[16,128,256]{2,1,0:T(8,128)S(1)}, f32[16,128,256]{2,1,0:T(8,128)}, u32[]{:S(2)}) copy-start(f32[16,128,256]{2,1,0:T(8,128)} %param.10) | copy-start | bytes 6291460
  2.7 12.5 %collective-permute-start.2 = (f32[16,1,256]{2,1,0:T(1,128)S(1)}, f32[16,1,256]{2,1,0:T(1,128)S(1)}, u32[]{:S(2)}, u32[]{:S(2)}) collective-permute-start(f32[16,1,256]{2,1,0:T(1,128)S(1)} %broadcast_select_fusion.5), channel_id=1, source_target_pairs={{0,1},{1,0},{2,3},{3,2},{4,5},{5,4},{6,7},{7,6},{8,9},{9,8},{10,11... | collective-permute-start | bytes 49160 | tf_op jit(solution)/shard_map/ppermute | solution.py:36
  3.6 11.6 %collective-permute-start = (f32[1,128,256]{2,1,0:T(8,128)S(1)}, f32[1,128,256]{2,1,0:T(8,128)S(1)}, u32[]{:S(2)}, u32[]{:S(2)}) collective-permute-start(f32[1,128,256]{2,1,0:T(8,128)S(1)} %get-tuple-element.17), channel_id=1, source_target_pairs={{2,0},{4,2},{6,4},{8,6},{10,8},{12,10},{14,12},{16,14},{18,16},{20... | collective-permute-start | bytes 393224 | tf_op jit(solution)/shard_map/ppermute | solution.py:28
  11.8 12.0 %collective-permute-start.1 = (f32[1,128,256]{2,1,0:T(8,128)S(1)}, f32[1,128,256]{2,1,0:T(8,128)S(1)}, u32[]{:S(2)}, u32[]{:S(2)}) collective-permute-start(f32[1,128,256]{2,1,0:T(8,128)S(1)} %get-tuple-element.18), channel_id=1, source_target_pairs={{0,2},{2,4},{4,6},{6,8},{8,10},{10,12},{12,14},{14,16},{16,18},{18... | collective-permute-start | bytes 393224 | tf_op jit(solution)/shard_map/ppermute | solution.py:25
  14.4 0.7 copy-start.7
  14.4 9.3 %copy-start.5 = (f32[256,256,1]{0,1,2:T(8,128)S(1)}, f32[256,256,1]{0,1,2:T(8,128)}, u32[]{:S(2)}) copy-start(f32[256,256,1]{0,1,2:T(8,128)} %constant.76) | copy-start | bytes 786436
  14.5 9.3 %copy-start.8 = (s32[16,128,256]{2,1,0:T(8,128)S(1)}, s32[16,128,256]{2,1,0:T(8,128)}, u32[]{:S(2)}) copy-start(s32[16,128,256]{2,1,0:T(8,128)} %param.12) | copy-start | bytes 6291460
  29.6 33.9 %all-to-all-start = ((f32[128,2,16,128]{3,2,1,0:T(8,128)}), f32[128,2,16,128]{3,2,1,0:T(8,128)}, u32[]{:S(2)}, u32[]{:S(2)}) async-start(f32[128,2,16,128]{3,2,1,0:T(8,128)} %copy.20), calls=%async_computation | async-start | bytes 4194304 | tf_op jit(solution)/shard_map/all_to_all | solution.py:167
  73.1 1.0 copy-start.6
  77.7 2.4 %copy-start.2 = (f32[1024,64,16,1,1]{0,1,2,4,3:T(8,128)S(1)}, f32[1024,64,16,1,1]{0,1,2,4,3:T(8,128)}, u32[]{:S(2)}) copy-start(f32[1024,64,16,1,1]{0,1,2,4,3:T(8,128)} %constant.80) | copy-start | bytes 12582916
  127.7 8.8 %collective-permute-start.5 = (f32[16,1,256]{2,1,0:T(1,128)S(1)}, f32[16,1,256]{2,1,0:T(1,128)S(1)}, u32[]{:S(2)}, u32[]{:S(2)}) collective-permute-start(f32[16,1,256]{2,1,0:T(1,128)S(1)} %broadcast_select_fusion.2), channel_id=1, source_target_pairs={{0,1},{1,0},{2,3},{3,2},{4,5},{5,4},{6,7},{7,6},{8,9},{9,8},{10,11... | collective-permute-start | bytes 49160 | tf_op jit(solution)/shard_map/ppermute | solution.py:36
  128.2 8.4 %collective-permute-start.3 = (f32[1,128,256]{2,1,0:T(8,128)S(1)}, f32[1,128,256]{2,1,0:T(8,128)S(1)}, u32[]{:S(2)}, u32[]{:S(2)}) collective-permute-start(f32[1,128,256]{2,1,0:T(8,128)S(1)} %get-tuple-element.11), channel_id=1, source_target_pairs={{2,0},{4,2},{6,4},{8,6},{10,8},{12,10},{14,12},{16,14},{18,16},{20... | collective-permute-start | bytes 393224 | tf_op jit(solution)/shard_map/ppermute | solution.py:28
  132.3 12.0 %collective-permute-start.4 = (f32[1,128,256]{2,1,0:T(8,128)S(1)}, f32[1,128,256]{2,1,0:T(8,128)S(1)}, u32[]{:S(2)}, u32[]{:S(2)}) collective-permute-start(f32[1,128,256]{2,1,0:T(8,128)S(1)} %get-tuple-element.12), channel_id=1, source_target_pairs={{0,2},{2,4},{4,6},{6,8},{8,10},{10,12},{12,14},{14,16},{16,18},{18... | collective-permute-start | bytes 393224 | tf_op jit(solution)/shard_map/ppermute | solution.py:25
  134.2 10.1 %copy-start.1 = (f32[16,128,256]{2,1,0:T(8,128)S(1)}, f32[16,128,256]{2,1,0:T(8,128)}, u32[]{:S(2)}) copy-start(f32[16,128,256]{2,1,0:T(8,128)} %param.9) | copy-start | bytes 6291460
  134.2 10.1 %copy-start.4 = (f32[16,128,256]{2,1,0:T(8,128)S(1)}, f32[16,128,256]{2,1,0:T(8,128)}, u32[]{:S(2)}) copy-start(f32[16,128,256]{2,1,0:T(8,128)} %param.8) | copy-start | bytes 6291460

commit v2 on v1

--- a/solution.py
+++ b/solution.py
@@ -15,6 +15,7 @@
 
 helmholtz_shift = 0.001
 maximal_precision = lax.Precision.HIGHEST
+forward_precision = lax.Precision.HIGH
 
 
 def extended(block, sides, width):
@@ -161,7 +162,7 @@
     right_side = divergence - canopy_source(canopy_gore, inflow_rate)
     all_modes = jnp.arange(NT, dtype=jnp.int32)
     fourier = jnp.asarray(AZIMUTH_TABLE)
-    spectrum_in = jnp.einsum("xrt,tm->mxr", right_side, fourier, precision=maximal_precision)
+    spectrum_in = jnp.einsum("xrt,tm->mxr", right_side, fourier, precision=forward_precision)
     modes_each = NT // device_count
     spectrum_in = spectrum_in.reshape(device_count, modes_each, axial_block, radial_block)
     resident = lax.all_to_all(spectrum_in, both, split_axis=0, concat_axis=0, tiled=True)
@@ -170,9 +171,9 @@
     axial_table = jnp.asarray(AXIAL_TABLE).reshape(NX, gz_count, axial_block)
     radial_table = jnp.asarray(RADIAL_TABLE)
     axial_coefficient = jnp.einsum(
-        "kgx,grmxj->mkrj", axial_table, resident, precision=maximal_precision
+        "kgx,grmxj->mkrj", axial_table, resident, precision=forward_precision
     ).reshape(modes_each, NX, NR)
-    spectrum = jnp.einsum("sj,mkj->mks", radial_table, axial_coefficient, precision=maximal_precision)
+    spectrum = jnp.einsum("sj,mkj->mks", radial_table, axial_coefficient, precision=forward_precision)
     scaled = spectrum / denominator_of(mode_ids, jnp.arange(NR, dtype=jnp.int32))
     radial_returned = jnp.einsum("sj,mks->mkj", radial_table, scaled, precision=maximal_precision)
     radial_returned = radial_returned.reshape(modes_each, NX, row_count, radial_block)

time: 147 us -> 141 us (0.959)
  matrix products: 29.8 us -> 23.6 us
    dot_general x3, matrix products: 16.5 us -> 10.6 us  [the longest x1 6.33 us: body(): jnp.einsum('kgx,grmxj->mkrj', axial_table, resident, precision=forward_pr...]
where the time goes in v2:
time: 141 us
  waiting for transfers between devices  45 us (32%)
  blocking collectives  34.4 us (24%)
  matrix products  23.6 us (17%)
  starting transfers between devices  22.3 us (16%)
  other arithmetic  7.49 us (5%)
  local copies, waits for them, and re-layouts  7.41 us (5%)
    all_to_all x1, blocking collectives, body(): lax.all_to_all(physical_space, both, split_axis=0, concat_axis=0, tiled=T...  34.4 us
    all_to_all x1, waiting for transfers between devices, body(): lax.all_to_all(spectrum_in, both, split_axis=0, concat_axis=0, tiled=True)  28.8 us
    ppermute x2, waiting for transfers between devices, extended(): lax.ppermute(lax.slice_in_dim(block, block.shape[dim] - width, None, axis...  16.2 us
    ppermute x2, starting transfers between devices, extended(): lax.ppermute(lax.slice_in_dim(block, 0, width, axis=dim), axis, backward)  12.2 us
    dot_general x1, matrix products, body(): jnp.einsum('kgx,mkrj->grmxj', axial_table, radial_returned, precision=max...  6.77 us
    dot_general x1, matrix products, body(): jnp.einsum('kgx,grmxj->mkrj', axial_table, resident, precision=forward_pr...  6.33 us
    all_to_all x1, starting transfers between devices, body(): lax.all_to_all(spectrum_in, both, split_axis=0, concat_axis=0, tiled=True)  4.88 us
    ppermute x2, starting transfers between devices, extended(): lax.ppermute(lax.slice_in_dim(block, block.shape[dim] - width, None, axis...  3.84 us
  transfers between devices with their start and end apart: 7, of which 3 were waited for; matrix products, arithmetic and copies ran while one was open for 3% of the time, Pallas kernels for 0%

profile of v2, /device:TPU:6, one launch (start us, length us, event | category | flops | bytes accessed | tf_op | source)
XLA Modules:
  0.0 141.0 jit_solution(15461797871268169940)
XLA Ops:
  0.6 0.0 copy-start.3
  0.7 0.0 copy-start
  0.7 2.0 %broadcast_multiply_fusion = f32[16,128,256]{2,1,0:T(8,128)S(1)} fusion(f32[16,128,256]{2,1,0:T(8,128)} %param.9, f32[128]{0:T(128)S(1)} %convert_add_fusion), kind=kLoop, calls=%fused_computation.43 | loop fusion | flops 524288 | bytes 4194816 | tf_op jit(solution)/shard_map/mul | solution.py:151
  2.7 0.9 collective-permute-start.2
  3.6 0.0 copy-done.3
  3.6 8.1 %collective-permute-start = (f32[1,128,256]{2,1,0:T(8,128)S(1)}, f32[1,128,256]{2,1,0:T(8,128)S(1)}, u32[]{:S(2)}, u32[]{:S(2)}) collective-permute-start(f32[1,128,256]{2,1,0:T(8,128)S(1)} %get-tuple-element.17), channel_id=1, source_target_pairs={{2,0},{4,2},{6,4},{8,6},{10,8},{12,10},{14,12},{16,14},{18,16},{20... | collective-permute-start | bytes 393224 | tf_op jit(solution)/shard_map/ppermute | solution.py:29
  11.8 1.9 %collective-permute-start.1 = (f32[1,128,256]{2,1,0:T(8,128)S(1)}, f32[1,128,256]{2,1,0:T(8,128)S(1)}, u32[]{:S(2)}, u32[]{:S(2)}) collective-permute-start(f32[1,128,256]{2,1,0:T(8,128)S(1)} %get-tuple-element.18), channel_id=1, source_target_pairs={{0,2},{2,4},{4,6},{6,8},{8,10},{10,12},{12,14},{14,16},{16,18},{18... | collective-permute-start | bytes 393224 | tf_op jit(solution)/shard_map/ppermute | solution.py:26
  13.7 0.0 copy-done
  13.7 0.7 fusion.51
  14.4 0.0 copy-start.7
  14.4 0.0 copy-start.5
  14.5 0.0 copy-start.8
  14.5 0.4 fusion.50
  14.9 0.2 copy-done.7
  15.1 0.1 select_reduce_fusion
  15.2 0.0 collective-permute-done.2
  15.2 0.0 collective-permute-done
  15.2 8.5 %collective-permute-done.1 = f32[1,128,256]{2,1,0:T(8,128)S(1)} collective-permute-done((f32[1,128,256]{2,1,0:T(8,128)S(1)}, f32[1,128,256]{2,1,0:T(8,128)S(1)}, u32[]{:S(2)}, u32[]{:S(2)}) %collective-permute-start.1) | collective-permute-done | bytes 131104 | tf_op jit(solution)/shard_map/ppermute | solution.py:26
  23.8 0.0 copy-done.5
  23.8 0.0 copy-done.8
  23.8 2.4 %fusion.22 = f32[256,16,128]{2,0,1:T(8,128)S(1)} fusion(f32[256,256,1]{0,1,2:T(8,128)S(1)} %copy-done.5, f32[16,128,256]{2,1,0:T(8,128)S(1)} %broadcast_multiply_fusion, f32[16,1,256]{2,1,0:T(1,128)S(1)} %get-tuple-element.20, f32[16,1,256]{2,1,0:T(1,128)S(1)} %get-tuple-element.19, f32[16,128,256]{2,1,0:T(8,128)S(1)} %copy-done.3, ...), kind=kOutput, calls=%fused_computation.32 | convolution fusion | flops 814219264 | bytes 13142016 | tf_op jit(solution)/shard_map/xrt,tm->mxr/dot_general | solution.py:165
  26.2 2.5 %copy.20 = f32[128,2,16,128]{3,2,1,0:T(8,128)} copy(f32[128,2,16,128]{3,1,0,2:T(2,128)S(1)} %bitcast.37) | data formatting | bytes 4194304 | tf_op jit(solution)/shard_map/reshape | solution.py:167
  28.7 4.9 %all-to-all-start = ((f32[128,2,16,128]{3,2,1,0:T(8,128)}), f32[128,2,16,128]{3,2,1,0:T(8,128)}, u32[]{:S(2)}, u32[]{:S(2)}) async-start(f32[128,2,16,128]{3,2,1,0:T(8,128)} %copy.20), calls=%async_computation | async-start | bytes 4194304 | tf_op jit(solution)/shard_map/all_to_all | solution.py:168
  33.8 0.1 broadcast_add_fusion
  33.8 28.8 %all-to-all-done = f32[128,2,16,128]{3,2,1,0:T(8,128)} async-done(((f32[128,2,16,128]{3,2,1,0:T(8,128)}), f32[128,2,16,128]{3,2,1,0:T(8,128)}, u32[]{:S(2)}, u32[]{:S(2)}) %all-to-all-start) | async-done | bytes 2097184 | tf_op jit(solution)/shard_map/all_to_all | solution.py:168
  62.6 6.3 %fusion.53 = f32[2,2,128,1024,1]{3,2,1,0,4:T(8,128)S(1)} fusion(f32[64,2,2,16,128]{4,3,2,1,0:T(8,128)} %bitcast.2, f32[1024,64,16,1,1]{0,2,4,3,1:T(8,128)} %constant.77), kind=kOutput, calls=%fused_computation.81 | convolution fusion | flops 3221225472 | bytes 8388608 | tf_op jit(solution)/shard_map/kgx,grmxj->mkrj/dot_general | solution.py:173
  68.9 0.0 copy-start.6
  69.0 0.1 copy.31
  69.1 0.8 copy-done.6
  69.9 1.9 %fusion.54 = f32[2,1024,256]{2,1,0:T(8,128)S(1)} fusion(f32[2,1024,256]{1,2,0:T(8,128)S(1)} %bitcast.34, f32[256,256,1]{1,0,2:T(8,128)S(1)} %copy-done.6), kind=kOutput, calls=%fused_computation.82 | convolution fusion | flops 805306368 | bytes 4456448 | tf_op jit(solution)/shard_map/sj,mkj->mks/dot_general | solution.py:176
  71.8 0.0 copy-start.2
  71.8 2.4 %fusion.18 = f32[2,1024,256]{1,2,0:T(8,128)S(1)} fusion(f32[256,256,1]{1,0,2:T(8,128)S(1)} %copy-done.6, f32[2,1024,256]{2,1,0:T(8,128)S(1)} %fusion.54, f32[256]{0:T(256)S(1)} %multiply_subtract_fusion.1, f32[2,1024]{1,0:T(2,128)S(1)} %broadcast_add_fusion), kind=kOutput, calls=%fused_computation.28 | convolution fusion | flops 1612185600 | bytes 4465664 | tf_op jit(solution)/shard_map/sj,mks->mkj/dot_general | solution.py:178
  74.2 6.8 %convolution_bitcast_fusion = f32[64,2,2,16,128]{4,0,3,1,2:T(8,128)S(1)} fusion(f32[2,1024,2,128,1]{1,3,4,2,0:T(8,128)S(1)} %bitcast.36, f32[1024,64,16,1,1]{0,1,2,4,3:T(8,128)S(1)} %copy-done.2), kind=kOutput, calls=%fused_computation.33 | convolution fusion | flops 6442450944 | bytes 8388608 | tf_op jit(solution)/shard_map/kgx,mkrj->grmxj/dot_general | solution.py:180
  81.0 1.4 %copy.26 = f32[64,2,2,16,128]{4,3,2,1,0:T(8,128)S(1)} copy(f32[64,2,2,16,128]{4,0,3,1,2:T(8,128)S(1)} %convolution_bitcast_fusion) | data formatting | bytes 4194304 | tf_op jit(solution)/shard_map/kgx,mkrj->grmxj/transpose | solution.py:180
  82.4 34.4 %all_to_all.10 = f32[128,2,16,128]{3,2,1,0:T(8,128)S(1)} all-to-all(f32[128,2,16,128]{3,2,1,0:T(8,128)S(1)} %bitcast.35), channel_id=1, replica_groups=mesh['gz'=64,'row'=2] {'gz','row'}, dimensions={0} | all-to-all | bytes 4194304 | tf_op jit(solution)/shard_map/all_to_all | solution.py:183
  116.8 3.8 %fusion.24 = f32[16,128,256]{2,1,0:T(8,128)S(1)} fusion(f32[256,256,1]{0,1,2:T(8,128)S(1)} %copy-done.5, f32[256,16,128]{2,1,0:T(8,128)S(1)} %bitcast.33), kind=kOutput, calls=%fused_computation.34 | convolution fusion | flops 1611137024 | bytes 4456448 | tf_op jit(solution)/shard_map/qxr,tq->xrt/dot_general | solution.py:185
  120.6 0.7 fusion.48
  121.3 0.4 fusion.47
  121.8 0.4 collective-permute-start.5
  122.2 4.1 %collective-permute-start.3 = (f32[1,128,256]{2,1,0:T(8,128)S(1)}, f32[1,128,256]{2,1,0:T(8,128)S(1)}, u32[]{:S(2)}, u32[]{:S(2)}) collective-permute-start(f32[1,128,256]{2,1,0:T(8,128)S(1)} %get-tuple-element.11), channel_id=1, source_target_pairs={{2,0},{4,2},{6,4},{8,6},{10,8},{12,10},{14,12},{16,14},{18,16},{20... | collective-permute-start | bytes 393224 | tf_op jit(solution)/shard_map/ppermute | solution.py:29
  126.3 1.9 %collective-permute-start.4 = (f32[1,128,256]{2,1,0:T(8,128)S(1)}, f32[1,128,256]{2,1,0:T(8,128)S(1)}, u32[]{:S(2)}, u32[]{:S(2)}) collective-permute-start(f32[1,128,256]{2,1,0:T(8,128)S(1)} %get-tuple-element.12), channel_id=1, source_target_pairs={{0,2},{2,4},{4,6},{6,8},{8,10},{10,12},{12,14},{14,16},{16,18},{18... | collective-permute-start | bytes 393224 | tf_op jit(solution)/shard_map/ppermute | solution.py:26
  128.2 0.0 copy-start.1
  128.2 0.0 copy-start.4
  128.3 2.3 %fusion.15 = f32[16,128,256]{2,1,0:T(8,128)} fusion(f32[16,128,256]{2,1,0:T(8,128)S(1)} %copy-done, f32[16,128,1]{2,1,0:T(8,128)S(1)} %get-tuple-element.6, f32[16,128,255]{2,1,0:T(8,128)S(1)} %get-tuple-element.8, f32[16,128,255]{2,1,0:T(8,128)S(1)} %get-tuple-element.7, f32[16,128,1]{2,1,0:T(8,128)S(1)} %get-tuple-element.5, f32[128]{0:T(128)S(1)} %get-tuple-element.21), kind=kLoop, calls=%fused_computation.25 | loop fusion | flops 2621440 | bytes 8389120 | tf_op jit(solution)/shard_map/sub | solution.py:199
  130.6 0.0 collective-permute-done.5
  130.6 0.0 collective-permute-done.3
  130.6 7.7 %collective-permute-done.4 = f32[1,128,256]{2,1,0:T(8,128)S(1)} collective-permute-done((f32[1,128,256]{2,1,0:T(8,128)S(1)}, f32[1,128,256]{2,1,0:T(8,128)S(1)}, u32[]{:S(2)}, u32[]{:S(2)}) %collective-permute-start.4) | collective-permute-done | bytes 131104 | tf_op jit(solution)/shard_map/ppermute | solution.py:26
  138.3 2.7 %fusion.2 = (f32[16,128,256]{2,1,0:T(8,128)}, f32[16,128,256]{2,1,0:T(8,128)}) fusion(f32[16,128,256]{2,1,0:T(8,128)S(1)} %copy-done.1, f32[16,128,256]{2,1,0:T(8,128)S(1)} %fusion.24, f32[16,1,256]{2,1,0:T(1,128)S(1)} %get-tuple-element.4, f32[16,1,256]{2,1,0:T(1,128)S(1)} %get-tuple-element.3, f32[16,128,256]{2,1,0:T(8,128)S(1)} %copy-done.4, ...), kind=kLoop, calls=%fused_computation.3 | loop fusion | flops 5242880 | bytes 10780672 | tf_op jit(solution)/shard_map/sub | solution.py:198
  (15 shorter events, 0.3 us)
Async XLA Ops:
  0.6 3.0 %copy-start.3 = (f32[16,128,256]{2,1,0:T(8,128)S(1)}, f32[16,128,256]{2,1,0:T(8,128)}, u32[]{:S(2)}) copy-start(f32[16,128,256]{2,1,0:T(8,128)} %param.8) | copy-start | bytes 6291460
  0.7 13.0 %copy-start = (f32[16,128,256]{2,1,0:T(8,128)S(1)}, f32[16,128,256]{2,1,0:T(8,128)}, u32[]{:S(2)}) copy-start(f32[16,128,256]{2,1,0:T(8,128)} %param.10) | copy-start | bytes 6291460
  2.7 12.5 %collective-permute-start.2 = (f32[16,1,256]{2,1,0:T(1,128)S(1)}, f32[16,1,256]{2,1,0:T(1,128)S(1)}, u32[]{:S(2)}, u32[]{:S(2)}) collective-permute-start(f32[16,1,256]{2,1,0:T(1,128)S(1)} %broadcast_select_fusion.5), channel_id=1, source_target_pairs={{0,1},{1,0},{2,3},{3,2},{4,5},{5,4},{6,7},{7,6},{8,9},{9,8},{10,11... | collective-permute-start | bytes 49160 | tf_op jit(solution)/shard_map/ppermute | solution.py:37
  3.6 11.6 %collective-permute-start = (f32[1,128,256]{2,1,0:T(8,128)S(1)}, f32[1,128,256]{2,1,0:T(8,128)S(1)}, u32[]{:S(2)}, u32[]{:S(2)}) collective-permute-start(f32[1,128,256]{2,1,0:T(8,128)S(1)} %get-tuple-element.17), channel_id=1, source_target_pairs={{2,0},{4,2},{6,4},{8,6},{10,8},{12,10},{14,12},{16,14},{18,16},{20... | collective-permute-start | bytes 393224 | tf_op jit(solution)/shard_map/ppermute | solution.py:29
  11.8 12.0 %collective-permute-start.1 = (f32[1,128,256]{2,1,0:T(8,128)S(1)}, f32[1,128,256]{2,1,0:T(8,128)S(1)}, u32[]{:S(2)}, u32[]{:S(2)}) collective-permute-start(f32[1,128,256]{2,1,0:T(8,128)S(1)} %get-tuple-element.18), channel_id=1, source_target_pairs={{0,2},{2,4},{4,6},{6,8},{8,10},{10,12},{12,14},{14,16},{16,18},{18... | collective-permute-start | bytes 393224 | tf_op jit(solution)/shard_map/ppermute | solution.py:26
  14.4 0.7 copy-start.7
  14.4 9.3 %copy-start.5 = (f32[256,256,1]{0,1,2:T(8,128)S(1)}, f32[256,256,1]{0,1,2:T(8,128)}, u32[]{:S(2)}) copy-start(f32[256,256,1]{0,1,2:T(8,128)} %constant.76) | copy-start | bytes 786436
  14.5 9.3 %copy-start.8 = (s32[16,128,256]{2,1,0:T(8,128)S(1)}, s32[16,128,256]{2,1,0:T(8,128)}, u32[]{:S(2)}) copy-start(s32[16,128,256]{2,1,0:T(8,128)} %param.12) | copy-start | bytes 6291460
  28.7 33.9 %all-to-all-start = ((f32[128,2,16,128]{3,2,1,0:T(8,128)}), f32[128,2,16,128]{3,2,1,0:T(8,128)}, u32[]{:S(2)}, u32[]{:S(2)}) async-start(f32[128,2,16,128]{3,2,1,0:T(8,128)} %copy.20), calls=%async_computation | async-start | bytes 4194304 | tf_op jit(solution)/shard_map/all_to_all | solution.py:168
  68.9 1.0 copy-start.6
  71.8 2.4 %copy-start.2 = (f32[1024,64,16,1,1]{0,1,2,4,3:T(8,128)S(1)}, f32[1024,64,16,1,1]{0,1,2,4,3:T(8,128)}, u32[]{:S(2)}) copy-start(f32[1024,64,16,1,1]{0,1,2,4,3:T(8,128)} %constant.80) | copy-start | bytes 12582916
  121.8 8.8 %collective-permute-start.5 = (f32[16,1,256]{2,1,0:T(1,128)S(1)}, f32[16,1,256]{2,1,0:T(1,128)S(1)}, u32[]{:S(2)}, u32[]{:S(2)}) collective-permute-start(f32[16,1,256]{2,1,0:T(1,128)S(1)} %broadcast_select_fusion.2), channel_id=1, source_target_pairs={{0,1},{1,0},{2,3},{3,2},{4,5},{5,4},{6,7},{7,6},{8,9},{9,8},{10,11... | collective-permute-start | bytes 49160 | tf_op jit(solution)/shard_map/ppermute | solution.py:37
  122.2 8.4 %collective-permute-start.3 = (f32[1,128,256]{2,1,0:T(8,128)S(1)}, f32[1,128,256]{2,1,0:T(8,128)S(1)}, u32[]{:S(2)}, u32[]{:S(2)}) collective-permute-start(f32[1,128,256]{2,1,0:T(8,128)S(1)} %get-tuple-element.11), channel_id=1, source_target_pairs={{2,0},{4,2},{6,4},{8,6},{10,8},{12,10},{14,12},{16,14},{18,16},{20... | collective-permute-start | bytes 393224 | tf_op jit(solution)/shard_map/ppermute | solution.py:29
  126.3 12.0 %collective-permute-start.4 = (f32[1,128,256]{2,1,0:T(8,128)S(1)}, f32[1,128,256]{2,1,0:T(8,128)S(1)}, u32[]{:S(2)}, u32[]{:S(2)}) collective-permute-start(f32[1,128,256]{2,1,0:T(8,128)S(1)} %get-tuple-element.12), channel_id=1, source_target_pairs={{0,2},{2,4},{4,6},{6,8},{8,10},{10,12},{12,14},{14,16},{16,18},{18... | collective-permute-start | bytes 393224 | tf_op jit(solution)/shard_map/ppermute | solution.py:26
  128.2 10.1 %copy-start.1 = (f32[16,128,256]{2,1,0:T(8,128)S(1)}, f32[16,128,256]{2,1,0:T(8,128)}, u32[]{:S(2)}) copy-start(f32[16,128,256]{2,1,0:T(8,128)} %param.9) | copy-start | bytes 6291460
  128.2 10.1 %copy-start.4 = (f32[16,128,256]{2,1,0:T(8,128)S(1)}, f32[16,128,256]{2,1,0:T(8,128)}, u32[]{:S(2)}) copy-start(f32[16,128,256]{2,1,0:T(8,128)} %param.8) | copy-start | bytes 6291460

commit v3 on v2

--- a/solution.py
+++ b/solution.py
@@ -150,8 +150,13 @@
     axial_pad = extended(axial_vel, (("gz", 0),), 1)
     flux = radial_vel * radius
     if row_count == 2:
-        no_flux = jnp.zeros_like(flux[:, :1])
-        radial_flux = radial_neighbour(flux, no_flux, no_flux)
+        edge_radius = jnp.where(row_index == 0, radius[:, -1:], radius[:, :1])
+        edge_vel = jnp.where(row_index == 0, radial_vel[:, -1:], radial_vel[:, :1])
+        received = lax.ppermute(edge_vel * edge_radius, "row", [(0, 1), (1, 0)])
+        no_flux = jnp.zeros_like(received)
+        low = jnp.where(row_index == 0, no_flux, received)
+        high = jnp.where(row_index == 0, received, no_flux)
+        radial_flux = jnp.concatenate([low, flux, high], axis=1)
     else:
         radial_flux = extended(flux, (("row", 1),), 1)
     divergence = 0.5 * (axial_pad[2:] - axial_pad[:-2])

time: 141 us -> 144 us (1.021)
  local copies, waits for them, and re-layouts: 7.41 us -> 12.6 us
  waiting for transfers between devices: 45 us -> 41 us
    ppermute x2, waiting for transfers between devices: 16.2 us -> 12.2 us  [extended(): lax.ppermute(lax.slice_in_dim(block, block.shape[dim] - width, None, axis...]
    slice x2, local copies, waits for them, and re-layouts: 1.09 us -> 3.46 us  [body(): jnp.roll(swirl_vel, 1, 2)]
    mul x1, other arithmetic: 2.01 us -> 0.27 us  [body(): flux = radial_vel * radius]
  transfers between devices with their start and end apart: 7 -> 7, of which waited for: 3 -> 3; matrix products, arithmetic and copies ran while one was open for 3% -> 5% of each run, Pallas kernels for 0% -> 0%
where the time goes in v3:
time: 144 us
  waiting for transfers between devices  41 us (28%)
  blocking collectives  34.4 us (24%)
  matrix products  23.6 us (16%)
  starting transfers between devices  23.2 us (16%)
  local copies, waits for them, and re-layouts  12.6 us (9%)
  other arithmetic  6.74 us (5%)
  between operations  2.25 us (2%)
    all_to_all x1, blocking collectives, body(): lax.all_to_all(physical_space, both, split_axis=0, concat_axis=0, tiled=T...  34.4 us
    all_to_all x1, waiting for transfers between devices, body(): lax.all_to_all(spectrum_in, both, split_axis=0, concat_axis=0, tiled=True)  28.8 us
    ppermute x2, starting transfers between devices, extended(): lax.ppermute(lax.slice_in_dim(block, 0, width, axis=dim), axis, backward)  12.2 us
    ppermute x2, waiting for transfers between devices, extended(): lax.ppermute(lax.slice_in_dim(block, block.shape[dim] - width, None, axis...  12.2 us
    dot_general x1, matrix products, body(): jnp.einsum('kgx,mkrj->grmxj', axial_table, radial_returned, precision=max...  6.8 us
    dot_general x1, matrix products, body(): jnp.einsum('kgx,grmxj->mkrj', axial_table, resident, precision=forward_pr...  6.34 us
    all_to_all x1, starting transfers between devices, body(): lax.all_to_all(spectrum_in, both, split_axis=0, concat_axis=0, tiled=True)  5.79 us
    ppermute x2, starting transfers between devices, extended(): lax.ppermute(lax.slice_in_dim(block, block.shape[dim] - width, None, axis...  3.84 us
  transfers between devices with their start and end apart: 7, of which 3 were waited for; matrix products, arithmetic and copies ran while one was open for 5% of the time, Pallas kernels for 0%

profile of v3, /device:TPU:6, one launch (start us, length us, event | category | flops | bytes accessed | tf_op | source)
XLA Modules:
  0.0 143.6 jit_solution(15917242394870229917)
XLA Ops:
  0.7 0.5 fusion.54
  2.5 1.0 fusion.36
  3.5 0.9 collective-permute-start.2
  4.4 1.0 fusion.53
  5.4 8.1 %collective-permute-start = (f32[1,128,256]{2,1,0:T(8,128)S(1)}, f32[1,128,256]{2,1,0:T(8,128)S(1)}, u32[]{:S(2)}, u32[]{:S(2)}) collective-permute-start(f32[1,128,256]{2,1,0:T(8,128)S(1)} %get-tuple-element.17), channel_id=1, source_target_pairs={{2,0},{4,2},{6,4},{8,6},{10,8},{12,10},{14,12},{16,14},{18,16},{20... | collective-permute-start | bytes 393224 | tf_op jit(solution)/shard_map/ppermute | solution.py:29
  13.5 1.9 %collective-permute-start.1 = (f32[1,128,256]{2,1,0:T(8,128)S(1)}, f32[1,128,256]{2,1,0:T(8,128)S(1)}, u32[]{:S(2)}, u32[]{:S(2)}) collective-permute-start(f32[1,128,256]{2,1,0:T(8,128)S(1)} %get-tuple-element.18), channel_id=1, source_target_pairs={{0,2},{2,4},{4,6},{6,8},{8,10},{10,12},{12,14},{14,16},{16,18},{18... | collective-permute-start | bytes 393224 | tf_op jit(solution)/shard_map/ppermute | solution.py:26
  15.4 0.0 copy-start
  15.4 3.1 %fusion.52 = (f32[16,128,255]{2,1,0:T(8,128)S(1)}, f32[16,128,255]{2,1,0:T(8,128)S(1)}) fusion(f32[16,128,256]{2,1,0:T(8,128)} %param.10), kind=kLoop, calls=%fused_computation.81 | loop fusion | bytes 8355840 | tf_op jit(solution)/shard_map/jit(_roll_static)/slice | solution.py:164
  18.5 0.0 copy-done
  18.6 0.0 copy-start.1
  18.6 0.0 copy-start.9
  18.6 0.4 fusion.51
  19.0 1.2 copy-done.1
  20.2 0.3 broadcast_multiply_fusion
  20.4 0.4 copy-done.8
  20.8 0.1 select_reduce_fusion
  20.9 0.0 collective-permute-done.2
  20.9 0.0 collective-permute-done
  21.0 4.5 %collective-permute-done.1 = f32[1,128,256]{2,1,0:T(8,128)S(1)} collective-permute-done((f32[1,128,256]{2,1,0:T(8,128)S(1)}, f32[1,128,256]{2,1,0:T(8,128)S(1)}, u32[]{:S(2)}, u32[]{:S(2)}) %collective-permute-start.1) | collective-permute-done | bytes 131104 | tf_op jit(solution)/shard_map/ppermute | solution.py:26
  25.5 2.4 %fusion.22 = f32[256,16,128]{2,0,1:T(8,128)S(1)} fusion(f32[256,256,1]{0,1,2:T(8,128)S(1)} %copy-done.6, f32[16,128,256]{2,1,0:T(8,128)S(1)} %broadcast_multiply_fusion, f32[16,1,256]{2,1,0:T(1,128)S(1)} %get-tuple-element.22, f32[16,1,256]{2,1,0:T(1,128)S(1)} %get-tuple-element.21, f32[16,128,256]{2,1,0:T(8,128)S(1)} %copy-done.4, ...), kind=kOutput, calls=%fused_computation.32 | convolution fusion | flops 814219264 | bytes 13142016 | tf_op jit(solution)/shard_map/xrt,tm->mxr/dot_general | solution.py:170
  27.9 2.5 %copy.20 = f32[128,2,16,128]{3,2,1,0:T(8,128)} copy(f32[128,2,16,128]{3,1,0,2:T(2,128)S(1)} %bitcast.39) | data formatting | bytes 4194304 | tf_op jit(solution)/shard_map/reshape | solution.py:172
  30.4 5.8 %all-to-all-start = ((f32[128,2,16,128]{3,2,1,0:T(8,128)}), f32[128,2,16,128]{3,2,1,0:T(8,128)}, u32[]{:S(2)}, u32[]{:S(2)}) async-start(f32[128,2,16,128]{3,2,1,0:T(8,128)} %copy.20), calls=%async_computation | async-start | bytes 4194304 | tf_op jit(solution)/shard_map/all_to_all | solution.py:173
  36.4 0.1 broadcast_add_fusion
  36.5 28.8 %all-to-all-done = f32[128,2,16,128]{3,2,1,0:T(8,128)} async-done(((f32[128,2,16,128]{3,2,1,0:T(8,128)}), f32[128,2,16,128]{3,2,1,0:T(8,128)}, u32[]{:S(2)}, u32[]{:S(2)}) %all-to-all-start) | async-done | bytes 2097184 | tf_op jit(solution)/shard_map/all_to_all | solution.py:173
  65.2 6.3 %fusion.55 = f32[2,2,128,1024,1]{3,2,1,0,4:T(8,128)S(1)} fusion(f32[64,2,2,16,128]{4,3,2,1,0:T(8,128)} %bitcast.4, f32[1024,64,16,1,1]{0,2,4,3,1:T(8,128)} %constant.77), kind=kOutput, calls=%fused_computation.84 | convolution fusion | flops 3221225472 | bytes 8388608 | tf_op jit(solution)/shard_map/kgx,grmxj->mkrj/dot_general | solution.py:178
  71.6 0.0 copy-start.7
  71.6 0.1 copy.31
  71.7 0.8 copy-done.7
  72.5 1.8 %fusion.56 = f32[2,1024,256]{2,1,0:T(8,128)S(1)} fusion(f32[2,1024,256]{1,2,0:T(8,128)S(1)} %bitcast.36, f32[256,256,1]{1,0,2:T(8,128)S(1)} %copy-done.7), kind=kOutput, calls=%fused_computation.85 | convolution fusion | flops 805306368 | bytes 4456448 | tf_op jit(solution)/shard_map/sj,mkj->mks/dot_general | solution.py:181
  74.4 0.0 copy-start.3
  74.4 2.4 %fusion.18 = f32[2,1024,256]{1,2,0:T(8,128)S(1)} fusion(f32[256,256,1]{1,0,2:T(8,128)S(1)} %copy-done.7, f32[2,1024,256]{2,1,0:T(8,128)S(1)} %fusion.56, f32[256]{0:T(256)S(1)} %multiply_subtract_fusion.1, f32[2,1024]{1,0:T(2,128)S(1)} %broadcast_add_fusion), kind=kOutput, calls=%fused_computation.28 | convolution fusion | flops 1612185600 | bytes 4465664 | tf_op jit(solution)/shard_map/sj,mks->mkj/dot_general | solution.py:183
  76.8 6.8 %convolution_bitcast_fusion = f32[64,2,2,16,128]{4,0,3,1,2:T(8,128)S(1)} fusion(f32[2,1024,2,128,1]{1,3,4,2,0:T(8,128)S(1)} %bitcast.38, f32[1024,64,16,1,1]{0,1,2,4,3:T(8,128)S(1)} %copy-done.3), kind=kOutput, calls=%fused_computation.33 | convolution fusion | flops 6442450944 | bytes 8388608 | tf_op jit(solution)/shard_map/kgx,mkrj->grmxj/dot_general | solution.py:185
  83.6 1.4 %copy.26 = f32[64,2,2,16,128]{4,3,2,1,0:T(8,128)S(1)} copy(f32[64,2,2,16,128]{4,0,3,1,2:T(8,128)S(1)} %convolution_bitcast_fusion) | data formatting | bytes 4194304 | tf_op jit(solution)/shard_map/kgx,mkrj->grmxj/transpose | solution.py:185
  85.0 34.4 %all_to_all.10 = f32[128,2,16,128]{3,2,1,0:T(8,128)S(1)} all-to-all(f32[128,2,16,128]{3,2,1,0:T(8,128)S(1)} %bitcast.37), channel_id=1, replica_groups=mesh['gz'=64,'row'=2] {'gz','row'}, dimensions={0} | all-to-all | bytes 4194304 | tf_op jit(solution)/shard_map/all_to_all | solution.py:188
  119.4 3.8 %fusion.24 = f32[16,128,256]{2,1,0:T(8,128)S(1)} fusion(f32[256,256,1]{0,1,2:T(8,128)S(1)} %copy-done.6, f32[256,16,128]{2,1,0:T(8,128)S(1)} %bitcast.35), kind=kOutput, calls=%fused_computation.34 | convolution fusion | flops 1611137024 | bytes 4456448 | tf_op jit(solution)/shard_map/qxr,tq->xrt/dot_general | solution.py:190
  123.2 0.7 fusion.49
  124.0 0.4 fusion.48
  124.4 0.4 collective-permute-start.5
  124.8 4.1 %collective-permute-start.3 = (f32[1,128,256]{2,1,0:T(8,128)S(1)}, f32[1,128,256]{2,1,0:T(8,128)S(1)}, u32[]{:S(2)}, u32[]{:S(2)}) collective-permute-start(f32[1,128,256]{2,1,0:T(8,128)S(1)} %get-tuple-element.11), channel_id=1, source_target_pairs={{2,0},{4,2},{6,4},{8,6},{10,8},{12,10},{14,12},{16,14},{18,16},{20... | collective-permute-start | bytes 393224 | tf_op jit(solution)/shard_map/ppermute | solution.py:29
  128.9 1.9 %collective-permute-start.4 = (f32[1,128,256]{2,1,0:T(8,128)S(1)}, f32[1,128,256]{2,1,0:T(8,128)S(1)}, u32[]{:S(2)}, u32[]{:S(2)}) collective-permute-start(f32[1,128,256]{2,1,0:T(8,128)S(1)} %get-tuple-element.12), channel_id=1, source_target_pairs={{0,2},{2,4},{4,6},{6,8},{8,10},{10,12},{12,14},{14,16},{16,18},{18... | collective-permute-start | bytes 393224 | tf_op jit(solution)/shard_map/ppermute | solution.py:26
  130.8 0.0 copy-start.2
  130.9 0.0 copy-start.5
  130.9 2.3 %fusion.15 = f32[16,128,256]{2,1,0:T(8,128)} fusion(f32[16,128,256]{2,1,0:T(8,128)S(1)} %copy-done, f32[16,128,1]{2,1,0:T(8,128)S(1)} %get-tuple-element.6, f32[16,128,255]{2,1,0:T(8,128)S(1)} %get-tuple-element.8, f32[16,128,255]{2,1,0:T(8,128)S(1)} %get-tuple-element.7, f32[16,128,1]{2,1,0:T(8,128)S(1)} %get-tuple-element.5, f32[128]{0:T(128)S(1)} %get-tuple-element.24), kind=kLoop, calls=%fused_computation.25 | loop fusion | flops 2621440 | bytes 8389120 | tf_op jit(solution)/shard_map/sub | solution.py:204
  133.2 0.0 collective-permute-done.5
  133.2 0.0 collective-permute-done.3
  133.3 7.7 %collective-permute-done.4 = f32[1,128,256]{2,1,0:T(8,128)S(1)} collective-permute-done((f32[1,128,256]{2,1,0:T(8,128)S(1)}, f32[1,128,256]{2,1,0:T(8,128)S(1)}, u32[]{:S(2)}, u32[]{:S(2)}) %collective-permute-start.4) | collective-permute-done | bytes 131104 | tf_op jit(solution)/shard_map/ppermute | solution.py:26
  140.9 0.0 copy-done.2
  140.9 2.7 %fusion.2 = (f32[16,128,256]{2,1,0:T(8,128)}, f32[16,128,256]{2,1,0:T(8,128)}) fusion(f32[16,128,256]{2,1,0:T(8,128)S(1)} %copy-done.2, f32[16,128,256]{2,1,0:T(8,128)S(1)} %fusion.24, f32[16,1,256]{2,1,0:T(1,128)S(1)} %get-tuple-element.4, f32[16,1,256]{2,1,0:T(1,128)S(1)} %get-tuple-element.3, f32[16,128,256]{2,1,0:T(8,128)S(1)} %copy-done.5, ...), kind=kLoop, calls=%fused_computation.3 | loop fusion | flops 5242880 | bytes 10780672 | tf_op jit(solution)/shard_map/sub | solution.py:203
  (19 shorter events, 0.3 us)
Async XLA Ops:
  3.5 17.4 %collective-permute-start.2 = (f32[16,1,256]{2,1,0:T(1,128)S(1)}, f32[16,1,256]{2,1,0:T(1,128)S(1)}, u32[]{:S(2)}, u32[]{:S(2)}) collective-permute-start(f32[16,1,256]{2,1,0:T(1,128)S(1)} %fusion.36), channel_id=1, source_target_pairs={{0,1},{1,0},{2,3},{3,2},{4,5},{5,4},{6,7},{7,6},{8,9},{9,8},{10,11... | collective-permute-start | bytes 49160 | tf_op jit(solution)/shard_map/ppermute | solution.py:155
  5.4 15.6 %collective-permute-start = (f32[1,128,256]{2,1,0:T(8,128)S(1)}, f32[1,128,256]{2,1,0:T(8,128)S(1)}, u32[]{:S(2)}, u32[]{:S(2)}) collective-permute-start(f32[1,128,256]{2,1,0:T(8,128)S(1)} %get-tuple-element.17), channel_id=1, source_target_pairs={{2,0},{4,2},{6,4},{8,6},{10,8},{12,10},{14,12},{16,14},{18,16},{20... | collective-permute-start | bytes 393224 | tf_op jit(solution)/shard_map/ppermute | solution.py:29
  13.5 12.0 %collective-permute-start.1 = (f32[1,128,256]{2,1,0:T(8,128)S(1)}, f32[1,128,256]{2,1,0:T(8,128)S(1)}, u32[]{:S(2)}, u32[]{:S(2)}) collective-permute-start(f32[1,128,256]{2,1,0:T(8,128)S(1)} %get-tuple-element.18), channel_id=1, source_target_pairs={{0,2},{2,4},{4,6},{6,8},{8,10},{10,12},{12,14},{14,16},{16,18},{18... | collective-permute-start | bytes 393224 | tf_op jit(solution)/shard_map/ppermute | solution.py:26
  15.4 3.1 %copy-start = (f32[16,128,256]{2,1,0:T(8,128)S(1)}, f32[16,128,256]{2,1,0:T(8,128)}, u32[]{:S(2)}) copy-start(f32[16,128,256]{2,1,0:T(8,128)} %param.10) | copy-start | bytes 6291460
  18.6 1.6 %copy-start.1 = (f32[16,128,256]{2,1,0:T(8,128)S(1)}, f32[16,128,256]{2,1,0:T(8,128)}, u32[]{:S(2)}) copy-start(f32[16,128,256]{2,1,0:T(8,128)} %param.9) | copy-start | bytes 6291460
  18.6 6.9 %copy-start.9 = (s32[16,128,256]{2,1,0:T(8,128)S(1)}, s32[16,128,256]{2,1,0:T(8,128)}, u32[]{:S(2)}) copy-start(s32[16,128,256]{2,1,0:T(8,128)} %param.12) | copy-start | bytes 6291460
  20.2 0.7 copy-start.8
  20.2 5.3 %copy-start.4 = (f32[16,128,256]{2,1,0:T(8,128)S(1)}, f32[16,128,256]{2,1,0:T(8,128)}, u32[]{:S(2)}) copy-start(f32[16,128,256]{2,1,0:T(8,128)} %param.8) | copy-start | bytes 6291460
  20.2 5.3 %copy-start.6 = (f32[256,256,1]{0,1,2:T(8,128)S(1)}, f32[256,256,1]{0,1,2:T(8,128)}, u32[]{:S(2)}) copy-start(f32[256,256,1]{0,1,2:T(8,128)} %constant.76) | copy-start | bytes 786436
  30.4 34.8 %all-to-all-start = ((f32[128,2,16,128]{3,2,1,0:T(8,128)}), f32[128,2,16,128]{3,2,1,0:T(8,128)}, u32[]{:S(2)}, u32[]{:S(2)}) async-start(f32[128,2,16,128]{3,2,1,0:T(8,128)} %copy.20), calls=%async_computation | async-start | bytes 4194304 | tf_op jit(solution)/shard_map/all_to_all | solution.py:173
  71.6 1.0 copy-start.7
  74.4 2.4 %copy-start.3 = (f32[1024,64,16,1,1]{0,1,2,4,3:T(8,128)S(1)}, f32[1024,64,16,1,1]{0,1,2,4,3:T(8,128)}, u32[]{:S(2)}) copy-start(f32[1024,64,16,1,1]{0,1,2,4,3:T(8,128)} %constant.80) | copy-start | bytes 12582916
  124.4 8.8 %collective-permute-start.5 = (f32[16,1,256]{2,1,0:T(1,128)S(1)}, f32[16,1,256]{2,1,0:T(1,128)S(1)}, u32[]{:S(2)}, u32[]{:S(2)}) collective-permute-start(f32[16,1,256]{2,1,0:T(1,128)S(1)} %broadcast_select_fusion.2), channel_id=1, source_target_pairs={{0,1},{1,0},{2,3},{3,2},{4,5},{5,4},{6,7},{7,6},{8,9},{9,8},{10,11... | collective-permute-start | bytes 49160 | tf_op jit(solution)/shard_map/ppermute | solution.py:37
  124.8 8.4 %collective-permute-start.3 = (f32[1,128,256]{2,1,0:T(8,128)S(1)}, f32[1,128,256]{2,1,0:T(8,128)S(1)}, u32[]{:S(2)}, u32[]{:S(2)}) collective-permute-start(f32[1,128,256]{2,1,0:T(8,128)S(1)} %get-tuple-element.11), channel_id=1, source_target_pairs={{2,0},{4,2},{6,4},{8,6},{10,8},{12,10},{14,12},{16,14},{18,16},{20... | collective-permute-start | bytes 393224 | tf_op jit(solution)/shard_map/ppermute | solution.py:29
  128.9 12.0 %collective-permute-start.4 = (f32[1,128,256]{2,1,0:T(8,128)S(1)}, f32[1,128,256]{2,1,0:T(8,128)S(1)}, u32[]{:S(2)}, u32[]{:S(2)}) collective-permute-start(f32[1,128,256]{2,1,0:T(8,128)S(1)} %get-tuple-element.12), channel_id=1, source_target_pairs={{0,2},{2,4},{4,6},{6,8},{8,10},{10,12},{12,14},{14,16},{16,18},{18... | collective-permute-start | bytes 393224 | tf_op jit(solution)/shard_map/ppermute | solution.py:26
  130.8 10.1 %copy-start.2 = (f32[16,128,256]{2,1,0:T(8,128)S(1)}, f32[16,128,256]{2,1,0:T(8,128)}, u32[]{:S(2)}) copy-start(f32[16,128,256]{2,1,0:T(8,128)} %param.9) | copy-start | bytes 6291460
  130.9 10.1 %copy-start.5 = (f32[16,128,256]{2,1,0:T(8,128)S(1)}, f32[16,128,256]{2,1,0:T(8,128)}, u32[]{:S(2)}) copy-start(f32[16,128,256]{2,1,0:T(8,128)} %param.8) | copy-start | bytes 6291460

commit v4 on v2

--- a/solution.py
+++ b/solution.py
@@ -147,7 +147,7 @@
     own_first = row_index * radial_block
     own_cells = own_first + jnp.arange(radial_block, dtype=jnp.int32)
     radius = cell_radius(own_cells)[None, :, None]
-    axial_pad = extended(axial_vel, (("gz", 0),), 1)
+    axial_pad = jnp.pad(axial_vel, ((1, 1), (0, 0), (0, 0)))
     flux = radial_vel * radius
     if row_count == 2:
         no_flux = jnp.zeros_like(flux[:, :1])
@@ -162,11 +162,19 @@
     right_side = divergence - canopy_source(canopy_gore, inflow_rate)
     all_modes = jnp.arange(NT, dtype=jnp.int32)
     fourier = jnp.asarray(AZIMUTH_TABLE)
-    spectrum_in = jnp.einsum("xrt,tm->mxr", right_side, fourier, precision=forward_precision)
+    planes = jnp.concatenate([right_side, axial_vel[:1], axial_vel[-1:]], axis=0)
+    spectrum_in = jnp.einsum("xrt,tm->mxr", planes, fourier, precision=forward_precision)
     modes_each = NT // device_count
-    spectrum_in = spectrum_in.reshape(device_count, modes_each, axial_block, radial_block)
+    spectrum_in = spectrum_in.reshape(device_count, modes_each, axial_block + 2, radial_block)
     resident = lax.all_to_all(spectrum_in, both, split_axis=0, concat_axis=0, tiled=True)
-    resident = resident.reshape(gz_count, row_count, modes_each, axial_block, radial_block)
+    resident = resident.reshape(gz_count, row_count, modes_each, axial_block + 2, radial_block)
+    first_hat = resident[:, :, :, axial_block]
+    last_hat = resident[:, :, :, axial_block + 1]
+    next_first = jnp.concatenate([first_hat[1:], jnp.zeros_like(first_hat[:1])], axis=0)
+    prev_last = jnp.concatenate([jnp.zeros_like(last_hat[:1]), last_hat[:-1]], axis=0)
+    resident = resident[:, :, :, :axial_block]
+    resident = resident.at[:, :, :, axial_block - 1].add(0.5 * next_first)
+    resident = resident.at[:, :, :, 0].add(-0.5 * prev_last)
     mode_ids = lax.axis_index(both) * modes_each + jnp.arange(modes_each, dtype=jnp.int32)
     axial_table = jnp.asarray(AXIAL_TABLE).reshape(NX, gz_count, axial_block)
     radial_table = jnp.asarray(RADIAL_TABLE)
@@ -179,11 +187,20 @@
     radial_returned = radial_returned.reshape(modes_each, NX, row_count, radial_block)
     physical_space = jnp.einsum(
         "kgx,mkrj->grmxj", axial_table, radial_returned, precision=maximal_precision
-    ).reshape(device_count, modes_each, axial_block, radial_block)
-    returned = lax.all_to_all(physical_space, both, split_axis=0, concat_axis=0, tiled=True)
-    returned = returned.reshape(NT, axial_block, radial_block)
-    pressure = -jnp.einsum("qxr,tq->xrt", returned, fourier, precision=maximal_precision)
-    padded = extended(pressure, (("gz", 0),), 1)
+    )
+    first_p = physical_space[:, :, :, :1]
+    last_p = physical_space[:, :, :, -1:]
+    ghost_low = jnp.concatenate([jnp.zeros_like(last_p[:1]), last_p[:-1]], axis=0)
+    ghost_high = jnp.concatenate([first_p[1:], jnp.zeros_like(first_p[:1])], axis=0)
+    windows = jnp.concatenate([physical_space, ghost_low, ghost_high], axis=3)
+    windows = windows.reshape(device_count, modes_each, axial_block + 2, radial_block)
+    returned = lax.all_to_all(windows, both, split_axis=0, concat_axis=0, tiled=True)
+    returned = returned.reshape(NT, axial_block + 2, radial_block)
+    extended_p = -jnp.einsum("qxr,tq->xrt", returned, fourier, precision=maximal_precision)
+    pressure = extended_p[:axial_block]
+    padded = jnp.concatenate(
+        [extended_p[axial_block : axial_block + 1], pressure, extended_p[axial_block + 1 :]], axis=0
+    )
     if row_count == 2:
         sideways = radial_neighbour(pressure, pressure[:, :1], pressure[:, -1:])
         above = sideways[:, 2:]

time: 141 us -> 134 us (0.950); the launches traced: 141 us -> 131 us
  waiting for transfers between devices: 45 us -> 32.8 us
  local copies, waits for them, and re-layouts: 7.41 us -> 17.1 us
  starting transfers between devices: 22.3 us -> 12.8 us
  matrix products: 23.6 us -> 20 us
  other arithmetic: 7.49 us -> 10.6 us
  blocking collectives: 34.4 us -> 37.2 us
    ppermute x4 -> x0, waiting for transfers between devices: 16.2 us -> none  [the longest x2 16.2 us: extended(): lax.ppermute(lax.slice_in_dim(block, block.shape[dim] - width, None, axis...]
    ppermute x4 -> x0, starting transfers between devices: 16.1 us -> none  [the longest x2 12.2 us: extended(): lax.ppermute(lax.slice_in_dim(block, 0, width, axis=dim), axis, backward)]
    all_to_all x1, starting transfers between devices: 4.88 us -> 11.4 us  [body(): lax.all_to_all(spectrum_in, both, split_axis=0, concat_axis=0, tiled=True)]
    unnamed x18 -> x19, local copies, waits for them, and re-layouts: 1.09 us -> 5.02 us
    all_to_all x0 -> x2, local copies, waits for them, and re-layouts: none -> 3.22 us  [the longest x1 1.95 us: body(): lax.all_to_all(spectrum_in, both, split_axis=0, concat_axis=0, tiled=True)]
    all_to_all x1, blocking collectives: 34.4 us -> 37.2 us  [body(): lax.all_to_all(windows, both, split_axis=0, concat_axis=0, tiled=True)]
    dot_general x1, matrix products: 6.33 us -> 3.55 us  [body(): jnp.einsum('kgx,grmxj->mkrj', axial_table, resident, precision=forward_pr...]
    all_to_all x1, waiting for transfers between devices: 28.8 us -> 31.4 us  [body(): lax.all_to_all(spectrum_in, both, split_axis=0, concat_axis=0, tiled=True)]
  transfers between devices with their start and end apart: 7 -> 3, of which waited for: 3 -> 3; matrix products, arithmetic and copies ran while one was open for 3% -> 3% of each run, Pallas kernels for 0% -> 0%
where the time goes in v4:
time: 134 us; the launch traced here: 131 us
  blocking collectives  37.2 us (28%)
  waiting for transfers between devices  32.8 us (24%)
  matrix products  20 us (15%)
  local copies, waits for them, and re-layouts  17.1 us (13%)
  starting transfers between devices  12.8 us (10%)
  other arithmetic  10.6 us (8%)
    all_to_all x1, blocking collectives, body(): lax.all_to_all(windows, both, split_axis=0, concat_axis=0, tiled=True)  37.2 us
    all_to_all x1, waiting for transfers between devices, body(): lax.all_to_all(spectrum_in, both, split_axis=0, concat_axis=0, tiled=True)  31.4 us
    all_to_all x1, starting transfers between devices, body(): lax.all_to_all(spectrum_in, both, split_axis=0, concat_axis=0, tiled=True)  11.4 us
    dot_general x1, matrix products, body(): jnp.einsum('kgx,mkrj->grmxj', axial_table, radial_returned, precision=max...  6.99 us
    unnamed x19, local copies, waits for them, and re-layouts  5.02 us
    dot_general x1, matrix products, body(): jnp.einsum('qxr,tq->xrt', returned, fourier, precision=maximal_precision)  4 us
    dot_general x1, matrix products, body(): jnp.einsum('kgx,grmxj->mkrj', axial_table, resident, precision=forward_pr...  3.55 us
    sub x1, other arithmetic, body(): radial_projected_velocity = radial_vel - 0.5 * (above - below)  2.74 us
  transfers between devices with their start and end apart: 3, of which 3 were waited for; matrix products, arithmetic and copies ran while one was open for 3% of the time, Pallas kernels for 0%

profile of v4, /device:TPU:6, one launch (start us, length us, event | category | flops | bytes accessed | tf_op | source)
XLA Modules:
  0.0 131.3 jit_solution(371971685580350174)
XLA Ops:
  0.6 0.0 copy-start
  0.7 2.0 %broadcast_multiply_fusion = f32[16,128,256]{2,1,0:T(8,128)S(1)} fusion(f32[16,128,256]{2,1,0:T(8,128)} %param.13, f32[128]{0:T(128)S(1)} %convert_add_fusion), kind=kLoop, calls=%fused_computation.50 | loop fusion | flops 524288 | bytes 4194816 | tf_op jit(solution)/shard_map/mul | solution.py:151
  2.7 0.9 collective-permute-start
  3.6 0.7 fusion.51
  4.3 0.0 copy-start.2
  4.3 0.0 copy-start.8
  4.4 0.0 copy-start.5
  4.4 0.4 fusion.50
  4.7 1.2 copy-done.2
  6.0 0.1 select_reduce_fusion
  6.1 0.5 collective-permute-done
  6.5 0.0 copy-done.5
  6.6 2.6 %fusion.11 = f32[16,128,256]{2,1,0:T(8,128)S(1)} fusion(f32[16,128,256]{2,1,0:T(8,128)S(1)} %copy-done.2, f32[16,128,256]{2,1,0:T(8,128)S(1)} %broadcast_multiply_fusion, f32[16,1,256]{2,1,0:T(1,128)S(1)} %get-tuple-element.48, f32[16,1,256]{2,1,0:T(1,128)S(1)} %get-tuple-element.47, f32[16,128,1]{2,1,0:T(8,128)S(1)} %get-tuple-element.42, ...), kind=kLoop, calls=%fused_computation.18 | loop fusion | flops 7864320 | bytes 12617728 | tf_op jit(solution)/shard_map/sub | solution.py:162
  9.2 1.2 fusion
  10.5 2.3 %copy.56 = f32[128,2,18,128]{3,1,2,0:T(2,128)} copy(f32[128,2,18,128]{3,1,0,2:T(2,128)S(1)} %bitcast.52) | data formatting | bytes 4718592 | tf_op jit(solution)/shard_map/reshape | solution.py:168
  12.7 11.4 %all-to-all-start = ((f32[128,2,18,128]{3,1,2,0:T(2,128)}), f32[128,2,18,128]{3,1,2,0:T(2,128)}, u32[]{:S(2)}, u32[]{:S(2)}) async-start(f32[128,2,18,128]{3,1,2,0:T(2,128)} %copy.56), calls=%async_computation | async-start | bytes 4718592 | tf_op jit(solution)/shard_map/all_to_all | solution.py:169
  24.3 0.1 broadcast_add_fusion
  24.4 31.4 %all-to-all-done = f32[128,2,18,128]{3,1,2,0:T(2,128)} async-done(((f32[128,2,18,128]{3,1,2,0:T(2,128)}), f32[128,2,18,128]{3,1,2,0:T(2,128)}, u32[]{:S(2)}, u32[]{:S(2)}) %all-to-all-start) | async-done | bytes 2359328 | tf_op jit(solution)/shard_map/all_to_all | solution.py:169
  55.8 1.9 %copy.57 = f32[128,2,18,128]{3,0,2,1:T(8,128)S(1)} copy(f32[128,2,18,128]{3,1,2,0:T(2,128)} %all-to-all-done) | data formatting | bytes 4718592 | tf_op jit(solution)/shard_map/all_to_all | solution.py:169
  57.8 0.2 slice.223
  58.0 0.0 copy-start.1
  58.0 0.2 copy.82
  58.2 0.1 fusion.37
  58.4 0.2 fusion.35
  58.5 1.7 %copy-done.1 = f32[1024,64,16,1,1]{0,1,2,4,3:T(8,128)S(1)} copy-done((f32[1024,64,16,1,1]{0,1,2,4,3:T(8,128)S(1)}, f32[1024,64,16,1,1]{0,1,2,4,3:T(8,128)}, u32[]{:S(2)}) %copy-start.1) | copy-done | bytes 4194328
  60.2 3.5 %fusion.29 = f32[2,1024,2,128]{1,3,0,2:T(8,128)S(1)} fusion(f32[1024,64,16,1,1]{0,1,2,4,3:T(8,128)S(1)} %copy-done.1, f32[64,2,2,16,128]{4,1,0,2,3:T(2,128)S(1)} %fusion.35), kind=kOutput, calls=%fused_computation.45 | convolution fusion | flops 3221225472 | bytes 8388608 | tf_op jit(solution)/shard_map/kgx,grmxj->mkrj/dot_general | solution.py:181
  63.8 0.0 copy-start.7
  63.8 0.2 copy.62
  64.0 0.7 copy-done.7
  64.7 1.8 %fusion.53 = f32[2,1024,256]{2,1,0:T(8,128)S(1)} fusion(f32[2,1024,256]{1,2,0:T(8,128)S(1)} %bitcast.55, f32[256,256,1]{1,0,2:T(8,128)S(1)} %copy-done.7), kind=kOutput, calls=%fused_computation.92 | convolution fusion | flops 805306368 | bytes 4456448 | tf_op jit(solution)/shard_map/sj,mkj->mks/dot_general | solution.py:184
  66.6 2.4 %fusion.25 = f32[2,1024,256]{1,2,0:T(8,128)S(1)} fusion(f32[256,256,1]{1,0,2:T(8,128)S(1)} %copy-done.7, f32[2,1024,256]{2,1,0:T(8,128)S(1)} %fusion.53, f32[256]{0:T(256)S(1)} %multiply_subtract_fusion.1, f32[2,1024]{1,0:T(2,128)S(1)} %broadcast_add_fusion), kind=kOutput, calls=%fused_computation.40 | convolution fusion | flops 1612185600 | bytes 4465664 | tf_op jit(solution)/shard_map/sj,mks->mkj/dot_general | solution.py:186
  69.0 7.0 %convolution_bitcast_fusion = f32[64,2,2,16,128]{4,0,3,1,2:T(8,128)S(1)} fusion(f32[2,1024,2,128,1]{1,3,4,2,0:T(8,128)S(1)} %bitcast.56, f32[1024,64,16,1,1]{0,1,2,4,3:T(8,128)S(1)} %copy-done.1), kind=kOutput, calls=%fused_computation.46 | convolution fusion | flops 6442450944 | bytes 8388608 | tf_op jit(solution)/shard_map/kgx,mkrj->grmxj/dot_general | solution.py:188
  76.0 0.2 select_maximum_fusion
  76.2 1.9 %copy.66 = f32[64,2,2,18,128]{4,1,0,3,2:T(2,128)S(1)} copy(f32[64,2,2,18,128]{4,0,3,1,2:T(8,128)S(1)} %select_maximum_fusion) | data formatting | bytes 4718592 | tf_op jit(solution)/shard_map/concatenate | solution.py:195
  78.1 1.8 %copy.67 = f32[128,2,18,128]{3,1,2,0:T(2,128)S(1)} copy(f32[128,2,18,128]{3,0,2,1:T(8,128)S(1)} %bitcast.54) | data formatting | bytes 4718592 | tf_op jit(solution)/shard_map/reshape | solution.py:196
  80.0 37.2 %all_to_all.10 = f32[128,2,18,128]{3,1,2,0:T(2,128)S(1)} all-to-all(f32[128,2,18,128]{3,1,2,0:T(2,128)S(1)} %copy.67), channel_id=1, replica_groups=mesh['gz'=64,'row'=2] {'gz','row'}, dimensions={0} | all-to-all | bytes 4718592 | tf_op jit(solution)/shard_map/all_to_all | solution.py:197
  117.1 1.3 copy.68
  118.4 4.0 %convolution_negate_fusion = f32[18,128,256]{2,1,0:T(8,128)S(1)} fusion(f32[256,18,128]{2,0,1:T(8,128)S(1)} %bitcast.53, f32[256,256,1]{0,1,2:T(8,128)S(1)} %copy-done.6), kind=kOutput, calls=%fused_computation.44 | convolution fusion | flops 1812529152 | bytes 4980736 | tf_op jit(solution)/shard_map/qxr,tq->xrt/dot_general | solution.py:199
  122.4 0.7 fusion.47
  123.2 0.4 fusion.46
  123.6 0.4 collective-permute-start.1
  124.0 2.3 %fusion.22 = f32[16,128,256]{2,1,0:T(8,128)} fusion(f32[16,128,256]{2,1,0:T(8,128)S(1)} %copy-done, f32[16,128,1]{2,1,0:T(8,128)S(1)} %get-tuple-element.30, f32[16,128,255]{2,1,0:T(8,128)S(1)} %get-tuple-element.32, f32[16,128,255]{2,1,0:T(8,128)S(1)} %get-tuple-element.31, f32[16,128,1]{2,1,0:T(8,128)S(1)} %get-tuple-element.29, f32[128]{0:T(128)S(1)} %get-tuple-element.49), kind=kLoop, calls=%fused_computation.37 | loop fusion | flops 2621440 | bytes 8389120 | tf_op jit(solution)/shard_map/sub | solution.py:216
  126.4 0.0 copy-start.4
  126.4 0.1 slice.230
  126.5 0.9 collective-permute-done.1
  127.4 0.5 copy-done.3
  128.0 0.6 copy-done.4
  128.6 2.7 %fusion.14 = (f32[16,128,256]{2,1,0:T(8,128)}, f32[16,128,256]{2,1,0:T(8,128)}) fusion(f32[16,128,256]{2,1,0:T(8,128)S(1)} %copy-done.4, f32[16,128,256]{2,1,0:T(8,128)S(1)} %slice.230, f32[16,1,256]{2,1,0:T(1,128)S(1)} %get-tuple-element.28, f32[16,1,256]{2,1,0:T(1,128)S(1)} %get-tuple-element.27, f32[16,128,256]{2,1,0:T(8,128)S(1)} %copy-done.3, ...), kind=kLoop, calls=%fused_computation.22 | loop fusion | flops 5242880 | bytes 10780672 | tf_op jit(solution)/shard_map/sub | solution.py:215
  (19 shorter events, 0.4 us)
Async XLA Ops:
  0.6 3.0 %copy-start = (f32[16,128,256]{2,1,0:T(8,128)S(1)}, f32[16,128,256]{2,1,0:T(8,128)}, u32[]{:S(2)}) copy-start(f32[16,128,256]{2,1,0:T(8,128)} %param.14) | copy-start | bytes 6291460
  2.7 3.8 %collective-permute-start = (f32[16,1,256]{2,1,0:T(1,128)S(1)}, f32[16,1,256]{2,1,0:T(1,128)S(1)}, u32[]{:S(2)}, u32[]{:S(2)}) collective-permute-start(f32[16,1,256]{2,1,0:T(1,128)S(1)} %broadcast_select_fusion.5), channel_id=1, source_target_pairs={{0,1},{1,0},{2,3},{3,2},{4,5},{5,4},{6,7},{7,6},{8,9},{9,8},{10,11... | collective-permute-start | bytes 49160 | tf_op jit(solution)/shard_map/ppermute | solution.py:37
  4.3 1.6 %copy-start.2 = (f32[16,128,256]{2,1,0:T(8,128)S(1)}, f32[16,128,256]{2,1,0:T(8,128)}, u32[]{:S(2)}) copy-start(f32[16,128,256]{2,1,0:T(8,128)} %param.12) | copy-start | bytes 6291460
  4.3 1.6 %copy-start.8 = (f32[48]{0:T(128)S(1)}, f32[48]{0:T(128)}, u32[]{:S(2)}) copy-start(f32[48]{0:T(128)} %param.15) | copy-start | bytes 580
  4.4 2.2 %copy-start.5 = (s32[16,128,256]{2,1,0:T(8,128)S(1)}, s32[16,128,256]{2,1,0:T(8,128)}, u32[]{:S(2)}) copy-start(s32[16,128,256]{2,1,0:T(8,128)} %param.16) | copy-start | bytes 6291460
  6.6 2.6 %copy-start.6 = (f32[256,256,1]{0,1,2:T(8,128)S(1)}, f32[256,256,1]{0,1,2:T(8,128)}, u32[]{:S(2)}) copy-start(f32[256,256,1]{0,1,2:T(8,128)} %constant.146) | copy-start | bytes 786436
  12.7 43.1 %all-to-all-start = ((f32[128,2,18,128]{3,1,2,0:T(2,128)}), f32[128,2,18,128]{3,1,2,0:T(2,128)}, u32[]{:S(2)}, u32[]{:S(2)}) async-start(f32[128,2,18,128]{3,1,2,0:T(2,128)} %copy.56), calls=%async_computation | async-start | bytes 4718592 | tf_op jit(solution)/shard_map/all_to_all | solution.py:169
  58.0 2.2 %copy-start.1 = (f32[1024,64,16,1,1]{0,1,2,4,3:T(8,128)S(1)}, f32[1024,64,16,1,1]{0,1,2,4,3:T(8,128)}, u32[]{:S(2)}) copy-start(f32[1024,64,16,1,1]{0,1,2,4,3:T(8,128)} %constant.147) | copy-start | bytes 12582916
  63.8 1.0 copy-start.7
  123.6 3.8 %collective-permute-start.1 = (f32[16,1,256]{2,1,0:T(1,128)S(1)}, f32[16,1,256]{2,1,0:T(1,128)S(1)}, u32[]{:S(2)}, u32[]{:S(2)}) collective-permute-start(f32[16,1,256]{2,1,0:T(1,128)S(1)} %broadcast_select_fusion.2), channel_id=1, source_target_pairs={{0,1},{1,0},{2,3},{3,2},{4,5},{5,4},{6,7},{7,6},{8,9},{9,8},{10,11... | collective-permute-start | bytes 49160 | tf_op jit(solution)/shard_map/ppermute | solution.py:37
  126.4 1.6 %copy-start.3 = (f32[16,128,256]{2,1,0:T(8,128)S(1)}, f32[16,128,256]{2,1,0:T(8,128)}, u32[]{:S(2)}) copy-start(f32[16,128,256]{2,1,0:T(8,128)} %param.12) | copy-start | bytes 6291460
  126.4 2.2 %copy-start.4 = (f32[16,128,256]{2,1,0:T(8,128)S(1)}, f32[16,128,256]{2,1,0:T(8,128)}, u32[]{:S(2)}) copy-start(f32[16,128,256]{2,1,0:T(8,128)} %param.13) | copy-start | bytes 6291460

commit v5 on v4

--- a/solution.py
+++ b/solution.py
@@ -150,8 +150,13 @@
     axial_pad = jnp.pad(axial_vel, ((1, 1), (0, 0), (0, 0)))
     flux = radial_vel * radius
     if row_count == 2:
-        no_flux = jnp.zeros_like(flux[:, :1])
-        radial_flux = radial_neighbour(flux, no_flux, no_flux)
+        edge_radius = jnp.where(row_index == 0, radius[:, -1:], radius[:, :1])
+        edge_vel = jnp.where(row_index == 0, radial_vel[:, -1:], radial_vel[:, :1])
+        received = lax.ppermute(edge_vel * edge_radius, "row", [(0, 1), (1, 0)])
+        no_flux = jnp.zeros_like(received)
+        low = jnp.where(row_index == 0, no_flux, received)
+        high = jnp.where(row_index == 0, received, no_flux)
+        radial_flux = jnp.concatenate([low, flux, high], axis=1)
     else:
         radial_flux = extended(flux, (("row", 1),), 1)
     divergence = 0.5 * (axial_pad[2:] - axial_pad[:-2])

time: 134 us -> 138 us (1.030)
  local copies, waits for them, and re-layouts: 17.1 us -> 21.7 us
    slice x2, local copies, waits for them, and re-layouts: 1.07 us -> 3.43 us  [body(): jnp.roll(swirl_vel, 1, 2)]
    unnamed x19 -> x21, local copies, waits for them, and re-layouts: 5.02 us -> 6.77 us
    mul x1, other arithmetic: 2 us -> 0.28 us  [body(): flux = radial_vel * radius]
  transfers between devices with their start and end apart: 3 -> 3, of which waited for: 3 -> 2; matrix products, arithmetic and copies ran while one was open for 3% -> 5% of each run, Pallas kernels for 0% -> 0%
where the time goes in v5:
time: 138 us; the launch traced here: 136 us
  blocking collectives  37.2 us (27%)
  waiting for transfers between devices  32.3 us (23%)
  local copies, waits for them, and re-layouts  21.7 us (16%)
  matrix products  20 us (14%)
  starting transfers between devices  12.8 us (9%)
  other arithmetic  9.82 us (7%)
  between operations  2.26 us (2%)
    all_to_all x1, blocking collectives, body(): lax.all_to_all(windows, both, split_axis=0, concat_axis=0, tiled=True)  37.2 us
    all_to_all x1, waiting for transfers between devices, body(): lax.all_to_all(spectrum_in, both, split_axis=0, concat_axis=0, tiled=True)  31.4 us
    all_to_all x1, starting transfers between devices, body(): lax.all_to_all(spectrum_in, both, split_axis=0, concat_axis=0, tiled=True)  11.4 us
    dot_general x1, matrix products, body(): jnp.einsum('kgx,mkrj->grmxj', axial_table, radial_returned, precision=max...  7 us
    unnamed x21, local copies, waits for them, and re-layouts  6.77 us
    dot_general x1, matrix products, body(): jnp.einsum('qxr,tq->xrt', returned, fourier, precision=maximal_precision)  4 us
    dot_general x1, matrix products, body(): jnp.einsum('kgx,grmxj->mkrj', axial_table, resident, precision=forward_pr...  3.55 us
    slice x2, local copies, waits for them, and re-layouts, body(): jnp.roll(swirl_vel, 1, 2)  3.43 us
  transfers between devices with their start and end apart: 3, of which 2 were waited for; matrix products, arithmetic and copies ran while one was open for 5% of the time, Pallas kernels for 0%

profile of v5, /device:TPU:6, one launch (start us, length us, event | category | flops | bytes accessed | tf_op | source)
XLA Modules:
  0.0 136.1 jit_solution(13981155882489910987)
XLA Ops:
  0.7 0.5 fusion.54
  2.5 1.0 fusion.38
  3.5 0.9 collective-permute-start
  4.4 3.1 %fusion.52 = (f32[16,128,255]{2,1,0:T(8,128)S(1)}, f32[16,128,255]{2,1,0:T(8,128)S(1)}) fusion(f32[16,128,256]{2,1,0:T(8,128)} %param.14), kind=kLoop, calls=%fused_computation.92 | loop fusion | bytes 8355840 | tf_op jit(solution)/shard_map/jit(_roll_static)/slice | solution.py:164
  7.5 0.0 copy-start.4
  7.5 0.4 fusion.51
  7.9 1.2 copy-done.4
  9.1 0.3 broadcast_multiply_fusion
  9.4 1.3 copy-done.2
  10.7 0.1 select_reduce_fusion
  10.8 0.5 copy-done.6
  11.3 2.6 %fusion.11 = f32[16,128,256]{2,1,0:T(8,128)S(1)} fusion(f32[16,128,256]{2,1,0:T(8,128)S(1)} %copy-done.2, f32[16,128,256]{2,1,0:T(8,128)S(1)} %broadcast_multiply_fusion, f32[16,1,256]{2,1,0:T(1,128)S(1)} %get-tuple-element.50, f32[16,1,256]{2,1,0:T(1,128)S(1)} %get-tuple-element.49, f32[16,128,1]{2,1,0:T(8,128)S(1)} %get-tuple-element.42, ...), kind=kLoop, calls=%fused_computation.18 | loop fusion | flops 7864320 | bytes 12617728 | tf_op jit(solution)/shard_map/sub | solution.py:167
  13.9 1.2 fusion
  15.2 2.2 %copy.56 = f32[128,2,18,128]{3,1,2,0:T(2,128)} copy(f32[128,2,18,128]{3,1,0,2:T(2,128)S(1)} %bitcast.54) | data formatting | bytes 4718592 | tf_op jit(solution)/shard_map/reshape | solution.py:173
  17.4 11.4 %all-to-all-start = ((f32[128,2,18,128]{3,1,2,0:T(2,128)}), f32[128,2,18,128]{3,1,2,0:T(2,128)}, u32[]{:S(2)}, u32[]{:S(2)}) async-start(f32[128,2,18,128]{3,1,2,0:T(2,128)} %copy.56), calls=%async_computation | async-start | bytes 4718592 | tf_op jit(solution)/shard_map/all_to_all | solution.py:174
  29.0 0.1 broadcast_add_fusion
  29.1 31.4 %all-to-all-done = f32[128,2,18,128]{3,1,2,0:T(2,128)} async-done(((f32[128,2,18,128]{3,1,2,0:T(2,128)}), f32[128,2,18,128]{3,1,2,0:T(2,128)}, u32[]{:S(2)}, u32[]{:S(2)}) %all-to-all-start) | async-done | bytes 2359328 | tf_op jit(solution)/shard_map/all_to_all | solution.py:174
  60.5 1.9 %copy.57 = f32[128,2,18,128]{3,0,2,1:T(8,128)S(1)} copy(f32[128,2,18,128]{3,1,2,0:T(2,128)} %all-to-all-done) | data formatting | bytes 4718592 | tf_op jit(solution)/shard_map/all_to_all | solution.py:174
  62.5 0.2 slice.231
  62.7 0.0 copy-start.1
  62.8 0.2 copy.82
  63.0 0.1 fusion.37
  63.1 0.2 fusion.35
  63.2 1.7 %copy-done.1 = f32[1024,64,16,1,1]{0,1,2,4,3:T(8,128)S(1)} copy-done((f32[1024,64,16,1,1]{0,1,2,4,3:T(8,128)S(1)}, f32[1024,64,16,1,1]{0,1,2,4,3:T(8,128)}, u32[]{:S(2)}) %copy-start.1) | copy-done | bytes 4194328
  64.9 3.5 %fusion.29 = f32[2,1024,2,128]{1,3,0,2:T(8,128)S(1)} fusion(f32[1024,64,16,1,1]{0,1,2,4,3:T(8,128)S(1)} %copy-done.1, f32[64,2,2,16,128]{4,1,0,2,3:T(2,128)S(1)} %fusion.35), kind=kOutput, calls=%fused_computation.45 | convolution fusion | flops 3221225472 | bytes 8388608 | tf_op jit(solution)/shard_map/kgx,grmxj->mkrj/dot_general | solution.py:186
  68.5 0.0 copy-start.8
  68.5 0.2 copy.62
  68.7 0.7 copy-done.8
  69.4 1.8 %fusion.55 = f32[2,1024,256]{2,1,0:T(8,128)S(1)} fusion(f32[2,1024,256]{1,2,0:T(8,128)S(1)} %bitcast.57, f32[256,256,1]{1,0,2:T(8,128)S(1)} %copy-done.8), kind=kOutput, calls=%fused_computation.95 | convolution fusion | flops 805306368 | bytes 4456448 | tf_op jit(solution)/shard_map/sj,mkj->mks/dot_general | solution.py:189
  71.3 2.4 %fusion.25 = f32[2,1024,256]{1,2,0:T(8,128)S(1)} fusion(f32[256,256,1]{1,0,2:T(8,128)S(1)} %copy-done.8, f32[2,1024,256]{2,1,0:T(8,128)S(1)} %fusion.55, f32[256]{0:T(256)S(1)} %multiply_subtract_fusion.1, f32[2,1024]{1,0:T(2,128)S(1)} %broadcast_add_fusion), kind=kOutput, calls=%fused_computation.40 | convolution fusion | flops 1612185600 | bytes 4465664 | tf_op jit(solution)/shard_map/sj,mks->mkj/dot_general | solution.py:191
  73.7 7.0 %convolution_bitcast_fusion = f32[64,2,2,16,128]{4,0,3,1,2:T(8,128)S(1)} fusion(f32[2,1024,2,128,1]{1,3,4,2,0:T(8,128)S(1)} %bitcast.58, f32[1024,64,16,1,1]{0,1,2,4,3:T(8,128)S(1)} %copy-done.1), kind=kOutput, calls=%fused_computation.46 | convolution fusion | flops 6442450944 | bytes 8388608 | tf_op jit(solution)/shard_map/kgx,mkrj->grmxj/dot_general | solution.py:193
  80.7 0.2 select_maximum_fusion
  80.9 1.9 %copy.66 = f32[64,2,2,18,128]{4,1,0,3,2:T(2,128)S(1)} copy(f32[64,2,2,18,128]{4,0,3,1,2:T(8,128)S(1)} %select_maximum_fusion) | data formatting | bytes 4718592 | tf_op jit(solution)/shard_map/concatenate | solution.py:200
  82.9 1.8 %copy.67 = f32[128,2,18,128]{3,1,2,0:T(2,128)S(1)} copy(f32[128,2,18,128]{3,0,2,1:T(8,128)S(1)} %bitcast.56) | data formatting | bytes 4718592 | tf_op jit(solution)/shard_map/reshape | solution.py:201
  84.7 37.2 %all_to_all.10 = f32[128,2,18,128]{3,1,2,0:T(2,128)S(1)} all-to-all(f32[128,2,18,128]{3,1,2,0:T(2,128)S(1)} %copy.67), channel_id=1, replica_groups=mesh['gz'=64,'row'=2] {'gz','row'}, dimensions={0} | all-to-all | bytes 4718592 | tf_op jit(solution)/shard_map/all_to_all | solution.py:202
  121.9 1.3 copy.68
  123.1 4.0 %convolution_negate_fusion = f32[18,128,256]{2,1,0:T(8,128)S(1)} fusion(f32[256,18,128]{2,0,1:T(8,128)S(1)} %bitcast.55, f32[256,256,1]{0,1,2:T(8,128)S(1)} %copy-done.7), kind=kOutput, calls=%fused_computation.44 | convolution fusion | flops 1812529152 | bytes 4980736 | tf_op jit(solution)/shard_map/qxr,tq->xrt/dot_general | solution.py:204
  127.2 0.7 fusion.48
  127.9 0.4 fusion.47
  128.3 0.4 collective-permute-start.1
  128.8 2.3 %fusion.22 = f32[16,128,256]{2,1,0:T(8,128)} fusion(f32[16,128,256]{2,1,0:T(8,128)S(1)} %copy-done, f32[16,128,1]{2,1,0:T(8,128)S(1)} %get-tuple-element.30, f32[16,128,255]{2,1,0:T(8,128)S(1)} %get-tuple-element.32, f32[16,128,255]{2,1,0:T(8,128)S(1)} %get-tuple-element.31, f32[16,128,1]{2,1,0:T(8,128)S(1)} %get-tuple-element.29, f32[128]{0:T(128)S(1)} %get-tuple-element.52), kind=kLoop, calls=%fused_computation.37 | loop fusion | flops 2621440 | bytes 8389120 | tf_op jit(solution)/shard_map/sub | solution.py:221
  131.1 0.0 copy-start.3
  131.1 0.0 copy-start.5
  131.1 0.1 slice.238
  131.3 0.9 collective-permute-done.1
  132.2 0.5 copy-done.3
  132.7 0.6 copy-done.5
  133.3 2.7 %fusion.14 = (f32[16,128,256]{2,1,0:T(8,128)}, f32[16,128,256]{2,1,0:T(8,128)}) fusion(f32[16,128,256]{2,1,0:T(8,128)S(1)} %copy-done.5, f32[16,128,256]{2,1,0:T(8,128)S(1)} %slice.238, f32[16,1,256]{2,1,0:T(1,128)S(1)} %get-tuple-element.28, f32[16,1,256]{2,1,0:T(1,128)S(1)} %get-tuple-element.27, f32[16,128,256]{2,1,0:T(8,128)S(1)} %copy-done.3, ...), kind=kLoop, calls=%fused_computation.22 | loop fusion | flops 5242880 | bytes 10780672 | tf_op jit(solution)/shard_map/sub | solution.py:220
  (23 shorter events, 0.3 us)
Async XLA Ops:
  3.5 7.3 %collective-permute-start = (f32[16,1,256]{2,1,0:T(1,128)S(1)}, f32[16,1,256]{2,1,0:T(1,128)S(1)}, u32[]{:S(2)}, u32[]{:S(2)}) collective-permute-start(f32[16,1,256]{2,1,0:T(1,128)S(1)} %fusion.38), channel_id=1, source_target_pairs={{0,1},{1,0},{2,3},{3,2},{4,5},{5,4},{6,7},{7,6},{8,9},{9,8},{10,11... | collective-permute-start | bytes 49160 | tf_op jit(solution)/shard_map/ppermute | solution.py:155
  4.4 3.1 %copy-start = (f32[16,128,256]{2,1,0:T(8,128)S(1)}, f32[16,128,256]{2,1,0:T(8,128)}, u32[]{:S(2)}) copy-start(f32[16,128,256]{2,1,0:T(8,128)} %param.14) | copy-start | bytes 6291460
  7.5 1.6 %copy-start.4 = (f32[16,128,256]{2,1,0:T(8,128)S(1)}, f32[16,128,256]{2,1,0:T(8,128)}, u32[]{:S(2)}) copy-start(f32[16,128,256]{2,1,0:T(8,128)} %param.13) | copy-start | bytes 6291460
  9.1 1.6 %copy-start.2 = (f32[16,128,256]{2,1,0:T(8,128)S(1)}, f32[16,128,256]{2,1,0:T(8,128)}, u32[]{:S(2)}) copy-start(f32[16,128,256]{2,1,0:T(8,128)} %param.12) | copy-start | bytes 6291460
  9.1 1.6 %copy-start.9 = (f32[48]{0:T(128)S(1)}, f32[48]{0:T(128)}, u32[]{:S(2)}) copy-start(f32[48]{0:T(128)} %param.15) | copy-start | bytes 580
  9.1 2.2 %copy-start.6 = (s32[16,128,256]{2,1,0:T(8,128)S(1)}, s32[16,128,256]{2,1,0:T(8,128)}, u32[]{:S(2)}) copy-start(s32[16,128,256]{2,1,0:T(8,128)} %param.16) | copy-start | bytes 6291460
  11.3 2.6 %copy-start.7 = (f32[256,256,1]{0,1,2:T(8,128)S(1)}, f32[256,256,1]{0,1,2:T(8,128)}, u32[]{:S(2)}) copy-start(f32[256,256,1]{0,1,2:T(8,128)} %constant.146) | copy-start | bytes 786436
  17.4 43.1 %all-to-all-start = ((f32[128,2,18,128]{3,1,2,0:T(2,128)}), f32[128,2,18,128]{3,1,2,0:T(2,128)}, u32[]{:S(2)}, u32[]{:S(2)}) async-start(f32[128,2,18,128]{3,1,2,0:T(2,128)} %copy.56), calls=%async_computation | async-start | bytes 4718592 | tf_op jit(solution)/shard_map/all_to_all | solution.py:174
  62.7 2.2 %copy-start.1 = (f32[1024,64,16,1,1]{0,1,2,4,3:T(8,128)S(1)}, f32[1024,64,16,1,1]{0,1,2,4,3:T(8,128)}, u32[]{:S(2)}) copy-start(f32[1024,64,16,1,1]{0,1,2,4,3:T(8,128)} %constant.147) | copy-start | bytes 12582916
  68.5 1.0 copy-start.8
  128.3 3.8 %collective-permute-start.1 = (f32[16,1,256]{2,1,0:T(1,128)S(1)}, f32[16,1,256]{2,1,0:T(1,128)S(1)}, u32[]{:S(2)}, u32[]{:S(2)}) collective-permute-start(f32[16,1,256]{2,1,0:T(1,128)S(1)} %broadcast_select_fusion.2), channel_id=1, source_target_pairs={{0,1},{1,0},{2,3},{3,2},{4,5},{5,4},{6,7},{7,6},{8,9},{9,8},{10,11... | collective-permute-start | bytes 49160 | tf_op jit(solution)/shard_map/ppermute | solution.py:37
  131.1 1.6 %copy-start.3 = (f32[16,128,256]{2,1,0:T(8,128)S(1)}, f32[16,128,256]{2,1,0:T(8,128)}, u32[]{:S(2)}) copy-start(f32[16,128,256]{2,1,0:T(8,128)} %param.12) | copy-start | bytes 6291460
  131.1 2.2 %copy-start.5 = (f32[16,128,256]{2,1,0:T(8,128)S(1)}, f32[16,128,256]{2,1,0:T(8,128)}, u32[]{:S(2)}) copy-start(f32[16,128,256]{2,1,0:T(8,128)} %param.13) | copy-start | bytes 6291460

commit v6 on v4

--- a/solution.py
+++ b/solution.py
@@ -119,6 +119,17 @@
 
 AZIMUTH_TABLE = fixed_azimuth_basis()
 AXIAL_TABLE = fixed_axial_basis()
+
+
+def halo_axial_tables(blocks):
+    width = NX // blocks
+    table = AXIAL_TABLE.reshape(NX, blocks, width)
+    zero = np.zeros((NX, 1), np.float32)
+    below = np.concatenate([zero, AXIAL_TABLE[:, width - 1 : NX - 1 : width]], axis=1)
+    above = np.concatenate([AXIAL_TABLE[:, width::width], zero], axis=1)
+    forward = np.concatenate([table, 0.5 * below[:, :, None], -0.5 * above[:, :, None]], axis=2)
+    inverse = np.concatenate([table, below[:, :, None], above[:, :, None]], axis=2)
+    return forward.astype(np.float32), inverse.astype(np.float32)
 RADIAL_TABLE = fixed_radial_basis()
 
 
@@ -168,31 +179,19 @@
     spectrum_in = spectrum_in.reshape(device_count, modes_each, axial_block + 2, radial_block)
     resident = lax.all_to_all(spectrum_in, both, split_axis=0, concat_axis=0, tiled=True)
     resident = resident.reshape(gz_count, row_count, modes_each, axial_block + 2, radial_block)
-    first_hat = resident[:, :, :, axial_block]
-    last_hat = resident[:, :, :, axial_block + 1]
-    next_first = jnp.concatenate([first_hat[1:], jnp.zeros_like(first_hat[:1])], axis=0)
-    prev_last = jnp.concatenate([jnp.zeros_like(last_hat[:1]), last_hat[:-1]], axis=0)
-    resident = resident[:, :, :, :axial_block]
-    resident = resident.at[:, :, :, axial_block - 1].add(0.5 * next_first)
-    resident = resident.at[:, :, :, 0].add(-0.5 * prev_last)
     mode_ids = lax.axis_index(both) * modes_each + jnp.arange(modes_each, dtype=jnp.int32)
-    axial_table = jnp.asarray(AXIAL_TABLE).reshape(NX, gz_count, axial_block)
+    forward_table, inverse_table = halo_axial_tables(gz_count)
     radial_table = jnp.asarray(RADIAL_TABLE)
     axial_coefficient = jnp.einsum(
-        "kgx,grmxj->mkrj", axial_table, resident, precision=forward_precision
+        "kgx,grmxj->mkrj", jnp.asarray(forward_table), resident, precision=forward_precision
     ).reshape(modes_each, NX, NR)
     spectrum = jnp.einsum("sj,mkj->mks", radial_table, axial_coefficient, precision=forward_precision)
     scaled = spectrum / denominator_of(mode_ids, jnp.arange(NR, dtype=jnp.int32))
     radial_returned = jnp.einsum("sj,mks->mkj", radial_table, scaled, precision=maximal_precision)
     radial_returned = radial_returned.reshape(modes_each, NX, row_count, radial_block)
-    physical_space = jnp.einsum(
-        "kgx,mkrj->grmxj", axial_table, radial_returned, precision=maximal_precision
-    )
-    first_p = physical_space[:, :, :, :1]
-    last_p = physical_space[:, :, :, -1:]
-    ghost_low = jnp.concatenate([jnp.zeros_like(last_p[:1]), last_p[:-1]], axis=0)
-    ghost_high = jnp.concatenate([first_p[1:], jnp.zeros_like(first_p[:1])], axis=0)
-    windows = jnp.concatenate([physical_space, ghost_low, ghost_high], axis=3)
+    windows = jnp.einsum(
+        "kgx,mkrj->grmxj", jnp.asarray(inverse_table), radial_returned, precision=maximal_precision
+    )
     windows = windows.reshape(device_count, modes_each, axial_block + 2, radial_block)
     returned = lax.all_to_all(windows, both, split_axis=0, concat_axis=0, tiled=True)
     returned = returned.reshape(NT, axial_block + 2, radial_block)

time: 134 us -> 134 us (level)
  matrix products: 20 us -> 24.7 us
  local copies, waits for them, and re-layouts: 17.1 us -> 13 us
    dot_general x2, matrix products: 10.5 us -> 15.3 us  [the longest x1 7.92 us: body(): jnp.einsum('kgx,mkrj->grmxj', jnp.asarray(inverse_table), radial_returned...]
    all_to_all x1 -> x0, local copies, waits for them, and re-layouts: 1.95 us -> none  [body(): lax.all_to_all(spectrum_in, both, split_axis=0, concat_axis=0, tiled=True)]
    concatenate x1 -> x0, local copies, waits for them, and re-layouts: 1.95 us -> none  [body(): windows = jnp.concatenate([physical_space, ghost_low, ghost_high], axis=3)]
    transpose x1 -> x2, local copies, waits for them, and re-layouts: 0.24 us -> 2.18 us  [the longest x1 1.95 us: body(): jnp.einsum('kgx,mkrj->grmxj', jnp.asarray(inverse_table), radial_returned...]
    unnamed x19 -> x20, local copies, waits for them, and re-layouts: 5.02 us -> 3.13 us
where the time goes in v6:
time: 134 us; the launch traced here: 131 us
  blocking collectives  37.2 us (28%)
  waiting for transfers between devices  32.9 us (25%)
  matrix products  24.7 us (18%)
  local copies, waits for them, and re-layouts  13 us (10%)
  starting transfers between devices  12.6 us (9%)
  other arithmetic  10.1 us (8%)
    all_to_all x1, blocking collectives, body(): lax.all_to_all(windows, both, split_axis=0, concat_axis=0, tiled=True)  37.2 us
    all_to_all x1, waiting for transfers between devices, body(): lax.all_to_all(spectrum_in, both, split_axis=0, concat_axis=0, tiled=True)  31.6 us
    all_to_all x1, starting transfers between devices, body(): lax.all_to_all(spectrum_in, both, split_axis=0, concat_axis=0, tiled=True)  11.2 us
    dot_general x1, matrix products, body(): jnp.einsum('kgx,mkrj->grmxj', jnp.asarray(inverse_table), radial_returned...  7.92 us
    dot_general x1, matrix products, body(): jnp.einsum('kgx,grmxj->mkrj', jnp.asarray(forward_table), resident, preci...  7.36 us
    dot_general x1, matrix products, body(): jnp.einsum('qxr,tq->xrt', returned, fourier, precision=maximal_precision)  4 us
    unnamed x20, local copies, waits for them, and re-layouts  3.13 us
    sub x1, other arithmetic, body(): radial_projected_velocity = radial_vel - 0.5 * (above - below)  2.74 us
  transfers between devices with their start and end apart: 3, of which 3 were waited for; matrix products, arithmetic and copies ran while one was open for 3% of the time, Pallas kernels for 0%

profile of v6, /device:TPU:6, one launch (start us, length us, event | category | flops | bytes accessed | tf_op | source)
XLA Modules:
  0.0 131.5 jit_solution(5251263687583025631)
XLA Ops:
  0.6 0.0 copy-start
  0.7 2.0 %broadcast_multiply_fusion = f32[16,128,256]{2,1,0:T(8,128)S(1)} fusion(f32[16,128,256]{2,1,0:T(8,128)} %param.10, f32[128]{0:T(128)S(1)} %convert_add_fusion), kind=kLoop, calls=%fused_computation.44 | loop fusion | flops 524288 | bytes 4194816 | tf_op jit(solution)/shard_map/mul | solution.py:162
  2.7 0.9 collective-permute-start
  3.6 0.0 copy-done
  3.6 0.7 fusion.46
  4.3 0.0 copy-start.1
  4.3 0.0 copy-start.7
  4.4 0.0 copy-start.4
  4.4 0.4 fusion.45
  4.7 1.2 copy-done.1
  5.9 0.0 copy-done.7
  6.0 0.1 select_reduce_fusion
  6.1 0.5 collective-permute-done
  6.5 0.0 copy-done.4
  6.6 0.0 copy-start.5
  6.6 2.6 %fusion.12 = f32[16,128,256]{2,1,0:T(8,128)S(1)} fusion(f32[16,128,256]{2,1,0:T(8,128)S(1)} %copy-done.1, f32[16,128,256]{2,1,0:T(8,128)S(1)} %broadcast_multiply_fusion, f32[16,1,256]{2,1,0:T(1,128)S(1)} %get-tuple-element.20, f32[16,1,256]{2,1,0:T(1,128)S(1)} %get-tuple-element.19, f32[16,128,1]{2,1,0:T(8,128)S(1)} %get-tuple-element.14, ...), kind=kLoop, calls=%fused_computation.14 | loop fusion | flops 7864320 | bytes 12617728 | tf_op jit(solution)/shard_map/sub | solution.py:173
  9.2 0.0 copy-done.5
  9.2 1.2 fusion
  10.5 2.2 %copy.46 = f32[128,2,18,128]{3,1,2,0:T(2,128)} copy(f32[128,2,18,128]{3,1,0,2:T(2,128)S(1)} %bitcast.36) | data formatting | bytes 4718592 | tf_op jit(solution)/shard_map/reshape | solution.py:179
  12.7 11.2 %all-to-all-start = ((f32[128,2,18,128]{3,1,2,0:T(2,128)}), f32[128,2,18,128]{3,1,2,0:T(2,128)}, u32[]{:S(2)}, u32[]{:S(2)}) async-start(f32[128,2,18,128]{3,1,2,0:T(2,128)} %copy.46), calls=%async_computation | async-start | bytes 4718592 | tf_op jit(solution)/shard_map/all_to_all | solution.py:180
  24.1 0.1 broadcast_add_fusion
  24.2 31.6 %all-to-all-done = f32[128,2,18,128]{3,1,2,0:T(2,128)} async-done(((f32[128,2,18,128]{3,1,2,0:T(2,128)}), f32[128,2,18,128]{3,1,2,0:T(2,128)}, u32[]{:S(2)}, u32[]{:S(2)}) %all-to-all-start) | async-done | bytes 2359328 | tf_op jit(solution)/shard_map/all_to_all | solution.py:180
  55.8 7.4 %fusion.28 = f32[2,1024,2,128]{1,3,0,2:T(8,128)S(1)} fusion(f32[1024,64,18,1,1]{0,1,2,4,3:T(8,128)} %constant.82, f32[64,2,2,18,128]{4,2,3,1,0:T(2,128)} %bitcast.2), kind=kOutput, calls=%fused_computation.40 | convolution fusion | flops 3623878656 | bytes 9175040 | tf_op jit(solution)/shard_map/kgx,grmxj->mkrj/dot_general | solution.py:185
  63.2 0.0 copy-start.6
  63.2 0.2 copy.49
  63.4 0.7 copy-done.6
  64.1 1.8 %fusion.48 = f32[2,1024,256]{2,1,0:T(8,128)S(1)} fusion(f32[2,1024,256]{1,2,0:T(8,128)S(1)} %bitcast.39, f32[256,256,1]{1,0,2:T(8,128)S(1)} %copy-done.6), kind=kOutput, calls=%fused_computation.78 | convolution fusion | flops 805306368 | bytes 4456448 | tf_op jit(solution)/shard_map/sj,mkj->mks/dot_general | solution.py:188
  66.0 0.0 slice-start.1
  66.0 2.4 %fusion.24 = f32[2,1024,256]{1,2,0:T(8,128)S(1)} fusion(f32[256,256,1]{1,0,2:T(8,128)S(1)} %copy-done.6, f32[2,1024,256]{2,1,0:T(8,128)S(1)} %fusion.48, f32[256]{0:T(256)S(1)} %multiply_subtract_fusion.1, f32[2,1024]{1,0:T(2,128)S(1)} %broadcast_add_fusion), kind=kOutput, calls=%fused_computation.34 | convolution fusion | flops 1612185600 | bytes 4465664 | tf_op jit(solution)/shard_map/sj,mks->mkj/dot_general | solution.py:190
  68.4 0.0 slice-done
  68.4 0.0 slice-done.1
  68.4 7.9 %convolution_bitcast_fusion = f32[64,2,2,18,128]{4,0,3,1,2:T(8,128)S(1)} fusion(f32[2,1024,2,128,1]{1,3,4,2,0:T(8,128)S(1)} %bitcast.42, f32[1024,64,18,1,1]{0,1,2,4,3:T(8,128)S(1)} %bitcast.41), kind=kOutput, calls=%fused_computation.39 | convolution fusion | flops 7247757312 | bytes 9175040 | tf_op jit(solution)/shard_map/kgx,mkrj->grmxj/dot_general | solution.py:192
  76.3 1.9 %copy.53 = f32[64,2,2,18,128]{4,1,0,3,2:T(2,128)S(1)} copy(f32[64,2,2,18,128]{4,0,3,1,2:T(8,128)S(1)} %convolution_bitcast_fusion) | data formatting | bytes 4718592 | tf_op jit(solution)/shard_map/kgx,mkrj->grmxj/transpose | solution.py:192
  78.3 1.8 %copy.54 = f32[128,2,18,128]{3,1,2,0:T(2,128)S(1)} copy(f32[128,2,18,128]{3,0,2,1:T(8,128)S(1)} %bitcast.38) | data formatting | bytes 4718592 | tf_op jit(solution)/shard_map/reshape | solution.py:195
  80.1 37.2 %all_to_all.10 = f32[128,2,18,128]{3,1,2,0:T(2,128)S(1)} all-to-all(f32[128,2,18,128]{3,1,2,0:T(2,128)S(1)} %copy.54), channel_id=1, replica_groups=mesh['gz'=64,'row'=2] {'gz','row'}, dimensions={0} | all-to-all | bytes 4718592 | tf_op jit(solution)/shard_map/all_to_all | solution.py:196
  117.3 1.3 copy.55
  118.5 4.0 %convolution_negate_fusion = f32[18,128,256]{2,1,0:T(8,128)S(1)} fusion(f32[256,18,128]{2,0,1:T(8,128)S(1)} %bitcast.37, f32[256,256,1]{0,1,2:T(8,128)S(1)} %copy-done.5), kind=kOutput, calls=%fused_computation.38 | convolution fusion | flops 1812529152 | bytes 4980736 | tf_op jit(solution)/shard_map/qxr,tq->xrt/dot_general | solution.py:198
  122.6 0.7 fusion.43
  123.3 0.4 fusion.42
  123.7 0.4 collective-permute-start.1
  124.2 2.3 %fusion.23 = f32[16,128,256]{2,1,0:T(8,128)} fusion(f32[16,128,256]{2,1,0:T(8,128)S(1)} %copy-done, f32[16,128,1]{2,1,0:T(8,128)S(1)} %get-tuple-element.6, f32[16,128,255]{2,1,0:T(8,128)S(1)} %get-tuple-element.8, f32[16,128,255]{2,1,0:T(8,128)S(1)} %get-tuple-element.7, f32[16,128,1]{2,1,0:T(8,128)S(1)} %get-tuple-element.5, f32[128]{0:T(128)S(1)} %get-tuple-element.21), kind=kLoop, calls=%fused_computation.33 | loop fusion | flops 2621440 | bytes 8389120 | tf_op jit(solution)/shard_map/sub | solution.py:215
  126.5 0.0 copy-start.2
  126.5 0.0 copy-start.3
  126.5 0.1 slice.120
  126.7 0.9 collective-permute-done.1
  127.6 0.5 copy-done.2
  128.1 0.6 copy-done.3
  128.7 2.7 %fusion.15 = (f32[16,128,256]{2,1,0:T(8,128)}, f32[16,128,256]{2,1,0:T(8,128)}) fusion(f32[16,128,256]{2,1,0:T(8,128)S(1)} %copy-done.3, f32[16,128,256]{2,1,0:T(8,128)S(1)} %slice.120, f32[16,1,256]{2,1,0:T(1,128)S(1)} %get-tuple-element.4, f32[16,1,256]{2,1,0:T(1,128)S(1)} %get-tuple-element.3, f32[16,128,256]{2,1,0:T(8,128)S(1)} %copy-done.2, ...), kind=kLoop, calls=%fused_computation.18 | loop fusion | flops 5242880 | bytes 10780672 | tf_op jit(solution)/shard_map/sub | solution.py:214
  (14 shorter events, 0.3 us)
Async XLA Ops:
  0.6 3.0 %copy-start = (f32[16,128,256]{2,1,0:T(8,128)S(1)}, f32[16,128,256]{2,1,0:T(8,128)}, u32[]{:S(2)}) copy-start(f32[16,128,256]{2,1,0:T(8,128)} %param.11) | copy-start | bytes 6291460
  2.7 3.8 %collective-permute-start = (f32[16,1,256]{2,1,0:T(1,128)S(1)}, f32[16,1,256]{2,1,0:T(1,128)S(1)}, u32[]{:S(2)}, u32[]{:S(2)}) collective-permute-start(f32[16,1,256]{2,1,0:T(1,128)S(1)} %broadcast_select_fusion.5), channel_id=1, source_target_pairs={{0,1},{1,0},{2,3},{3,2},{4,5},{5,4},{6,7},{7,6},{8,9},{9,8},{10,11... | collective-permute-start | bytes 49160 | tf_op jit(solution)/shard_map/ppermute | solution.py:37
  4.3 1.6 %copy-start.1 = (f32[16,128,256]{2,1,0:T(8,128)S(1)}, f32[16,128,256]{2,1,0:T(8,128)}, u32[]{:S(2)}) copy-start(f32[16,128,256]{2,1,0:T(8,128)} %param.9) | copy-start | bytes 6291460
  4.3 1.6 %copy-start.7 = (f32[48]{0:T(128)S(1)}, f32[48]{0:T(128)}, u32[]{:S(2)}) copy-start(f32[48]{0:T(128)} %param.12) | copy-start | bytes 580
  4.4 2.2 %copy-start.4 = (s32[16,128,256]{2,1,0:T(8,128)S(1)}, s32[16,128,256]{2,1,0:T(8,128)}, u32[]{:S(2)}) copy-start(s32[16,128,256]{2,1,0:T(8,128)} %param.13) | copy-start | bytes 6291460
  6.6 2.6 %copy-start.5 = (f32[256,256,1]{0,1,2:T(8,128)S(1)}, f32[256,256,1]{0,1,2:T(8,128)}, u32[]{:S(2)}) copy-start(f32[256,256,1]{0,1,2:T(8,128)} %constant.81) | copy-start | bytes 786436
  12.7 43.1 %all-to-all-start = ((f32[128,2,18,128]{3,1,2,0:T(2,128)}), f32[128,2,18,128]{3,1,2,0:T(2,128)}, u32[]{:S(2)}, u32[]{:S(2)}) async-start(f32[128,2,18,128]{3,1,2,0:T(2,128)} %copy.46), calls=%async_computation | async-start | bytes 4718592 | tf_op jit(solution)/shard_map/all_to_all | solution.py:180
  63.2 1.0 copy-start.6
  64.1 4.3 %slice-start = ((s8[4718592]{0:T(1024)(128)(4,1)}), s8[4194304]{0:T(1024)(128)(4,1)S(1)}, s32[]{:S(2)}) async-start(s8[4718592]{0:T(1024)(128)(4,1)} %bitcast.40), calls=%async_computation.2 | async-start | bytes 8388608
  66.0 2.4 %slice-start.1 = ((s8[4718592]{0:T(1024)(128)(4,1)}), s8[524288]{0:T(1024)(128)(4,1)S(1)}, s32[]{:S(2)}) async-start(s8[4718592]{0:T(1024)(128)(4,1)} %bitcast.40), calls=%async_computation.3 | async-start | bytes 1048576
  123.7 3.8 %collective-permute-start.1 = (f32[16,1,256]{2,1,0:T(1,128)S(1)}, f32[16,1,256]{2,1,0:T(1,128)S(1)}, u32[]{:S(2)}, u32[]{:S(2)}) collective-permute-start(f32[16,1,256]{2,1,0:T(1,128)S(1)} %broadcast_select_fusion.2), channel_id=1, source_target_pairs={{0,1},{1,0},{2,3},{3,2},{4,5},{5,4},{6,7},{7,6},{8,9},{9,8},{10,11... | collective-permute-start | bytes 49160 | tf_op jit(solution)/shard_map/ppermute | solution.py:37
  126.5 1.6 %copy-start.2 = (f32[16,128,256]{2,1,0:T(8,128)S(1)}, f32[16,128,256]{2,1,0:T(8,128)}, u32[]{:S(2)}) copy-start(f32[16,128,256]{2,1,0:T(8,128)} %param.9) | copy-start | bytes 6291460
  126.5 2.2 %copy-start.3 = (f32[16,128,256]{2,1,0:T(8,128)S(1)}, f32[16,128,256]{2,1,0:T(8,128)}, u32[]{:S(2)}) copy-start(f32[16,128,256]{2,1,0:T(8,128)} %param.10) | copy-start | bytes 6291460

commit v7 on v6

--- a/solution.py
+++ b/solution.py
@@ -180,7 +180,7 @@
     resident = lax.all_to_all(spectrum_in, both, split_axis=0, concat_axis=0, tiled=True)
     resident = resident.reshape(gz_count, row_count, modes_each, axial_block + 2, radial_block)
     mode_ids = lax.axis_index(both) * modes_each + jnp.arange(modes_each, dtype=jnp.int32)
-    forward_table, inverse_table = halo_axial_tables(gz_count)
+    forward_table = halo_axial_tables(gz_count)[0]
     radial_table = jnp.asarray(RADIAL_TABLE)
     axial_coefficient = jnp.einsum(
         "kgx,grmxj->mkrj", jnp.asarray(forward_table), resident, precision=forward_precision
@@ -189,9 +189,17 @@
     scaled = spectrum / denominator_of(mode_ids, jnp.arange(NR, dtype=jnp.int32))
     radial_returned = jnp.einsum("sj,mks->mkj", radial_table, scaled, precision=maximal_precision)
     radial_returned = radial_returned.reshape(modes_each, NX, row_count, radial_block)
-    windows = jnp.einsum(
-        "kgx,mkrj->grmxj", jnp.asarray(inverse_table), radial_returned, precision=maximal_precision
-    )
+    physical_space = jnp.einsum(
+        "kgx,mkrj->grmxj",
+        jnp.asarray(AXIAL_TABLE).reshape(NX, gz_count, axial_block),
+        radial_returned,
+        precision=maximal_precision,
+    )
+    first_p = physical_space[:, :, :, :1]
+    last_p = physical_space[:, :, :, -1:]
+    ghost_low = jnp.concatenate([jnp.zeros_like(last_p[:1]), last_p[:-1]], axis=0)
+    ghost_high = jnp.concatenate([first_p[1:], jnp.zeros_like(first_p[:1])], axis=0)
+    windows = jnp.concatenate([physical_space, ghost_low, ghost_high], axis=3)
     windows = windows.reshape(device_count, modes_each, axial_block + 2, radial_block)
     returned = lax.all_to_all(windows, both, split_axis=0, concat_axis=0, tiled=True)
     returned = returned.reshape(NT, axial_block + 2, radial_block)

time: 134 us -> 133 us (level)
    concatenate x0 -> x1, local copies, waits for them, and re-layouts: none -> 2.16 us  [body(): windows = jnp.concatenate([physical_space, ghost_low, ghost_high], axis=3)]
    transpose x1 -> x0, local copies, waits for them, and re-layouts: 1.95 us -> none  [body(): jnp.einsum('kgx,mkrj->grmxj', jnp.asarray(inverse_table), radial_returned...]
    unnamed x20 -> x18, local copies, waits for them, and re-layouts: 3.13 us -> 3.12 us
where the time goes in v7:
time: 133 us; the launch traced here: 131 us
  blocking collectives  37.2 us (28%)
  waiting for transfers between devices  32.9 us (25%)
  matrix products  23.6 us (18%)
  local copies, waits for them, and re-layouts  13.2 us (10%)
  starting transfers between devices  12.6 us (9%)
  other arithmetic  10.3 us (8%)
    all_to_all x1, blocking collectives, body(): lax.all_to_all(windows, both, split_axis=0, concat_axis=0, tiled=True)  37.2 us
    all_to_all x1, waiting for transfers between devices, body(): lax.all_to_all(spectrum_in, both, split_axis=0, concat_axis=0, tiled=True)  31.6 us
    all_to_all x1, starting transfers between devices, body(): lax.all_to_all(spectrum_in, both, split_axis=0, concat_axis=0, tiled=True)  11.2 us
    dot_general x1, matrix products, body(): jnp.einsum('kgx,grmxj->mkrj', jnp.asarray(forward_table), resident, preci...  7.36 us
    dot_general x1, matrix products, body(): jnp.einsum('kgx,mkrj->grmxj', jnp.asarray(AXIAL_TABLE).reshape(NX, gz_cou...  6.77 us
    dot_general x1, matrix products, body(): jnp.einsum('qxr,tq->xrt', returned, fourier, precision=maximal_precision)  4 us
    unnamed x18, local copies, waits for them, and re-layouts  3.12 us
    sub x1, other arithmetic, body(): radial_projected_velocity = radial_vel - 0.5 * (above - below)  2.74 us
  transfers between devices with their start and end apart: 3, of which 3 were waited for; matrix products, arithmetic and copies ran while one was open for 3% of the time, Pallas kernels for 0%

profile of v7, /device:TPU:6, one launch (start us, length us, event | category | flops | bytes accessed | tf_op | source)
XLA Modules:
  0.0 130.7 jit_solution(14582566149684006117)
XLA Ops:
  0.6 0.0 copy-start
  0.7 2.0 %broadcast_multiply_fusion = f32[16,128,256]{2,1,0:T(8,128)S(1)} fusion(f32[16,128,256]{2,1,0:T(8,128)} %param.10, f32[128]{0:T(128)S(1)} %convert_add_fusion), kind=kLoop, calls=%fused_computation.50 | loop fusion | flops 524288 | bytes 4194816 | tf_op jit(solution)/shard_map/mul | solution.py:162
  2.7 0.9 collective-permute-start
  3.6 0.0 copy-done
  3.6 0.7 fusion.48
  4.3 0.0 copy-start.1
  4.3 0.0 copy-start.8
  4.4 0.0 copy-start.5
  4.4 0.4 fusion.47
  4.7 1.2 copy-done.1
  5.9 0.0 copy-done.8
  6.0 0.1 select_reduce_fusion
  6.1 0.5 collective-permute-done
  6.5 0.0 copy-done.5
  6.6 0.0 copy-start.6
  6.6 2.6 %fusion.13 = f32[16,128,256]{2,1,0:T(8,128)S(1)} fusion(f32[16,128,256]{2,1,0:T(8,128)S(1)} %copy-done.1, f32[16,128,256]{2,1,0:T(8,128)S(1)} %broadcast_multiply_fusion, f32[16,1,256]{2,1,0:T(1,128)S(1)} %get-tuple-element.22, f32[16,1,256]{2,1,0:T(1,128)S(1)} %get-tuple-element.21, f32[16,128,1]{2,1,0:T(8,128)S(1)} %get-tuple-element.16, ...), kind=kLoop, calls=%fused_computation.20 | loop fusion | flops 7864320 | bytes 12617728 | tf_op jit(solution)/shard_map/sub | solution.py:173
  9.2 0.0 copy-done.6
  9.2 1.2 fusion
  10.5 2.2 %copy.46 = f32[128,2,18,128]{3,1,2,0:T(2,128)} copy(f32[128,2,18,128]{3,1,0,2:T(2,128)S(1)} %bitcast.36) | data formatting | bytes 4718592 | tf_op jit(solution)/shard_map/reshape | solution.py:179
  12.7 11.2 %all-to-all-start = ((f32[128,2,18,128]{3,1,2,0:T(2,128)}), f32[128,2,18,128]{3,1,2,0:T(2,128)}, u32[]{:S(2)}, u32[]{:S(2)}) async-start(f32[128,2,18,128]{3,1,2,0:T(2,128)} %copy.46), calls=%async_computation | async-start | bytes 4718592 | tf_op jit(solution)/shard_map/all_to_all | solution.py:180
  24.1 0.1 broadcast_add_fusion
  24.2 31.6 %all-to-all-done = f32[128,2,18,128]{3,1,2,0:T(2,128)} async-done(((f32[128,2,18,128]{3,1,2,0:T(2,128)}), f32[128,2,18,128]{3,1,2,0:T(2,128)}, u32[]{:S(2)}, u32[]{:S(2)}) %all-to-all-start) | async-done | bytes 2359328 | tf_op jit(solution)/shard_map/all_to_all | solution.py:180
  55.8 7.4 %fusion.29 = f32[2,1024,2,128]{1,3,0,2:T(8,128)S(1)} fusion(f32[1024,64,18,1,1]{0,1,2,4,3:T(8,128)} %constant.88, f32[64,2,2,18,128]{4,2,3,1,0:T(2,128)} %bitcast.2), kind=kOutput, calls=%fused_computation.45 | convolution fusion | flops 3623878656 | bytes 9175040 | tf_op jit(solution)/shard_map/kgx,grmxj->mkrj/dot_general | solution.py:185
  63.1 0.0 copy-start.7
  63.2 0.2 copy.49
  63.4 0.7 copy-done.7
  64.1 1.8 %fusion.50 = f32[2,1024,256]{2,1,0:T(8,128)S(1)} fusion(f32[2,1024,256]{1,2,0:T(8,128)S(1)} %bitcast.39, f32[256,256,1]{1,0,2:T(8,128)S(1)} %copy-done.7), kind=kOutput, calls=%fused_computation.85 | convolution fusion | flops 805306368 | bytes 4456448 | tf_op jit(solution)/shard_map/sj,mkj->mks/dot_general | solution.py:188
  65.9 0.0 copy-start.4
  66.0 2.4 %fusion.25 = f32[2,1024,256]{1,2,0:T(8,128)S(1)} fusion(f32[256,256,1]{1,0,2:T(8,128)S(1)} %copy-done.7, f32[2,1024,256]{2,1,0:T(8,128)S(1)} %fusion.50, f32[256]{0:T(256)S(1)} %multiply_subtract_fusion.1, f32[2,1024]{1,0:T(2,128)S(1)} %broadcast_add_fusion), kind=kOutput, calls=%fused_computation.40 | convolution fusion | flops 1612185600 | bytes 4465664 | tf_op jit(solution)/shard_map/sj,mks->mkj/dot_general | solution.py:190
  68.3 0.0 copy-done.4
  68.4 6.8 %convolution_bitcast_fusion = f32[64,2,2,16,128]{4,0,3,1,2:T(8,128)S(1)} fusion(f32[2,1024,2,128,1]{1,3,4,2,0:T(8,128)S(1)} %bitcast.40, f32[1024,64,16,1,1]{0,1,2,4,3:T(8,128)S(1)} %copy-done.4), kind=kOutput, calls=%fused_computation.46 | convolution fusion | flops 6442450944 | bytes 8388608 | tf_op jit(solution)/shard_map/kgx,mkrj->grmxj/dot_general | solution.py:192
  75.2 0.2 select_maximum_fusion
  75.4 2.2 %copy.53 = f32[64,2,2,18,128]{4,1,0,3,2:T(2,128)S(1)} copy(f32[64,2,2,18,128]{4,0,3,1,2:T(8,128)S(1)} %select_maximum_fusion) | data formatting | bytes 4718592 | tf_op jit(solution)/shard_map/concatenate | solution.py:202
  77.5 1.8 %copy.54 = f32[128,2,18,128]{3,1,2,0:T(2,128)S(1)} copy(f32[128,2,18,128]{3,0,2,1:T(8,128)S(1)} %bitcast.38) | data formatting | bytes 4718592 | tf_op jit(solution)/shard_map/reshape | solution.py:203
  79.3 37.2 %all_to_all.10 = f32[128,2,18,128]{3,1,2,0:T(2,128)S(1)} all-to-all(f32[128,2,18,128]{3,1,2,0:T(2,128)S(1)} %copy.54), channel_id=1, replica_groups=mesh['gz'=64,'row'=2] {'gz','row'}, dimensions={0} | all-to-all | bytes 4718592 | tf_op jit(solution)/shard_map/all_to_all | solution.py:204
  116.5 1.3 copy.55
  117.8 4.0 %convolution_negate_fusion = f32[18,128,256]{2,1,0:T(8,128)S(1)} fusion(f32[256,18,128]{2,0,1:T(8,128)S(1)} %bitcast.37, f32[256,256,1]{0,1,2:T(8,128)S(1)} %copy-done.6), kind=kOutput, calls=%fused_computation.44 | convolution fusion | flops 1812529152 | bytes 4980736 | tf_op jit(solution)/shard_map/qxr,tq->xrt/dot_general | solution.py:206
  121.8 0.7 fusion.44
  122.6 0.4 fusion.43
  123.0 0.4 collective-permute-start.1
  123.4 2.3 %fusion.24 = f32[16,128,256]{2,1,0:T(8,128)} fusion(f32[16,128,256]{2,1,0:T(8,128)S(1)} %copy-done, f32[16,128,1]{2,1,0:T(8,128)S(1)} %get-tuple-element.6, f32[16,128,255]{2,1,0:T(8,128)S(1)} %get-tuple-element.8, f32[16,128,255]{2,1,0:T(8,128)S(1)} %get-tuple-element.7, f32[16,128,1]{2,1,0:T(8,128)S(1)} %get-tuple-element.5, f32[128]{0:T(128)S(1)} %get-tuple-element.23), kind=kLoop, calls=%fused_computation.39 | loop fusion | flops 2621440 | bytes 8389120 | tf_op jit(solution)/shard_map/sub | solution.py:223
  125.8 0.0 copy-start.2
  125.8 0.0 copy-start.3
  125.8 0.1 slice.134
  125.9 0.9 collective-permute-done.1
  126.8 0.5 copy-done.2
  127.4 0.6 copy-done.3
  128.0 2.7 %fusion.16 = (f32[16,128,256]{2,1,0:T(8,128)}, f32[16,128,256]{2,1,0:T(8,128)}) fusion(f32[16,128,256]{2,1,0:T(8,128)S(1)} %copy-done.3, f32[16,128,256]{2,1,0:T(8,128)S(1)} %slice.134, f32[16,1,256]{2,1,0:T(1,128)S(1)} %get-tuple-element.4, f32[16,1,256]{2,1,0:T(1,128)S(1)} %get-tuple-element.3, f32[16,128,256]{2,1,0:T(8,128)S(1)} %copy-done.2, ...), kind=kLoop, calls=%fused_computation.24 | loop fusion | flops 5242880 | bytes 10780672 | tf_op jit(solution)/shard_map/sub | solution.py:222
  (13 shorter events, 0.3 us)
Async XLA Ops:
  0.6 3.0 %copy-start = (f32[16,128,256]{2,1,0:T(8,128)S(1)}, f32[16,128,256]{2,1,0:T(8,128)}, u32[]{:S(2)}) copy-start(f32[16,128,256]{2,1,0:T(8,128)} %param.11) | copy-start | bytes 6291460
  2.7 3.8 %collective-permute-start = (f32[16,1,256]{2,1,0:T(1,128)S(1)}, f32[16,1,256]{2,1,0:T(1,128)S(1)}, u32[]{:S(2)}, u32[]{:S(2)}) collective-permute-start(f32[16,1,256]{2,1,0:T(1,128)S(1)} %broadcast_select_fusion.5), channel_id=1, source_target_pairs={{0,1},{1,0},{2,3},{3,2},{4,5},{5,4},{6,7},{7,6},{8,9},{9,8},{10,11... | collective-permute-start | bytes 49160 | tf_op jit(solution)/shard_map/ppermute | solution.py:37
  4.3 1.6 %copy-start.1 = (f32[16,128,256]{2,1,0:T(8,128)S(1)}, f32[16,128,256]{2,1,0:T(8,128)}, u32[]{:S(2)}) copy-start(f32[16,128,256]{2,1,0:T(8,128)} %param.9) | copy-start | bytes 6291460
  4.3 1.6 %copy-start.8 = (f32[48]{0:T(128)S(1)}, f32[48]{0:T(128)}, u32[]{:S(2)}) copy-start(f32[48]{0:T(128)} %param.12) | copy-start | bytes 580
  4.4 2.2 %copy-start.5 = (s32[16,128,256]{2,1,0:T(8,128)S(1)}, s32[16,128,256]{2,1,0:T(8,128)}, u32[]{:S(2)}) copy-start(s32[16,128,256]{2,1,0:T(8,128)} %param.13) | copy-start | bytes 6291460
  6.6 2.6 %copy-start.6 = (f32[256,256,1]{0,1,2:T(8,128)S(1)}, f32[256,256,1]{0,1,2:T(8,128)}, u32[]{:S(2)}) copy-start(f32[256,256,1]{0,1,2:T(8,128)} %constant.87) | copy-start | bytes 786436
  12.7 43.1 %all-to-all-start = ((f32[128,2,18,128]{3,1,2,0:T(2,128)}), f32[128,2,18,128]{3,1,2,0:T(2,128)}, u32[]{:S(2)}, u32[]{:S(2)}) async-start(f32[128,2,18,128]{3,1,2,0:T(2,128)} %copy.46), calls=%async_computation | async-start | bytes 4718592 | tf_op jit(solution)/shard_map/all_to_all | solution.py:180
  63.1 1.0 copy-start.7
  65.9 2.4 %copy-start.4 = (f32[1024,64,16,1,1]{0,1,2,4,3:T(8,128)S(1)}, f32[1024,64,16,1,1]{0,1,2,4,3:T(8,128)}, u32[]{:S(2)}) copy-start(f32[1024,64,16,1,1]{0,1,2,4,3:T(8,128)} %constant.90) | copy-start | bytes 12582916
  123.0 3.8 %collective-permute-start.1 = (f32[16,1,256]{2,1,0:T(1,128)S(1)}, f32[16,1,256]{2,1,0:T(1,128)S(1)}, u32[]{:S(2)}, u32[]{:S(2)}) collective-permute-start(f32[16,1,256]{2,1,0:T(1,128)S(1)} %broadcast_select_fusion.2), channel_id=1, source_target_pairs={{0,1},{1,0},{2,3},{3,2},{4,5},{5,4},{6,7},{7,6},{8,9},{9,8},{10,11... | collective-permute-start | bytes 49160 | tf_op jit(solution)/shard_map/ppermute | solution.py:37
  125.8 1.6 %copy-start.2 = (f32[16,128,256]{2,1,0:T(8,128)S(1)}, f32[16,128,256]{2,1,0:T(8,128)}, u32[]{:S(2)}) copy-start(f32[16,128,256]{2,1,0:T(8,128)} %param.9) | copy-start | bytes 6291460
  125.8 2.2 %copy-start.3 = (f32[16,128,256]{2,1,0:T(8,128)S(1)}, f32[16,128,256]{2,1,0:T(8,128)}, u32[]{:S(2)}) copy-start(f32[16,128,256]{2,1,0:T(8,128)} %param.10) | copy-start | bytes 6291460

commit v8 on v7

--- a/solution.py
+++ b/solution.py
@@ -159,14 +159,21 @@
     own_cells = own_first + jnp.arange(radial_block, dtype=jnp.int32)
     radius = cell_radius(own_cells)[None, :, None]
     axial_pad = jnp.pad(axial_vel, ((1, 1), (0, 0), (0, 0)))
-    flux = radial_vel * radius
     if row_count == 2:
-        no_flux = jnp.zeros_like(flux[:, :1])
-        radial_flux = radial_neighbour(flux, no_flux, no_flux)
+        send = jnp.where(row_index == 0, radial_vel[:, -1:], radial_vel[:, :1])
+        received = lax.ppermute(send, "row", [(0, 1), (1, 0)])
+        no_vel = jnp.zeros_like(received)
+        low = jnp.where(row_index == 0, no_vel, received)
+        high = jnp.where(row_index == 0, received, no_vel)
+        up = jnp.concatenate([radial_vel[:, 1:], high], axis=1) * cell_radius(own_cells + 1)[None, :, None]
+        down = jnp.concatenate([low, radial_vel[:, :-1]], axis=1) * cell_radius(own_cells - 1)[None, :, None]
+        radial_term = (up - down) / (2.0 * radius)
     else:
+        flux = radial_vel * radius
         radial_flux = extended(flux, (("row", 1),), 1)
+        radial_term = (radial_flux[:, 2:] - radial_flux[:, :-2]) / (2.0 * radius)
     divergence = 0.5 * (axial_pad[2:] - axial_pad[:-2])
-    divergence = divergence + (radial_flux[:, 2:] - radial_flux[:, :-2]) / (2.0 * radius)
+    divergence = divergence + radial_term
     divergence = divergence + (jnp.roll(swirl_vel, -1, 2) - jnp.roll(swirl_vel, 1, 2)) / (
         2.0 * radius * spacing
     )

time: 133 us -> 143 us (1.075)
  local copies, waits for them, and re-layouts: 13.2 us -> 20.7 us
  other arithmetic: 10.3 us -> 13.4 us
    slice x0 -> x1, local copies, waits for them, and re-layouts: none -> 4.72 us  [body(): radial_vel[:, :-1]]
    sub x1, other arithmetic: 2.63 us -> 6.8 us  [body(): right_side = divergence - canopy_source(canopy_gore, inflow_rate)]
    slice x2, local copies, waits for them, and re-layouts: 1.07 us -> 4.09 us  [body(): jnp.roll(swirl_vel, 1, 2)]
    mul x1 -> x0, other arithmetic: 2 us -> none  [body(): flux = radial_vel * radius]
    unnamed x18 -> x14, local copies, waits for them, and re-layouts: 3.12 us -> 1.9 us
  transfers between devices with their start and end apart: 3 -> 3, of which waited for: 3 -> 2; matrix products, arithmetic and copies ran while one was open for 3% -> 9% of each run, Pallas kernels for 0% -> 0%
where the time goes in v8:
time: 143 us; the launch traced here: 141 us
  blocking collectives  37.2 us (26%)
  waiting for transfers between devices  32.5 us (23%)
  matrix products  23.6 us (17%)
  local copies, waits for them, and re-layouts  20.7 us (14%)
  other arithmetic  13.4 us (9%)
  starting transfers between devices  12.6 us (9%)
    all_to_all x1, blocking collectives, body(): lax.all_to_all(windows, both, split_axis=0, concat_axis=0, tiled=True)  37.2 us
    all_to_all x1, waiting for transfers between devices, body(): lax.all_to_all(spectrum_in, both, split_axis=0, concat_axis=0, tiled=True)  31.6 us
    all_to_all x1, starting transfers between devices, body(): lax.all_to_all(spectrum_in, both, split_axis=0, concat_axis=0, tiled=True)  11.3 us
    dot_general x1, matrix products, body(): jnp.einsum('kgx,grmxj->mkrj', jnp.asarray(forward_table), resident, preci...  7.36 us
    sub x1, other arithmetic, body(): right_side = divergence - canopy_source(canopy_gore, inflow_rate)  6.8 us
    dot_general x1, matrix products, body(): jnp.einsum('kgx,mkrj->grmxj', jnp.asarray(AXIAL_TABLE).reshape(NX, gz_cou...  6.78 us
    slice x1, local copies, waits for them, and re-layouts, body(): radial_vel[:, :-1]  4.72 us
    slice x2, local copies, waits for them, and re-layouts, body(): jnp.roll(swirl_vel, 1, 2)  4.09 us
  transfers between devices with their start and end apart: 3, of which 2 were waited for; matrix products, arithmetic and copies ran while one was open for 9% of the time, Pallas kernels for 0%

profile of v8, /device:TPU:6, one launch (start us, length us, event | category | flops | bytes accessed | tf_op | source)
XLA Modules:
  0.0 140.9 jit_solution(7025012443194818006)
XLA Ops:
  0.6 1.0 broadcast_select_fusion.5
  1.6 0.0 copy-start
  1.6 0.9 collective-permute-start
  2.6 4.7 %fusion.51 = (f32[16,127,256]{2,1,0:T(8,128)}, f32[16,127,256]{2,1,0:T(8,128)}) fusion(f32[16,128,256]{2,1,0:T(8,128)} %param.10), kind=kLoop, calls=%fused_computation.86 | loop fusion | bytes 8323072 | tf_op jit(solution)/shard_map/slice | solution.py:169
  7.3 0.0 copy-done
  7.3 2.8 %fusion.50 = (f32[16,128,255]{2,1,0:T(8,128)}, f32[16,128,255]{2,1,0:T(8,128)}) fusion(f32[16,128,256]{2,1,0:T(8,128)S(1)} %copy-done), kind=kLoop, calls=%fused_computation.85 | loop fusion | bytes 8355840 | tf_op jit(solution)/shard_map/jit(_roll_static)/slice | solution.py:177
  10.0 0.0 copy-start.6
  10.0 1.3 fusion.49
  11.4 1.0 fusion.52
  12.4 0.0 copy-done.6
  12.4 0.1 select_reduce_fusion
  12.5 0.0 collective-permute-done
  12.5 0.0 copy-start.4
  12.5 6.8 %fusion.13 = f32[16,128,256]{2,1,0:T(8,128)S(1)} fusion(f32[16,128,256]{2,1,0:T(8,128)} %param.9, f32[16,1,256]{2,1,0:T(1,128)S(1)} %get-tuple-element.24, f32[16,127,256]{2,1,0:T(8,128)} %get-tuple-element.20, f32[16,127,256]{2,1,0:T(8,128)} %get-tuple-element.19, f32[16,1,256]{2,1,0:T(1,128)S(1)} %get-tuple-element.23, ...), kind=kLoop, calls=%fused_computation.20 | loop fusion | flops 8912896 | bytes 14683136 | tf_op jit(solution)/shard_map/sub | solution.py:180
  19.4 0.0 copy-done.4
  19.4 1.2 fusion
  20.6 2.2 %copy.46 = f32[128,2,18,128]{3,1,2,0:T(2,128)} copy(f32[128,2,18,128]{3,1,0,2:T(2,128)S(1)} %bitcast.36) | data formatting | bytes 4718592 | tf_op jit(solution)/shard_map/reshape | solution.py:186
  22.9 11.3 %all-to-all-start = ((f32[128,2,18,128]{3,1,2,0:T(2,128)}), f32[128,2,18,128]{3,1,2,0:T(2,128)}, u32[]{:S(2)}, u32[]{:S(2)}) async-start(f32[128,2,18,128]{3,1,2,0:T(2,128)} %copy.46), calls=%async_computation | async-start | bytes 4718592 | tf_op jit(solution)/shard_map/all_to_all | solution.py:187
  34.3 0.1 broadcast_add_fusion
  34.3 31.6 %all-to-all-done = f32[128,2,18,128]{3,1,2,0:T(2,128)} async-done(((f32[128,2,18,128]{3,1,2,0:T(2,128)}), f32[128,2,18,128]{3,1,2,0:T(2,128)}, u32[]{:S(2)}, u32[]{:S(2)}) %all-to-all-start) | async-done | bytes 2359328 | tf_op jit(solution)/shard_map/all_to_all | solution.py:187
  66.0 7.4 %fusion.29 = f32[2,1024,2,128]{1,3,0,2:T(8,128)S(1)} fusion(f32[1024,64,18,1,1]{0,1,2,4,3:T(8,128)} %constant.90, f32[64,2,2,18,128]{4,2,3,1,0:T(2,128)} %bitcast.2), kind=kOutput, calls=%fused_computation.45 | convolution fusion | flops 3623878656 | bytes 9175040 | tf_op jit(solution)/shard_map/kgx,grmxj->mkrj/dot_general | solution.py:192
  73.3 0.0 copy-start.5
  73.3 0.2 copy.49
  73.6 0.7 copy-done.5
  74.3 1.8 %fusion.53 = f32[2,1024,256]{2,1,0:T(8,128)S(1)} fusion(f32[2,1024,256]{1,2,0:T(8,128)S(1)} %bitcast.39, f32[256,256,1]{1,0,2:T(8,128)S(1)} %copy-done.5), kind=kOutput, calls=%fused_computation.88 | convolution fusion | flops 805306368 | bytes 4456448 | tf_op jit(solution)/shard_map/sj,mkj->mks/dot_general | solution.py:195
  76.1 0.0 copy-start.3
  76.1 2.4 %fusion.25 = f32[2,1024,256]{1,2,0:T(8,128)S(1)} fusion(f32[256,256,1]{1,0,2:T(8,128)S(1)} %copy-done.5, f32[2,1024,256]{2,1,0:T(8,128)S(1)} %fusion.53, f32[256]{0:T(256)S(1)} %multiply_subtract_fusion.1, f32[2,1024]{1,0:T(2,128)S(1)} %broadcast_add_fusion), kind=kOutput, calls=%fused_computation.40 | convolution fusion | flops 1612185600 | bytes 4465664 | tf_op jit(solution)/shard_map/sj,mks->mkj/dot_general | solution.py:197
  78.5 0.0 copy-done.3
  78.5 6.8 %convolution_bitcast_fusion = f32[64,2,2,16,128]{4,0,3,1,2:T(8,128)S(1)} fusion(f32[2,1024,2,128,1]{1,3,4,2,0:T(8,128)S(1)} %bitcast.40, f32[1024,64,16,1,1]{0,1,2,4,3:T(8,128)S(1)} %copy-done.3), kind=kOutput, calls=%fused_computation.46 | convolution fusion | flops 6442450944 | bytes 8388608 | tf_op jit(solution)/shard_map/kgx,mkrj->grmxj/dot_general | solution.py:199
  85.4 0.2 select_maximum_fusion
  85.5 2.2 %copy.53 = f32[64,2,2,18,128]{4,1,0,3,2:T(2,128)S(1)} copy(f32[64,2,2,18,128]{4,0,3,1,2:T(8,128)S(1)} %select_maximum_fusion) | data formatting | bytes 4718592 | tf_op jit(solution)/shard_map/concatenate | solution.py:209
  87.7 1.8 %copy.54 = f32[128,2,18,128]{3,1,2,0:T(2,128)S(1)} copy(f32[128,2,18,128]{3,0,2,1:T(8,128)S(1)} %bitcast.38) | data formatting | bytes 4718592 | tf_op jit(solution)/shard_map/reshape | solution.py:210
  89.5 37.2 %all_to_all.10 = f32[128,2,18,128]{3,1,2,0:T(2,128)S(1)} all-to-all(f32[128,2,18,128]{3,1,2,0:T(2,128)S(1)} %copy.54), channel_id=1, replica_groups=mesh['gz'=64,'row'=2] {'gz','row'}, dimensions={0} | all-to-all | bytes 4718592 | tf_op jit(solution)/shard_map/all_to_all | solution.py:211
  126.7 1.3 copy.55
  128.0 4.0 %convolution_negate_fusion = f32[18,128,256]{2,1,0:T(8,128)S(1)} fusion(f32[256,18,128]{2,0,1:T(8,128)S(1)} %bitcast.37, f32[256,256,1]{0,1,2:T(8,128)S(1)} %copy-done.4), kind=kOutput, calls=%fused_computation.44 | convolution fusion | flops 1812529152 | bytes 4980736 | tf_op jit(solution)/shard_map/qxr,tq->xrt/dot_general | solution.py:213
  132.0 0.7 fusion.46
  132.8 0.4 fusion.45
  133.1 0.4 collective-permute-start.1
  133.6 2.3 %fusion.24 = f32[16,128,256]{2,1,0:T(8,128)} fusion(f32[16,128,256]{2,1,0:T(8,128)S(1)} %copy-done, f32[16,128,1]{2,1,0:T(8,128)S(1)} %get-tuple-element.6, f32[16,128,255]{2,1,0:T(8,128)S(1)} %get-tuple-element.8, f32[16,128,255]{2,1,0:T(8,128)S(1)} %get-tuple-element.7, f32[16,128,1]{2,1,0:T(8,128)S(1)} %get-tuple-element.5, f32[128]{0:T(128)S(1)} %get-tuple-element.27), kind=kLoop, calls=%fused_computation.39 | loop fusion | flops 2621440 | bytes 8389120 | tf_op jit(solution)/shard_map/sub | solution.py:230
  135.9 0.0 copy-start.1
  136.0 0.0 copy-start.2
  136.0 0.1 slice.130
  136.1 0.9 collective-permute-done.1
  137.0 0.5 copy-done.1
  137.5 0.6 copy-done.2
  138.2 2.7 %fusion.16 = (f32[16,128,256]{2,1,0:T(8,128)}, f32[16,128,256]{2,1,0:T(8,128)}) fusion(f32[16,128,256]{2,1,0:T(8,128)S(1)} %copy-done.1, f32[16,128,256]{2,1,0:T(8,128)S(1)} %slice.130, f32[16,1,256]{2,1,0:T(1,128)S(1)} %get-tuple-element.4, f32[16,1,256]{2,1,0:T(1,128)S(1)} %get-tuple-element.3, f32[16,128,256]{2,1,0:T(8,128)S(1)} %copy-done.2, ...), kind=kLoop, calls=%fused_computation.24 | loop fusion | flops 5242880 | bytes 10780672 | tf_op jit(solution)/shard_map/sub | solution.py:229
  (11 shorter events, 0.3 us)
Async XLA Ops:
  1.6 5.6 %copy-start = (f32[16,128,256]{2,1,0:T(8,128)S(1)}, f32[16,128,256]{2,1,0:T(8,128)}, u32[]{:S(2)}) copy-start(f32[16,128,256]{2,1,0:T(8,128)} %param.11) | copy-start | bytes 6291460
  1.6 10.9 %collective-permute-start = (f32[16,1,256]{2,1,0:T(1,128)S(1)}, f32[16,1,256]{2,1,0:T(1,128)S(1)}, u32[]{:S(2)}, u32[]{:S(2)}) collective-permute-start(f32[16,1,256]{2,1,0:T(1,128)S(1)} %broadcast_select_fusion.5), channel_id=1, source_target_pairs={{0,1},{1,0},{2,3},{3,2},{4,5},{5,4},{6,7},{7,6},{8,9},{9,8},{10,11... | collective-permute-start | bytes 49160 | tf_op jit(solution)/shard_map/ppermute | solution.py:164
  10.0 2.3 %copy-start.6 = (f32[48]{0:T(128)S(1)}, f32[48]{0:T(128)}, u32[]{:S(2)}) copy-start(f32[48]{0:T(128)} %param.12) | copy-start | bytes 580
  12.5 6.8 %copy-start.4 = (f32[256,256,1]{0,1,2:T(8,128)S(1)}, f32[256,256,1]{0,1,2:T(8,128)}, u32[]{:S(2)}) copy-start(f32[256,256,1]{0,1,2:T(8,128)} %constant.89) | copy-start | bytes 786436
  22.9 43.1 %all-to-all-start = ((f32[128,2,18,128]{3,1,2,0:T(2,128)}), f32[128,2,18,128]{3,1,2,0:T(2,128)}, u32[]{:S(2)}, u32[]{:S(2)}) async-start(f32[128,2,18,128]{3,1,2,0:T(2,128)} %copy.46), calls=%async_computation | async-start | bytes 4718592 | tf_op jit(solution)/shard_map/all_to_all | solution.py:187
  73.3 1.0 copy-start.5
  76.1 2.4 %copy-start.3 = (f32[1024,64,16,1,1]{0,1,2,4,3:T(8,128)S(1)}, f32[1024,64,16,1,1]{0,1,2,4,3:T(8,128)}, u32[]{:S(2)}) copy-start(f32[1024,64,16,1,1]{0,1,2,4,3:T(8,128)} %constant.92) | copy-start | bytes 12582916
  133.1 3.8 %collective-permute-start.1 = (f32[16,1,256]{2,1,0:T(1,128)S(1)}, f32[16,1,256]{2,1,0:T(1,128)S(1)}, u32[]{:S(2)}, u32[]{:S(2)}) collective-permute-start(f32[16,1,256]{2,1,0:T(1,128)S(1)} %broadcast_select_fusion.2), channel_id=1, source_target_pairs={{0,1},{1,0},{2,3},{3,2},{4,5},{5,4},{6,7},{7,6},{8,9},{9,8},{10,11... | collective-permute-start | bytes 49160 | tf_op jit(solution)/shard_map/ppermute | solution.py:37
  135.9 1.6 %copy-start.1 = (f32[16,128,256]{2,1,0:T(8,128)S(1)}, f32[16,128,256]{2,1,0:T(8,128)}, u32[]{:S(2)}) copy-start(f32[16,128,256]{2,1,0:T(8,128)} %param.10) | copy-start | bytes 6291460
  136.0 2.2 %copy-start.2 = (f32[16,128,256]{2,1,0:T(8,128)S(1)}, f32[16,128,256]{2,1,0:T(8,128)}, u32[]{:S(2)}) copy-start(f32[16,128,256]{2,1,0:T(8,128)} %param.9) | copy-start | bytes 6291460

commit v9 on v7

--- a/solution.py
+++ b/solution.py
@@ -202,8 +202,12 @@
     windows = jnp.concatenate([physical_space, ghost_low, ghost_high], axis=3)
     windows = windows.reshape(device_count, modes_each, axial_block + 2, radial_block)
     returned = lax.all_to_all(windows, both, split_axis=0, concat_axis=0, tiled=True)
-    returned = returned.reshape(NT, axial_block + 2, radial_block)
-    extended_p = -jnp.einsum("qxr,tq->xrt", returned, fourier, precision=maximal_precision)
+    extended_p = -jnp.einsum(
+        "smxr,tsm->xrt",
+        returned,
+        fourier.reshape(NT, device_count, modes_each),
+        precision=maximal_precision,
+    )
     pressure = extended_p[:axial_block]
     padded = jnp.concatenate(
         [extended_p[axial_block : axial_block + 1], pressure, extended_p[axial_block + 1 :]], axis=0

time: 133 us -> 132 us (level)
    unnamed x18 -> x20, local copies, waits for them, and re-layouts: 3.12 us -> 3.13 us
where the time goes in v9:
time: 132 us; the launch traced here: 130 us
  blocking collectives  37.3 us (28%)
  waiting for transfers between devices  32.9 us (25%)
  matrix products  23.6 us (18%)
  starting transfers between devices  12.6 us (10%)
  local copies, waits for them, and re-layouts  12 us (9%)
  other arithmetic  10.3 us (8%)
    all_to_all x1, blocking collectives, body(): lax.all_to_all(windows, both, split_axis=0, concat_axis=0, tiled=True)  37.3 us
    all_to_all x1, waiting for transfers between devices, body(): lax.all_to_all(spectrum_in, both, split_axis=0, concat_axis=0, tiled=True)  31.6 us
    all_to_all x1, starting transfers between devices, body(): lax.all_to_all(spectrum_in, both, split_axis=0, concat_axis=0, tiled=True)  11.2 us
    dot_general x1, matrix products, body(): jnp.einsum('kgx,grmxj->mkrj', jnp.asarray(forward_table), resident, preci...  7.36 us
    dot_general x1, matrix products, body(): jnp.einsum('kgx,mkrj->grmxj', jnp.asarray(AXIAL_TABLE).reshape(NX, gz_cou...  6.78 us
    dot_general x1, matrix products, body(): jnp.einsum('smxr,tsm->xrt', returned, fourier.reshape(NT, device_count, m...  3.97 us
    unnamed x20, local copies, waits for them, and re-layouts  3.13 us
    sub x1, other arithmetic, body(): radial_projected_velocity = radial_vel - 0.5 * (above - below)  2.74 us
  transfers between devices with their start and end apart: 3, of which 3 were waited for; matrix products, arithmetic and copies ran while one was open for 3% of the time, Pallas kernels for 0%

profile of v9, /device:TPU:6, one launch (start us, length us, event | category | flops | bytes accessed | tf_op | source)
XLA Modules:
  0.0 129.6 jit_solution(9682733950263875565)
XLA Ops:
  0.6 0.0 copy-start
  0.7 2.0 %broadcast_multiply_fusion = f32[16,128,256]{2,1,0:T(8,128)S(1)} fusion(f32[16,128,256]{2,1,0:T(8,128)} %param.10, f32[128]{0:T(128)S(1)} %convert_add_fusion), kind=kLoop, calls=%fused_computation.52 | loop fusion | flops 524288 | bytes 4194816 | tf_op jit(solution)/shard_map/mul | solution.py:162
  2.7 0.9 collective-permute-start
  3.6 0.0 copy-done
  3.6 0.7 fusion.52
  4.3 0.0 copy-start.1
  4.3 0.0 copy-start.9
  4.4 0.0 copy-start.5
  4.4 0.4 fusion.51
  4.7 1.2 copy-done.1
  5.9 0.0 copy-done.9
  6.0 0.1 select_reduce_fusion
  6.1 0.5 collective-permute-done
  6.5 0.0 copy-done.5
  6.6 2.6 %fusion.15 = f32[16,128,256]{2,1,0:T(8,128)S(1)} fusion(f32[16,128,256]{2,1,0:T(8,128)S(1)} %copy-done.1, f32[16,128,256]{2,1,0:T(8,128)S(1)} %broadcast_multiply_fusion, f32[16,1,256]{2,1,0:T(1,128)S(1)} %get-tuple-element.22, f32[16,1,256]{2,1,0:T(1,128)S(1)} %get-tuple-element.21, f32[16,128,1]{2,1,0:T(8,128)S(1)} %get-tuple-element.16, ...), kind=kLoop, calls=%fused_computation.23 | loop fusion | flops 7864320 | bytes 12617728 | tf_op jit(solution)/shard_map/sub | solution.py:173
  9.2 0.0 copy-done.8
  9.2 1.2 fusion
  10.5 2.3 %copy.39 = f32[128,2,18,128]{3,1,2,0:T(2,128)} copy(f32[128,2,18,128]{3,1,0,2:T(2,128)S(1)} %bitcast.37) | data formatting | bytes 4718592 | tf_op jit(solution)/shard_map/reshape | solution.py:179
  12.7 11.2 %all-to-all-start = ((f32[128,2,18,128]{3,1,2,0:T(2,128)}), f32[128,2,18,128]{3,1,2,0:T(2,128)}, u32[]{:S(2)}, u32[]{:S(2)}) async-start(f32[128,2,18,128]{3,1,2,0:T(2,128)} %copy.39), calls=%async_computation | async-start | bytes 4718592 | tf_op jit(solution)/shard_map/all_to_all | solution.py:180
  24.1 0.1 broadcast_add_fusion
  24.2 31.6 %all-to-all-done = f32[128,2,18,128]{3,1,2,0:T(2,128)} async-done(((f32[128,2,18,128]{3,1,2,0:T(2,128)}), f32[128,2,18,128]{3,1,2,0:T(2,128)}, u32[]{:S(2)}, u32[]{:S(2)}) %all-to-all-start) | async-done | bytes 2359328 | tf_op jit(solution)/shard_map/all_to_all | solution.py:180
  55.8 7.4 %fusion.33 = f32[2,1024,2,128]{1,3,0,2:T(8,128)S(1)} fusion(f32[1024,64,18,1,1]{0,1,2,4,3:T(8,128)} %constant.89, f32[64,2,2,18,128]{4,2,3,1,0:T(2,128)} %bitcast.2), kind=kOutput, calls=%fused_computation.47 | convolution fusion | flops 3623878656 | bytes 9175040 | tf_op jit(solution)/shard_map/kgx,grmxj->mkrj/dot_general | solution.py:185
  63.2 0.0 copy-start.7
  63.2 0.2 copy.42
  63.4 0.7 copy-done.7
  64.1 1.8 %fusion.54 = f32[2,1024,256]{2,1,0:T(8,128)S(1)} fusion(f32[2,1024,256]{1,2,0:T(8,128)S(1)} %bitcast.39, f32[256,256,1]{1,0,2:T(8,128)S(1)} %copy-done.7), kind=kOutput, calls=%fused_computation.87 | convolution fusion | flops 805306368 | bytes 4456448 | tf_op jit(solution)/shard_map/sj,mkj->mks/dot_general | solution.py:188
  66.0 0.0 copy-start.4
  66.0 2.4 %fusion.27 = f32[2,1024,256]{1,2,0:T(8,128)S(1)} fusion(f32[256,256,1]{1,0,2:T(8,128)S(1)} %copy-done.7, f32[2,1024,256]{2,1,0:T(8,128)S(1)} %fusion.54, f32[256]{0:T(256)S(1)} %multiply_subtract_fusion.1, f32[2,1024]{1,0:T(2,128)S(1)} %broadcast_add_fusion), kind=kOutput, calls=%fused_computation.43 | convolution fusion | flops 1612185600 | bytes 4465664 | tf_op jit(solution)/shard_map/sj,mks->mkj/dot_general | solution.py:190
  68.4 0.0 copy-done.4
  68.4 6.8 %convolution_bitcast_fusion = f32[64,2,2,16,128]{4,0,3,1,2:T(8,128)S(1)} fusion(f32[2,1024,2,128,1]{1,3,4,2,0:T(8,128)S(1)} %bitcast.40, f32[1024,64,16,1,1]{0,1,2,4,3:T(8,128)S(1)} %copy-done.4), kind=kOutput, calls=%fused_computation.48 | convolution fusion | flops 6442450944 | bytes 8388608 | tf_op jit(solution)/shard_map/kgx,mkrj->grmxj/dot_general | solution.py:192
  75.2 0.2 select_maximum_fusion
  75.4 2.2 %copy.46 = f32[64,2,2,18,128]{4,1,0,3,2:T(2,128)S(1)} copy(f32[64,2,2,18,128]{4,0,3,1,2:T(8,128)S(1)} %select_maximum_fusion) | data formatting | bytes 4718592 | tf_op jit(solution)/shard_map/concatenate | solution.py:202
  77.5 1.8 %copy.47 = f32[128,2,18,128]{3,1,2,0:T(2,128)S(1)} copy(f32[128,2,18,128]{3,0,2,1:T(8,128)S(1)} %bitcast.38) | data formatting | bytes 4718592 | tf_op jit(solution)/shard_map/reshape | solution.py:203
  79.4 0.0 copy-start.6
  79.4 37.3 %all_to_all.10 = f32[128,2,18,128]{3,1,2,0:T(2,128)S(1)} all-to-all(f32[128,2,18,128]{3,1,2,0:T(2,128)S(1)} %copy.47), channel_id=1, replica_groups=mesh['gz'=64,'row'=2] {'gz','row'}, dimensions={0} | all-to-all | bytes 4718592 | tf_op jit(solution)/shard_map/all_to_all | solution.py:204
  116.7 0.0 copy-done.6
  116.7 4.0 %bitcast_negate_fusion = f32[18,128,256]{2,1,0:T(8,128)S(1)} fusion(f32[256,128,2,1]{1,0,2,3:T(8,128)S(1)} %copy-done.6, f32[128,2,18,128]{3,1,2,0:T(2,128)S(1)} %all_to_all.10), kind=kOutput, calls=%fused_computation.11 | convolution fusion | flops 1812529152 | bytes 4980736 | tf_op jit(solution)/shard_map/smxr,tsm->xrt/dot_general | solution.py:205
  120.7 0.7 fusion.48
  121.4 0.4 fusion.47
  121.8 0.4 collective-permute-start.1
  122.3 2.3 %fusion.26 = f32[16,128,256]{2,1,0:T(8,128)} fusion(f32[16,128,256]{2,1,0:T(8,128)S(1)} %copy-done, f32[16,128,1]{2,1,0:T(8,128)S(1)} %get-tuple-element.6, f32[16,128,255]{2,1,0:T(8,128)S(1)} %get-tuple-element.8, f32[16,128,255]{2,1,0:T(8,128)S(1)} %get-tuple-element.7, f32[16,128,1]{2,1,0:T(8,128)S(1)} %get-tuple-element.5, f32[128]{0:T(128)S(1)} %get-tuple-element.23), kind=kLoop, calls=%fused_computation.42 | loop fusion | flops 2621440 | bytes 8389120 | tf_op jit(solution)/shard_map/sub | solution.py:227
  124.6 0.0 copy-start.2
  124.6 0.0 copy-start.3
  124.6 0.1 slice.134
  124.8 0.9 collective-permute-done.1
  125.7 0.5 copy-done.2
  126.2 0.6 copy-done.3
  126.8 2.7 %fusion.18 = (f32[16,128,256]{2,1,0:T(8,128)}, f32[16,128,256]{2,1,0:T(8,128)}) fusion(f32[16,128,256]{2,1,0:T(8,128)S(1)} %copy-done.3, f32[16,128,256]{2,1,0:T(8,128)S(1)} %slice.134, f32[16,1,256]{2,1,0:T(1,128)S(1)} %get-tuple-element.4, f32[16,1,256]{2,1,0:T(1,128)S(1)} %get-tuple-element.3, f32[16,128,256]{2,1,0:T(8,128)S(1)} %copy-done.2, ...), kind=kLoop, calls=%fused_computation.27 | loop fusion | flops 5242880 | bytes 10780672 | tf_op jit(solution)/shard_map/sub | solution.py:226
  (14 shorter events, 0.3 us)
Async XLA Ops:
  0.6 3.0 %copy-start = (f32[16,128,256]{2,1,0:T(8,128)S(1)}, f32[16,128,256]{2,1,0:T(8,128)}, u32[]{:S(2)}) copy-start(f32[16,128,256]{2,1,0:T(8,128)} %param.11) | copy-start | bytes 6291460
  2.7 3.8 %collective-permute-start = (f32[16,1,256]{2,1,0:T(1,128)S(1)}, f32[16,1,256]{2,1,0:T(1,128)S(1)}, u32[]{:S(2)}, u32[]{:S(2)}) collective-permute-start(f32[16,1,256]{2,1,0:T(1,128)S(1)} %broadcast_select_fusion.5), channel_id=1, source_target_pairs={{0,1},{1,0},{2,3},{3,2},{4,5},{5,4},{6,7},{7,6},{8,9},{9,8},{10,11... | collective-permute-start | bytes 49160 | tf_op jit(solution)/shard_map/ppermute | solution.py:37
  4.3 1.6 %copy-start.1 = (f32[16,128,256]{2,1,0:T(8,128)S(1)}, f32[16,128,256]{2,1,0:T(8,128)}, u32[]{:S(2)}) copy-start(f32[16,128,256]{2,1,0:T(8,128)} %param.9) | copy-start | bytes 6291460
  4.3 1.6 %copy-start.9 = (f32[48]{0:T(128)S(1)}, f32[48]{0:T(128)}, u32[]{:S(2)}) copy-start(f32[48]{0:T(128)} %param.12) | copy-start | bytes 580
  4.4 2.2 %copy-start.5 = (s32[16,128,256]{2,1,0:T(8,128)S(1)}, s32[16,128,256]{2,1,0:T(8,128)}, u32[]{:S(2)}) copy-start(s32[16,128,256]{2,1,0:T(8,128)} %param.13) | copy-start | bytes 6291460
  6.6 2.6 %copy-start.8 = (f32[256,256,1]{0,1,2:T(8,128)S(1)}, f32[256,256,1]{0,1,2:T(8,128)}, u32[]{:S(2)}) copy-start(f32[256,256,1]{0,1,2:T(8,128)} %constant.88) | copy-start | bytes 786436
  12.7 43.1 %all-to-all-start = ((f32[128,2,18,128]{3,1,2,0:T(2,128)}), f32[128,2,18,128]{3,1,2,0:T(2,128)}, u32[]{:S(2)}, u32[]{:S(2)}) async-start(f32[128,2,18,128]{3,1,2,0:T(2,128)} %copy.39), calls=%async_computation | async-start | bytes 4718592 | tf_op jit(solution)/shard_map/all_to_all | solution.py:180
  63.2 1.0 copy-start.7
  66.0 2.4 %copy-start.4 = (f32[1024,64,16,1,1]{0,1,2,4,3:T(8,128)S(1)}, f32[1024,64,16,1,1]{0,1,2,4,3:T(8,128)}, u32[]{:S(2)}) copy-start(f32[1024,64,16,1,1]{0,1,2,4,3:T(8,128)} %constant.91) | copy-start | bytes 12582916
  79.4 37.3 %copy-start.6 = (f32[256,128,2,1]{1,0,2,3:T(8,128)S(1)}, f32[256,128,2,1]{1,0,2,3:T(8,128)}, u32[]{:S(2)}) copy-start(f32[256,128,2,1]{1,0,2,3:T(8,128)} %constant.92) | copy-start | bytes 786436
  121.8 3.8 %collective-permute-start.1 = (f32[16,1,256]{2,1,0:T(1,128)S(1)}, f32[16,1,256]{2,1,0:T(1,128)S(1)}, u32[]{:S(2)}, u32[]{:S(2)}) collective-permute-start(f32[16,1,256]{2,1,0:T(1,128)S(1)} %broadcast_select_fusion.2), channel_id=1, source_target_pairs={{0,1},{1,0},{2,3},{3,2},{4,5},{5,4},{6,7},{7,6},{8,9},{9,8},{10,11... | collective-permute-start | bytes 49160 | tf_op jit(solution)/shard_map/ppermute | solution.py:37
  124.6 1.6 %copy-start.2 = (f32[16,128,256]{2,1,0:T(8,128)S(1)}, f32[16,128,256]{2,1,0:T(8,128)}, u32[]{:S(2)}) copy-start(f32[16,128,256]{2,1,0:T(8,128)} %param.9) | copy-start | bytes 6291460
  124.6 2.2 %copy-start.3 = (f32[16,128,256]{2,1,0:T(8,128)S(1)}, f32[16,128,256]{2,1,0:T(8,128)}, u32[]{:S(2)}) copy-start(f32[16,128,256]{2,1,0:T(8,128)} %param.10) | copy-start | bytes 6291460

commit v10 on v9

--- a/solution.py
+++ b/solution.py
@@ -118,6 +118,8 @@
 
 
 AZIMUTH_TABLE = fixed_azimuth_basis()
+SHIFTED_TABLE = (np.roll(AZIMUTH_TABLE.astype(np.float64), 1, axis=0)
+                 - np.roll(AZIMUTH_TABLE.astype(np.float64), -1, axis=0)).astype(np.float32)
 AXIAL_TABLE = fixed_axial_basis()
 
 
@@ -167,14 +169,16 @@
         radial_flux = extended(flux, (("row", 1),), 1)
     divergence = 0.5 * (axial_pad[2:] - axial_pad[:-2])
     divergence = divergence + (radial_flux[:, 2:] - radial_flux[:, :-2]) / (2.0 * radius)
-    divergence = divergence + (jnp.roll(swirl_vel, -1, 2) - jnp.roll(swirl_vel, 1, 2)) / (
-        2.0 * radius * spacing
-    )
     right_side = divergence - canopy_source(canopy_gore, inflow_rate)
     all_modes = jnp.arange(NT, dtype=jnp.int32)
     fourier = jnp.asarray(AZIMUTH_TABLE)
     planes = jnp.concatenate([right_side, axial_vel[:1], axial_vel[-1:]], axis=0)
     spectrum_in = jnp.einsum("xrt,tm->mxr", planes, fourier, precision=forward_precision)
+    swirl_modes = jnp.einsum(
+        "xrt,tm->mxr", swirl_vel, jnp.asarray(SHIFTED_TABLE), precision=forward_precision
+    ) / (2.0 * radius[:, :, 0] * spacing)
+    swirl_modes = jnp.concatenate([swirl_modes, jnp.zeros_like(swirl_modes[:, :2])], axis=1)
+    spectrum_in = spectrum_in + swirl_modes
     modes_each = NT // device_count
     spectrum_in = spectrum_in.reshape(device_count, modes_each, axial_block + 2, radial_block)
     resident = lax.all_to_all(spectrum_in, both, split_axis=0, concat_axis=0, tiled=True)

time: 132 us -> 130 us (0.985)
  other arithmetic: 10.3 us -> 8.7 us
  local copies, waits for them, and re-layouts: 12 us -> 10.5 us
    sub x1, other arithmetic: 2.63 us -> 1.03 us  [body(): right_side = divergence - canopy_source(canopy_gore, inflow_rate)]
    unnamed x20 -> x22, local copies, waits for them, and re-layouts: 3.13 us -> 2.69 us
where the time goes in v10:
time: 130 us; the launch traced here: 128 us
  blocking collectives  37.3 us (29%)
  waiting for transfers between devices  33.4 us (26%)
  matrix products  24.8 us (19%)
  starting transfers between devices  12.2 us (9%)
  local copies, waits for them, and re-layouts  10.5 us (8%)
  other arithmetic  8.7 us (7%)
    all_to_all x1, blocking collectives, body(): lax.all_to_all(windows, both, split_axis=0, concat_axis=0, tiled=True)  37.3 us
    all_to_all x1, waiting for transfers between devices, body(): lax.all_to_all(spectrum_in, both, split_axis=0, concat_axis=0, tiled=True)  31.6 us
    all_to_all x1, starting transfers between devices, body(): lax.all_to_all(spectrum_in, both, split_axis=0, concat_axis=0, tiled=True)  10.9 us
    dot_general x1, matrix products, body(): jnp.einsum('kgx,grmxj->mkrj', jnp.asarray(forward_table), resident, preci...  7.36 us
    dot_general x1, matrix products, body(): jnp.einsum('kgx,mkrj->grmxj', jnp.asarray(AXIAL_TABLE).reshape(NX, gz_cou...  6.78 us
    dot_general x1, matrix products, body(): jnp.einsum('smxr,tsm->xrt', returned, fourier.reshape(NT, device_count, m...  3.97 us
    sub x1, other arithmetic, body(): radial_projected_velocity = radial_vel - 0.5 * (above - below)  2.74 us
    unnamed x22, local copies, waits for them, and re-layouts  2.69 us
  transfers between devices with their start and end apart: 3, of which 3 were waited for; matrix products, arithmetic and copies ran while one was open for 3% of the time, Pallas kernels for 0%

profile of v10, /device:TPU:6, one launch (start us, length us, event | category | flops | bytes accessed | tf_op | source)
XLA Modules:
  0.0 127.9 jit_solution(16537641355316922032)
XLA Ops:
  0.6 0.0 copy-start
  0.7 0.0 copy-start.4
  0.7 0.0 copy-start.10
  0.7 2.1 %broadcast_multiply_fusion = f32[16,128,256]{2,1,0:T(8,128)S(1)} fusion(f32[16,128,256]{2,1,0:T(8,128)} %param.11, f32[128]{0:T(128)S(1)} %convert_add_fusion), kind=kLoop, calls=%fused_computation.51 | loop fusion | flops 524288 | bytes 4194816 | tf_op jit(solution)/shard_map/mul | solution.py:164
  2.8 0.9 collective-permute-start
  3.7 0.0 copy-done
  3.8 0.0 copy-done.4
  3.8 0.0 copy-done.10
  3.8 0.0 copy-start.9
  3.8 0.0 copy-start.3
  3.8 1.2 convolution_divide_fusion
  5.0 0.0 copy-done.9
  5.0 0.1 select_reduce_fusion
  5.1 1.5 %collective-permute-done = f32[16,1,256]{2,1,0:T(1,128)S(1)} collective-permute-done((f32[16,1,256]{2,1,0:T(1,128)S(1)}, f32[16,1,256]{2,1,0:T(1,128)S(1)}, u32[]{:S(2)}, u32[]{:S(2)}) %collective-permute-start) | collective-permute-done | bytes 16416 | tf_op jit(solution)/shard_map/ppermute | solution.py:37
  6.7 0.0 copy-done.3
  6.7 0.0 copy-start.6
  6.7 1.0 fusion.14
  7.7 0.0 copy-done.6
  7.7 1.3 %pad_add_fusion = f32[256,18,128]{2,0,1:T(8,128)S(1)} fusion(f32[256,16,128]{2,0,1:T(8,128)S(1)} %convolution_divide_fusion, f32[256,256,1]{0,1,2:T(8,128)S(1)} %copy-done.6, f32[1,128,256]{2,1,0:T(8,128)S(1)} %get-tuple-element.16, f32[1,128,256]{2,1,0:T(8,128)S(1)} %get-tuple-element.15, f32[16,128,256]{2,1,0:T(8,128)S(1)} %fusion.14), kind=kOutput, calls=%fused_computation.16 | convolution fusion | flops 907739136 | bytes 7077888 | tf_op jit(solution)/shard_map/xrt,tm->mxr/dot_general | solution.py:176
  9.1 2.2 %copy.40 = f32[128,2,18,128]{3,1,2,0:T(2,128)} copy(f32[128,2,18,128]{3,1,0,2:T(2,128)S(1)} %bitcast.40) | data formatting | bytes 4718592 | tf_op jit(solution)/shard_map/reshape | solution.py:183
  11.3 10.9 %all-to-all-start = ((f32[128,2,18,128]{3,1,2,0:T(2,128)}), f32[128,2,18,128]{3,1,2,0:T(2,128)}, u32[]{:S(2)}, u32[]{:S(2)}) async-start(f32[128,2,18,128]{3,1,2,0:T(2,128)} %copy.40), calls=%async_computation | async-start | bytes 4718592 | tf_op jit(solution)/shard_map/all_to_all | solution.py:184
  22.4 0.1 broadcast_add_fusion
  22.4 31.6 %all-to-all-done = f32[128,2,18,128]{3,1,2,0:T(2,128)} async-done(((f32[128,2,18,128]{3,1,2,0:T(2,128)}), f32[128,2,18,128]{3,1,2,0:T(2,128)}, u32[]{:S(2)}, u32[]{:S(2)}) %all-to-all-start) | async-done | bytes 2359328 | tf_op jit(solution)/shard_map/all_to_all | solution.py:184
  54.0 7.4 %fusion.33 = f32[2,1024,2,128]{1,3,0,2:T(8,128)S(1)} fusion(f32[1024,64,18,1,1]{0,1,2,4,3:T(8,128)} %constant.99, f32[64,2,2,18,128]{4,2,3,1,0:T(2,128)} %bitcast.3), kind=kOutput, calls=%fused_computation.45 | convolution fusion | flops 3623878656 | bytes 9175040 | tf_op jit(solution)/shard_map/kgx,grmxj->mkrj/dot_general | solution.py:189
  61.4 0.0 copy-start.8
  61.4 0.2 copy.43
  61.7 0.7 copy-done.8
  62.4 1.8 %fusion.52 = f32[2,1024,256]{2,1,0:T(8,128)S(1)} fusion(f32[2,1024,256]{1,2,0:T(8,128)S(1)} %bitcast.42, f32[256,256,1]{1,0,2:T(8,128)S(1)} %copy-done.8), kind=kOutput, calls=%fused_computation.84 | convolution fusion | flops 805306368 | bytes 4456448 | tf_op jit(solution)/shard_map/sj,mkj->mks/dot_general | solution.py:192
  64.2 0.0 copy-start.2
  64.2 2.4 %fusion.25 = f32[2,1024,256]{1,2,0:T(8,128)S(1)} fusion(f32[256,256,1]{1,0,2:T(8,128)S(1)} %copy-done.8, f32[2,1024,256]{2,1,0:T(8,128)S(1)} %fusion.52, f32[256]{0:T(256)S(1)} %multiply_subtract_fusion.1, f32[2,1024]{1,0:T(2,128)S(1)} %broadcast_add_fusion), kind=kOutput, calls=%fused_computation.41 | convolution fusion | flops 1612185600 | bytes 4465664 | tf_op jit(solution)/shard_map/sj,mks->mkj/dot_general | solution.py:194
  66.6 6.8 %convolution_bitcast_fusion = f32[64,2,2,16,128]{4,0,3,1,2:T(8,128)S(1)} fusion(f32[2,1024,2,128,1]{1,3,4,2,0:T(8,128)S(1)} %bitcast.43, f32[1024,64,16,1,1]{0,1,2,4,3:T(8,128)S(1)} %copy-done.2), kind=kOutput, calls=%fused_computation.46 | convolution fusion | flops 6442450944 | bytes 8388608 | tf_op jit(solution)/shard_map/kgx,mkrj->grmxj/dot_general | solution.py:196
  73.4 0.2 select_maximum_fusion
  73.6 2.2 %copy.47 = f32[64,2,2,18,128]{4,1,0,3,2:T(2,128)S(1)} copy(f32[64,2,2,18,128]{4,0,3,1,2:T(8,128)S(1)} %select_maximum_fusion) | data formatting | bytes 4718592 | tf_op jit(solution)/shard_map/concatenate | solution.py:206
  75.8 1.8 %copy.48 = f32[128,2,18,128]{3,1,2,0:T(2,128)S(1)} copy(f32[128,2,18,128]{3,0,2,1:T(8,128)S(1)} %bitcast.41) | data formatting | bytes 4718592 | tf_op jit(solution)/shard_map/reshape | solution.py:207
  77.6 0.0 copy-start.7
  77.6 37.3 %all_to_all.10 = f32[128,2,18,128]{3,1,2,0:T(2,128)S(1)} all-to-all(f32[128,2,18,128]{3,1,2,0:T(2,128)S(1)} %copy.48), channel_id=1, replica_groups=mesh['gz'=64,'row'=2] {'gz','row'}, dimensions={0} | all-to-all | bytes 4718592 | tf_op jit(solution)/shard_map/all_to_all | solution.py:208
  114.9 4.0 %bitcast_negate_fusion = f32[18,128,256]{2,1,0:T(8,128)S(1)} fusion(f32[256,128,2,1]{1,0,2,3:T(8,128)S(1)} %copy-done.7, f32[128,2,18,128]{3,1,2,0:T(2,128)S(1)} %all_to_all.10), kind=kOutput, calls=%fused_computation.11 | convolution fusion | flops 1812529152 | bytes 4980736 | tf_op jit(solution)/shard_map/smxr,tsm->xrt/dot_general | solution.py:209
  118.9 0.7 fusion.48
  119.7 0.0 copy-start.5
  119.7 0.4 fusion.47
  120.1 0.4 collective-permute-start.1
  120.5 0.7 copy-done.5
  121.3 2.2 %fusion.24 = f32[16,128,256]{2,1,0:T(8,128)} fusion(f32[16,128,256]{2,1,0:T(8,128)S(1)} %copy-done.5, f32[16,128,1]{2,1,0:T(8,128)S(1)} %get-tuple-element.6, f32[16,128,255]{2,1,0:T(8,128)S(1)} %get-tuple-element.8, f32[16,128,255]{2,1,0:T(8,128)S(1)} %get-tuple-element.7, f32[16,128,1]{2,1,0:T(8,128)S(1)} %get-tuple-element.5, f32[128]{0:T(128)S(1)} %get-tuple-element.19), kind=kLoop, calls=%fused_computation.40 | loop fusion | flops 2621440 | bytes 8389120 | tf_op jit(solution)/shard_map/sub | solution.py:231
  123.5 0.0 copy-start.1
  123.5 0.1 slice.118
  123.7 0.2 collective-permute-done.1
  123.9 1.2 copy-done.1
  125.1 2.7 %fusion.17 = (f32[16,128,256]{2,1,0:T(8,128)}, f32[16,128,256]{2,1,0:T(8,128)}) fusion(f32[16,128,256]{2,1,0:T(8,128)S(1)} %copy-done.1, f32[16,128,256]{2,1,0:T(8,128)S(1)} %slice.118, f32[16,1,256]{2,1,0:T(1,128)S(1)} %get-tuple-element.4, f32[16,1,256]{2,1,0:T(1,128)S(1)} %get-tuple-element.3, f32[16,128,256]{2,1,0:T(8,128)S(1)} %copy-done, ...), kind=kLoop, calls=%fused_computation.27 | loop fusion | flops 5242880 | bytes 10780672 | tf_op jit(solution)/shard_map/sub | solution.py:230
  (15 shorter events, 0.3 us)
Async XLA Ops:
  0.6 3.1 %copy-start = (f32[16,128,256]{2,1,0:T(8,128)S(1)}, f32[16,128,256]{2,1,0:T(8,128)}, u32[]{:S(2)}) copy-start(f32[16,128,256]{2,1,0:T(8,128)} %param.10) | copy-start | bytes 6291460
  0.7 3.1 %copy-start.4 = (f32[16,128,256]{2,1,0:T(8,128)S(1)}, f32[16,128,256]{2,1,0:T(8,128)}, u32[]{:S(2)}) copy-start(f32[16,128,256]{2,1,0:T(8,128)} %param.12) | copy-start | bytes 6291460
  0.7 3.1 %copy-start.10 = (f32[256,256,1]{0,1,2:T(8,128)S(1)}, f32[256,256,1]{0,1,2:T(8,128)}, u32[]{:S(2)}) copy-start(f32[256,256,1]{0,1,2:T(8,128)} %constant.98) | copy-start | bytes 786436
  2.8 3.8 %collective-permute-start = (f32[16,1,256]{2,1,0:T(1,128)S(1)}, f32[16,1,256]{2,1,0:T(1,128)S(1)}, u32[]{:S(2)}, u32[]{:S(2)}) collective-permute-start(f32[16,1,256]{2,1,0:T(1,128)S(1)} %broadcast_select_fusion.5), channel_id=1, source_target_pairs={{0,1},{1,0},{2,3},{3,2},{4,5},{5,4},{6,7},{7,6},{8,9},{9,8},{10,11... | collective-permute-start | bytes 49160 | tf_op jit(solution)/shard_map/ppermute | solution.py:37
  3.8 1.2 copy-start.9
  3.8 2.9 %copy-start.3 = (s32[16,128,256]{2,1,0:T(8,128)S(1)}, s32[16,128,256]{2,1,0:T(8,128)}, u32[]{:S(2)}) copy-start(s32[16,128,256]{2,1,0:T(8,128)} %param.14) | copy-start | bytes 6291460
  6.7 1.1 copy-start.6
  11.3 42.7 %all-to-all-start = ((f32[128,2,18,128]{3,1,2,0:T(2,128)}), f32[128,2,18,128]{3,1,2,0:T(2,128)}, u32[]{:S(2)}, u32[]{:S(2)}) async-start(f32[128,2,18,128]{3,1,2,0:T(2,128)} %copy.40), calls=%async_computation | async-start | bytes 4718592 | tf_op jit(solution)/shard_map/all_to_all | solution.py:184
  61.4 1.0 copy-start.8
  64.2 2.4 %copy-start.2 = (f32[1024,64,16,1,1]{0,1,2,4,3:T(8,128)S(1)}, f32[1024,64,16,1,1]{0,1,2,4,3:T(8,128)}, u32[]{:S(2)}) copy-start(f32[1024,64,16,1,1]{0,1,2,4,3:T(8,128)} %constant.101) | copy-start | bytes 12582916
  77.6 37.3 %copy-start.7 = (f32[256,128,2,1]{1,0,2,3:T(8,128)S(1)}, f32[256,128,2,1]{1,0,2,3:T(8,128)}, u32[]{:S(2)}) copy-start(f32[256,128,2,1]{1,0,2,3:T(8,128)} %constant.102) | copy-start | bytes 786436
  119.7 1.6 %copy-start.5 = (f32[16,128,256]{2,1,0:T(8,128)S(1)}, f32[16,128,256]{2,1,0:T(8,128)}, u32[]{:S(2)}) copy-start(f32[16,128,256]{2,1,0:T(8,128)} %param.12) | copy-start | bytes 6291460
  120.1 3.8 %collective-permute-start.1 = (f32[16,1,256]{2,1,0:T(1,128)S(1)}, f32[16,1,256]{2,1,0:T(1,128)S(1)}, u32[]{:S(2)}, u32[]{:S(2)}) collective-permute-start(f32[16,1,256]{2,1,0:T(1,128)S(1)} %broadcast_select_fusion.2), channel_id=1, source_target_pairs={{0,1},{1,0},{2,3},{3,2},{4,5},{5,4},{6,7},{7,6},{8,9},{9,8},{10,11... | collective-permute-start | bytes 49160 | tf_op jit(solution)/shard_map/ppermute | solution.py:37
  123.5 1.6 %copy-start.1 = (f32[16,128,256]{2,1,0:T(8,128)S(1)}, f32[16,128,256]{2,1,0:T(8,128)}, u32[]{:S(2)}) copy-start(f32[16,128,256]{2,1,0:T(8,128)} %param.11) | copy-start | bytes 6291460
